TPU v7x, 256 devices: a whole 4x4x8 slice. The times are simulated.
256 devices in a mesh: row: 8 (over y, core), col: 32 (over x, z).
Axes of the slice: x: 4, y: 4, z: 8, core: 2. Of those that a mesh axis runs over, the one named last changes fastest.
Arguments:
- tokens: bfloat16 [256, 512, 192], P('row', 'col'), may hold values from -6 to 6
- tissue: int32 [256, 512], P('row', 'col'), may hold values 0 or 1
- ln_gain: float32 [192], replicated, may hold values from 0.5 to 1.5
- in_weight: bfloat16 [192, 768], replicated, may hold values from -0.4375 to 0.4375
- conv_weight: bfloat16 [3, 3, 384], replicated, may hold values from -2 to 2
- conv_bias: float32 [384], replicated, may hold values from -3 to 3
- proj_weight: bfloat16 [4, 384, 44], replicated, may hold values from -0.3125 to 0.3125
- dt_weight: bfloat16 [4, 12, 384], replicated, may hold values from -1.75 to 1.75
- dt_bias: float32 [4, 384], replicated, may hold values from -4 to -1
- a_rate: float32 [4, 384, 16], replicated, may hold values from 0.001 to 1
- skip_d: float32 [4, 384], replicated, may hold values from 0.5 to 1.5
- out_gain: float32 [384], replicated, may hold values from 0.5 to 1.5
- out_weight: bfloat16 [384, 192], replicated, may hold values from -0.3125 to 0.3125
Outputs:
- result: bfloat16 [256, 512, 192], P('row', 'col')
Inputs may be any that keep to these rules, and one draw needn't show every extreme that they name: 1 marks a tissue token, 0 a background token.
All inputs are finite; a program needn't handle non-finite values. No bound on the sum of `tissue` on one device may be relied on, other than what follows from the above.
Results may differ from a plain program's by a relative error of at most 0.0055.
Values may be sent and summed in bfloat16 or wider, within the bound.
No kernel may reach another device: no remote copies, remote signals or barrier semaphores. Data moves between devices by JAX's collectives and lax.ppermute only.
A program may use at most 256 MiB of HBM per device.

v0:
```python
import functools

import jax
import jax.numpy as jnp
from jax import lax
from jax.experimental import pallas as pl
from jax.sharding import PartitionSpec as P


def padded_2(block, sides, width):
    for axis, dim in sides:
        count = lax.axis_size(axis)
        forward = [(i, i + 1) for i in range(count - 1)]
        backward = [(target, source) for source, target in forward]
        low = lax.ppermute(
            lax.slice_in_dim(block, block.shape[dim] - width, None, axis=dim), axis, forward
        )
        high = lax.ppermute(lax.slice_in_dim(block, 0, width, axis=dim), axis, backward)
        block = jnp.concatenate([low, block, high], axis=dim)
    return block


def layer_norm(values, gain):
    center = values - jnp.mean(values, axis=-1, keepdims=True)
    spread = jnp.mean(center * center, axis=-1, keepdims=True)
    return center * lax.rsqrt(spread + 1e-05) * gain


def conv_silu(padded, conv_weight, conv_bias, height, width):
    summed = jnp.broadcast_to(conv_bias, (height, width, conv_bias.shape[0]))
    for offset_row in range(3):
        for offset_col in range(3):
            window = padded[offset_row : offset_row + height, offset_col : offset_col + width]
            summed = summed + window.astype(jnp.float32) * conv_weight[
                offset_row, offset_col
            ].astype(jnp.float32)
    return jax.nn.silu(summed).astype(jnp.bfloat16)


def direction_inputs(seq_x, seq_mask, proj_one, dtw_one, dtb_one):
    rank = dtw_one.shape[0]
    nstate = (proj_one.shape[1] - rank) // 2
    length, seqs, inner = seq_x.shape
    flat = seq_x.reshape(length * seqs, inner)
    projections = jnp.dot(flat, proj_one, preferred_element_type=jnp.float32)
    rate_low = projections[:, :rank].astype(jnp.bfloat16)
    delta = jax.nn.softplus(
        jnp.dot(rate_low, dtw_one, preferred_element_type=jnp.float32) + dtb_one
    )
    delta = delta.reshape(length, seqs, inner) * seq_mask[:, :, None]
    entry = projections[:, rank : rank + nstate].reshape(length, seqs, nstate)
    readout = projections[:, rank + nstate :].reshape(length, seqs, nstate)
    return (delta, entry, readout)


def scan_kernel(neg_rate_ref, skip_ref, x_ref, delta_ref, entry_ref, readout_ref, *rest,
                length, reverse, with_init, with_y):
    rest = list(rest)
    init_ref = rest.pop(0) if with_init else None
    y_ref = rest.pop(0) if with_y else None
    state_ref = rest.pop(0)
    nstate = neg_rate_ref.shape[0]
    if with_init:
        state_ref[...] = init_ref[...]
    else:
        state_ref[...] = jnp.zeros(state_ref.shape, state_ref.dtype)

    def step(i, carry):
        t = length - 1 - i if reverse else i
        delta = delta_ref[t]
        x_wide = x_ref[t].astype(jnp.float32)
        drive = delta * x_wide
        entry = entry_ref[t]
        readout = readout_ref[t]
        total = jnp.zeros_like(delta)
        for n in range(nstate):
            state = (
                jnp.exp(delta * neg_rate_ref[pl.ds(n, 1), :]) * state_ref[n]
                + drive * entry[:, n : n + 1]
            )
            state_ref[n] = state
            if with_y:
                total = total + readout[:, n : n + 1] * state
        if with_y:
            y_ref[t] = total + skip_ref[...] * x_wide
        return carry

    lax.fori_loop(0, length, step, 0)


def run_scan(seq_x, delta, entry, readout, neg_rate, skip, init, reverse, with_y):
    length, seqs, inner = delta.shape
    nstate = neg_rate.shape[0]
    state_shape = jax.ShapeDtypeStruct((nstate, seqs, inner), jnp.float32)
    out_shape = [state_shape]
    if with_y:
        out_shape = [jax.ShapeDtypeStruct((length, seqs, inner), jnp.float32), state_shape]
    args = [neg_rate, skip.reshape(1, inner), seq_x, delta, entry, readout]
    if init is not None:
        args.append(init)
    kernel = functools.partial(
        scan_kernel, length=length, reverse=reverse, with_init=init is not None, with_y=with_y
    )
    return pl.pallas_call(kernel, out_shape=tuple(out_shape))(*args)


def combine(earlier, later, neg_rate):
    decay = jnp.exp(later[0][None] * neg_rate[:, None, :])
    return (earlier[0] + later[0], decay * earlier[1] + later[1])


def carried_in(total, end_state, neg_rate, axis, reverse):
    count = lax.axis_size(axis)
    inclusive = (total, end_state)
    exclusive = None
    shift = 1
    while shift < count:
        if reverse:
            pairs = [(i + shift, i) for i in range(count - shift)]
        else:
            pairs = [(i, i + shift) for i in range(count - shift)]
        got = tuple(lax.ppermute(a, axis, pairs) for a in inclusive)
        exclusive = got if exclusive is None else combine(got, exclusive, neg_rate)
        if 2 * shift < count:
            inclusive = combine(got, inclusive, neg_rate)
        shift *= 2
    if exclusive is None:
        return jnp.zeros_like(end_state)
    return exclusive[1]


def direction(seq_x, seq_mask, k, proj_weight, dt_weight, dt_bias, a_rate, skip_d, axis, reverse):
    delta, entry, readout = direction_inputs(
        seq_x, seq_mask, proj_weight[k], dt_weight[k], dt_bias[k]
    )
    neg_rate = -jnp.transpose(a_rate[k])
    (end_state,) = run_scan(seq_x, delta, entry, readout, neg_rate, skip_d[k], None, reverse, False)
    total = jnp.sum(delta, axis=0)
    init = carried_in(total, end_state, neg_rate, axis, reverse)
    y, _ = run_scan(seq_x, delta, entry, readout, neg_rate, skip_d[k], init, reverse, True)
    return y


def local(
    tokens,
    tissue,
    ln_gain,
    in_weight,
    conv_weight,
    conv_bias,
    proj_weight,
    dt_weight,
    dt_bias,
    a_rate,
    skip_d,
    out_gain,
    out_weight,
):
    rows_here, cols_here, width = tokens.shape
    inner = in_weight.shape[1] // 2
    normed = layer_norm(tokens.astype(jnp.float32), ln_gain).astype(jnp.bfloat16)
    projected = jnp.dot(
        normed.reshape(rows_here * cols_here, width), in_weight, preferred_element_type=jnp.float32
    )
    projected = projected.astype(jnp.bfloat16).reshape(rows_here, cols_here, 2 * inner)
    inner_part = projected[:, :, :inner]
    gate_part = projected[:, :, inner:]
    padded = padded_2(inner_part, (("row", 0), ("col", 1)), 1)
    conv_out = conv_silu(padded, conv_weight, conv_bias, rows_here, cols_here)
    tissue_wide = tissue.astype(jnp.float32)
    conv_t = jnp.transpose(conv_out, (1, 0, 2))
    tissue_t = jnp.transpose(tissue_wide)
    common = (proj_weight, dt_weight, dt_bias, a_rate, skip_d)
    along_rows = direction(conv_t, tissue_t, 0, *common, "col", False)
    along_rows = along_rows + direction(conv_t, tissue_t, 2, *common, "col", True)
    along_cols = direction(conv_out, tissue_wide, 1, *common, "row", False)
    along_cols = along_cols + direction(conv_out, tissue_wide, 3, *common, "row", True)
    mixed_sum = jnp.transpose(along_rows, (1, 0, 2)) + along_cols
    mixed = (layer_norm(mixed_sum, out_gain) * jax.nn.silu(gate_part.astype(jnp.float32))).astype(
        jnp.bfloat16
    )
    branch = jnp.dot(
        mixed.reshape(rows_here * cols_here, inner), out_weight, preferred_element_type=jnp.float32
    )
    branch = branch.reshape(rows_here, cols_here, width)
    return (tokens.astype(jnp.float32) + tissue_wide[:, :, None] * branch).astype(jnp.bfloat16)


def solution(mesh):
    return jax.shard_map(
        local,
        mesh=mesh,
        in_specs=(
            P("row", "col", None),
            P("row", "col"),
            P(),
            P(),
            P(),
            P(),
            P(),
            P(),
            P(),
            P(),
            P(),
            P(),
            P(),
        ),
        out_specs=P("row", "col", None),
        check_vma=False,
    )
```

profile of v0, /device:TPU:14, one launch (start us, length us, event | category | flops | bytes accessed | tf_op | source)
XLA Modules:
  0.0 289.3 jit_solution(10183582515242596828)
XLA Ops:
  3.8 2.1 collective-permute-start
  5.8 3.6 %collective-permute-start.1 = (bf16[1,16,384]{2,1,0:T(8,128)(2,1)S(1)}, bf16[1,16,384]{2,1,0:T(8,128)(2,1)S(1)}, u32[]{:S(2)}, u32[]{:S(2)}) collective-permute-start(bf16[1,16,384]{2,1,0:T(8,128)(2,1)S(1)} %get-tuple-element.43), channel_id=1, source_target_pairs={{32,0},{64,32},{96,64},{128,96},{160,128},{192,160},{224,192},{33,... | collective-permute-start | bytes 36872 | tf_op jit(solution)/shard_map/ppermute | solution.py:18
  11.3 3.8 %collective-permute-start.2 = (bf16[34,1,384]{2,1,0:T(2,128)(2,1)S(1)}, bf16[34,1,384]{2,1,0:T(2,128)(2,1)S(1)}, u32[]{:S(2)}, u32[]{:S(2)}) collective-permute-start(bf16[34,1,384]{2,1,0:T(2,128)(2,1)S(1)} %get-tuple-element.46), channel_id=1, source_target_pairs={{0,1},{1,2},{2,3},{3,4},{4,5},{5,6},{6,7},{7,8},{8,9},{9,10},{10,1... | collective-permute-start | bytes 78344 | tf_op jit(solution)/shard_map/ppermute | solution.py:15
  15.1 6.1 %collective-permute-start.3 = (bf16[34,1,384]{2,1,0:T(2,128)(2,1)S(1)}, bf16[34,1,384]{2,1,0:T(2,128)(2,1)S(1)}, u32[]{:S(2)}, u32[]{:S(2)}) collective-permute-start(bf16[34,1,384]{2,1,0:T(2,128)(2,1)S(1)} %get-tuple-element.47), channel_id=1, source_target_pairs={{1,0},{2,1},{3,2},{4,3},{5,4},{6,5},{7,6},{8,7},{9,8},{10,9},{11,1... | collective-permute-start | bytes 78344 | tf_op jit(solution)/shard_map/ppermute | solution.py:18
  21.4 1.7 collective-permute-done.3
  27.5 2.2 collective-permute-start.4
  31.3 5.2 %shard_map.127 = f32[16,32,384]{2,1,0:T(8,128)} custom-call(f32[16,384]{1,0:T(8,128)} %get-tuple-element.54.neg_rate_ref, f32[1,384]{1,0:T(1,128)} %get-tuple-element.74.skip_ref, bf16[16,32,384]{2,1,0:T(8,128)(2,1)} %copy-done.2, f32[16,32,384]{2,1,0:T(8,128)} %get-tuple-element.36.delta_ref, f32[16,32,16]{2,1,0:T(8,128)} %bitcast.80, f32[16,32,16]{2,1,0:T(8,128)} %bitcast.82), custom_call_target="tpu_custom_call" | custom-call | tf_op jit(solution)/shard_map/pallas_call | solution.py:104
  36.6 4.8 %collective-permute-start.8 = (f32[16,32,384]{2,1,0:T(8,128)}, f32[16,32,384]{2,1,0:T(8,128)S(1)}, u32[]{:S(2)}, u32[]{:S(2)}) collective-permute-start(f32[16,32,384]{2,1,0:T(8,128)} %shard_map.127), channel_id=1, source_target_pairs={{0,1},{1,2},{2,3},{3,4},{4,5},{5,6},{6,7},{7,8},{8,9},{9,10},{10,1... | collective-permute-start | bytes 2359304 | tf_op jit(solution)/shard_map/ppermute | solution.py:122
  41.4 3.3 %collective-permute-start.13 = (f32[32,384]{1,0:T(8,128)S(1)}, f32[32,384]{1,0:T(8,128)S(1)}, u32[]{:S(2)}, u32[]{:S(2)}) collective-permute-start(f32[32,384]{1,0:T(8,128)S(1)} %get-tuple-element.70), channel_id=1, source_target_pairs={{1,0},{2,1},{3,2},{4,3},{5,4},{6,5},{7,6},{8,7},{9,8},{10,9},{11,1... | collective-permute-start | bytes 147464 | tf_op jit(solution)/shard_map/ppermute | solution.py:122
  46.4 5.1 %shard_map.129 = f32[16,32,384]{2,1,0:T(8,128)} custom-call(f32[16,384]{1,0:T(8,128)} %get-tuple-element.55.neg_rate_ref, f32[1,384]{1,0:T(1,128)} %get-tuple-element.75.skip_ref, bf16[16,32,384]{2,1,0:T(8,128)(2,1)} %copy-done.2, f32[16,32,384]{2,1,0:T(8,128)} %get-tuple-element.71.delta_ref, f32[16,32,16]{2,1,0:T(8,128)} %bitcast.76, f32[16,32,16]{2,1,0:T(8,128)} %bitcast.78), custom_call_target="tpu_custom_call" | custom-call | tf_op jit(solution)/shard_map/pallas_call | solution.py:104
  51.6 3.9 %collective-permute-start.17 = (f32[16,32,384]{2,1,0:T(8,128)}, f32[16,32,384]{2,1,0:T(8,128)S(1)}, u32[]{:S(2)}, u32[]{:S(2)}) collective-permute-start(f32[16,32,384]{2,1,0:T(8,128)} %shard_map.129), channel_id=1, source_target_pairs={{1,0},{2,1},{3,2},{4,3},{5,4},{6,5},{7,6},{8,7},{9,8},{10,9},{11,1... | collective-permute-start | bytes 2359304 | tf_op jit(solution)/shard_map/ppermute | solution.py:122
  57.3 3.5 %collective-permute-start.5 = (f32[32,384]{1,0:T(8,128)S(1)}, f32[32,384]{1,0:T(8,128)S(1)}, u32[]{:S(2)}, u32[]{:S(2)}) collective-permute-start(f32[32,384]{1,0:T(8,128)S(1)} %add.250), channel_id=1, source_target_pairs={{0,2},{1,3},{2,4},{3,5},{4,6},{5,7},{6,8},{7,9},{8,10},{9,11},{10,... | collective-permute-start | bytes 147464 | tf_op jit(solution)/shard_map/ppermute | solution.py:122
  62.1 2.1 collective-permute-start.27
  64.2 2.4 collective-permute-start.22
  66.7 5.4 %collective-permute-start.14 = (f32[32,384]{1,0:T(8,128)S(1)}, f32[32,384]{1,0:T(8,128)S(1)}, u32[]{:S(2)}, u32[]{:S(2)}) collective-permute-start(f32[32,384]{1,0:T(8,128)S(1)} %add.268), channel_id=1, source_target_pairs={{2,0},{3,1},{4,2},{5,3},{6,4},{7,5},{8,6},{9,7},{10,8},{11,9},{12,... | collective-permute-start | bytes 147464 | tf_op jit(solution)/shard_map/ppermute | solution.py:122
  72.1 4.7 %collective-permute-start.6 = (f32[32,384]{1,0:T(8,128)S(1)}, f32[32,384]{1,0:T(8,128)S(1)}, u32[]{:S(2)}, u32[]{:S(2)}) collective-permute-start(f32[32,384]{1,0:T(8,128)S(1)} %add.251), channel_id=1, source_target_pairs={{0,4},{1,5},{2,6},{3,7},{4,8},{5,9},{6,10},{7,11},{8,12},{9,13},{1... | collective-permute-start | bytes 147464 | tf_op jit(solution)/shard_map/ppermute | solution.py:122
  77.5 1.9 collective-permute-start.28
  80.0 3.9 %collective-permute-start.23 = (f32[16,384]{1,0:T(8,128)}, f32[16,384]{1,0:T(8,128)}, u32[]{:S(2)}, u32[]{:S(2)}) collective-permute-start(f32[16,384]{1,0:T(8,128)} %add.287), channel_id=1, source_target_pairs={{0,64},{32,96},{64,128},{96,160},{128,192},{160,224},{1,65},{33,97... | collective-permute-start | bytes 73736 | tf_op jit(solution)/shard_map/ppermute | solution.py:122
  84.6 6.0 %collective-permute-start.15 = (f32[32,384]{1,0:T(8,128)}, f32[32,384]{1,0:T(8,128)}, u32[]{:S(2)}, u32[]{:S(2)}) collective-permute-start(f32[32,384]{1,0:T(8,128)} %add.269), channel_id=1, source_target_pairs={{4,0},{5,1},{6,2},{7,3},{8,4},{9,5},{10,6},{11,7},{12,8},{13,9},{1... | collective-permute-start | bytes 147464 | tf_op jit(solution)/shard_map/ppermute | solution.py:122
  92.9 1.9 collective-permute-start.9
  95.9 6.9 %collective-permute-start.18 = (f32[16,32,384]{2,1,0:T(8,128)}, f32[16,32,384]{2,1,0:T(8,128)S(1)}, u32[]{:S(2)}, u32[]{:S(2)}) collective-permute-start(f32[16,32,384]{2,1,0:T(8,128)} %multiply_add_fusion.3), channel_id=1, source_target_pairs={{2,0},{3,1},{4,2},{5,3},{6,4},{7,5},{8,6},{9,7},{10,8},{11,9},{12,... | collective-permute-start | bytes 2359304 | tf_op jit(solution)/shard_map/ppermute | solution.py:122
  105.1 1.6 copy.54
  106.7 1.6 copy.49
  108.3 1.6 copy.50
  109.9 6.1 %shard_map.133 = f32[16,16,384]{2,1,0:T(8,128)} custom-call(f32[16,384]{1,0:T(8,128)} %get-tuple-element.56.neg_rate_ref, f32[1,384]{1,0:T(1,128)} %get-tuple-element.76.skip_ref, bf16[32,16,384]{2,1,0:T(8,128)(2,1)} %copy-done.1, f32[32,16,384]{2,1,0:T(8,128)} %get-tuple-element.29.delta_ref, f32[32,16,16]{2,1,0:T(8,128)} %bitcast.88, f32[32,16,16]{2,1,0:T(8,128)} %bitcast.90), custom_call_target="tpu_custom_call" | custom-call | tf_op jit(solution)/shard_map/pallas_call | solution.py:104
  115.9 6.0 %shard_map.131 = f32[16,16,384]{2,1,0:T(8,128)} custom-call(f32[16,384]{1,0:T(8,128)} %get-tuple-element.57.neg_rate_ref, f32[1,384]{1,0:T(1,128)} %get-tuple-element.77.skip_ref, bf16[32,16,384]{2,1,0:T(8,128)(2,1)} %copy-done.1, f32[32,16,384]{2,1,0:T(8,128)} %get-tuple-element.69.delta_ref, f32[32,16,16]{2,1,0:T(8,128)} %bitcast.84, f32[32,16,16]{2,1,0:T(8,128)} %bitcast.86), custom_call_target="tpu_custom_call" | custom-call | tf_op jit(solution)/shard_map/pallas_call | solution.py:104
  122.7 1.9 collective-permute-start.29
  126.0 2.4 collective-permute-start.24
  129.3 4.5 %collective-permute-start.16 = (f32[32,384]{1,0:T(8,128)S(1)}, f32[32,384]{1,0:T(8,128)S(1)}, u32[]{:S(2)}, u32[]{:S(2)}) collective-permute-start(f32[32,384]{1,0:T(8,128)S(1)} %add.270), channel_id=1, source_target_pairs={{8,0},{9,1},{10,2},{11,3},{12,4},{13,5},{14,6},{15,7},{16,8},{17,9... | collective-permute-start | bytes 147464 | tf_op jit(solution)/shard_map/ppermute | solution.py:122
  138.4 3.6 %collective-permute-start.10 = (f32[16,32,384]{2,1,0:T(8,128)S(1)}, f32[16,32,384]{2,1,0:T(8,128)S(1)}, u32[]{:S(2)}, u32[]{:S(2)}) collective-permute-start(f32[16,32,384]{2,1,0:T(8,128)S(1)} %multiply_add_fusion.6), channel_id=1, source_target_pairs={{0,4},{1,5},{2,6},{3,7},{4,8},{5,9},{6,10},{7,11},{8,12},{9,13},{1... | collective-permute-start | bytes 2359304 | tf_op jit(solution)/shard_map/ppermute | solution.py:122
  143.4 7.3 %collective-permute-start.19 = (f32[16,32,384]{2,1,0:T(8,128)S(1)}, f32[16,32,384]{2,1,0:T(8,128)S(1)}, u32[]{:S(2)}, u32[]{:S(2)}) collective-permute-start(f32[16,32,384]{2,1,0:T(8,128)S(1)} %multiply_add_fusion.2), channel_id=1, source_target_pairs={{4,0},{5,1},{6,2},{7,3},{8,4},{9,5},{10,6},{11,7},{12,8},{13,9},{1... | collective-permute-start | bytes 2359304 | tf_op jit(solution)/shard_map/ppermute | solution.py:122
  150.8 3.0 %collective-permute-start.30 = (f32[16,16,384]{2,1,0:T(8,128)S(1)}, f32[16,16,384]{2,1,0:T(8,128)S(1)}, u32[]{:S(2)}, u32[]{:S(2)}) collective-permute-start(f32[16,16,384]{2,1,0:T(8,128)S(1)} %multiply_add_fusion.9), channel_id=1, source_target_pairs={{64,0},{96,32},{128,64},{160,96},{192,128},{224,160},{65,1},{97,33... | collective-permute-start | bytes 1179656 | tf_op jit(solution)/shard_map/ppermute | solution.py:122
  153.9 3.4 %collective-permute-start.25 = (f32[16,16,384]{2,1,0:T(8,128)S(1)}, f32[16,16,384]{2,1,0:T(8,128)S(1)}, u32[]{:S(2)}, u32[]{:S(2)}) collective-permute-start(f32[16,16,384]{2,1,0:T(8,128)S(1)} %multiply_add_fusion.11), channel_id=1, source_target_pairs={{0,64},{32,96},{64,128},{96,160},{128,192},{160,224},{1,65},{33,97... | collective-permute-start | bytes 1179656 | tf_op jit(solution)/shard_map/ppermute | solution.py:122
  157.4 18.8 %collective-permute-done.10 = f32[16,32,384]{2,1,0:T(8,128)S(1)} collective-permute-done((f32[16,32,384]{2,1,0:T(8,128)S(1)}, f32[16,32,384]{2,1,0:T(8,128)S(1)}, u32[]{:S(2)}, u32[]{:S(2)}) %collective-permute-start.10) | collective-permute-done | bytes 786464 | tf_op jit(solution)/shard_map/ppermute | solution.py:122
  177.7 15.7 %collective-permute-done.19 = f32[16,32,384]{2,1,0:T(8,128)S(1)} collective-permute-done((f32[16,32,384]{2,1,0:T(8,128)S(1)}, f32[16,32,384]{2,1,0:T(8,128)S(1)}, u32[]{:S(2)}, u32[]{:S(2)}) %collective-permute-start.19) | collective-permute-done | bytes 786464 | tf_op jit(solution)/shard_map/ppermute | solution.py:122
  194.4 18.6 %collective-permute-start.20 = (f32[16,32,384]{2,1,0:T(8,128)S(1)}, f32[16,32,384]{2,1,0:T(8,128)S(1)}, u32[]{:S(2)}, u32[]{:S(2)}) collective-permute-start(f32[16,32,384]{2,1,0:T(8,128)S(1)} %multiply_add_fusion.1), channel_id=1, source_target_pairs={{8,0},{9,1},{10,2},{11,3},{12,4},{13,5},{14,6},{15,7},{16,8},{17,9... | collective-permute-start | bytes 2359304 | tf_op jit(solution)/shard_map/ppermute | solution.py:122
  216.0 6.8 %collective-permute-start.26 = (f32[16,16,384]{2,1,0:T(8,128)}, f32[16,16,384]{2,1,0:T(8,128)}, u32[]{:S(2)}, u32[]{:S(2)}) collective-permute-start(f32[16,16,384]{2,1,0:T(8,128)} %multiply_add_fusion.10), channel_id=1, source_target_pairs={{0,128},{32,160},{64,192},{96,224},{1,129},{33,161},{65,193},{97,2... | collective-permute-start | bytes 1179656 | tf_op jit(solution)/shard_map/ppermute | solution.py:122
  222.8 1.9 multiply_add_fusion.4
  226.1 4.2 %collective-permute-done.20 = f32[16,32,384]{2,1,0:T(8,128)S(1)} collective-permute-done((f32[16,32,384]{2,1,0:T(8,128)S(1)}, f32[16,32,384]{2,1,0:T(8,128)S(1)}, u32[]{:S(2)}, u32[]{:S(2)}) %collective-permute-start.20) | collective-permute-done | bytes 786464 | tf_op jit(solution)/shard_map/ppermute | solution.py:122
  231.6 14.6 %collective-permute-start.21 = (f32[16,32,384]{2,1,0:T(8,128)}, f32[16,32,384]{2,1,0:T(8,128)}, u32[]{:S(2)}, u32[]{:S(2)}) collective-permute-start(f32[16,32,384]{2,1,0:T(8,128)} %multiply_add_fusion), channel_id=1, source_target_pairs={{16,0},{17,1},{18,2},{19,3},{20,4},{21,5},{22,6},{23,7},{24,8},{25... | collective-permute-start | bytes 2359304 | tf_op jit(solution)/shard_map/ppermute | solution.py:122
  247.1 8.0 %shard_map.134 = (f32[32,16,384]{2,1,0:T(8,128)}, f32[16,16,384]{2,1,0:T(8,128)}) custom-call(f32[16,384]{1,0:T(8,128)} %get-tuple-element.56.neg_rate_ref, f32[1,384]{1,0:T(1,128)} %get-tuple-element.76.skip_ref, bf16[32,16,384]{2,1,0:T(8,128)(2,1)} %copy-done.1, f32[32,16,384]{2,1,0:T(8,128)} %get-tuple-element.29.delta_ref, f32[32,16,16]{2,1,0:T(8,128)} %bitcast.89, ...), custom_call_target="tpu_custom_call" | custom-call | tf_op jit(solution)/shard_map/pallas_call | solution.py:104
  255.2 2.1 add_add_fusion.3.rest_0_
  257.3 8.0 %shard_map.132 = (f32[32,16,384]{2,1,0:T(8,128)}, f32[16,16,384]{2,1,0:T(8,128)}) custom-call(f32[16,384]{1,0:T(8,128)} %get-tuple-element.57.neg_rate_ref, f32[1,384]{1,0:T(1,128)} %get-tuple-element.77.skip_ref, bf16[32,16,384]{2,1,0:T(8,128)(2,1)} %copy-done.1, f32[32,16,384]{2,1,0:T(8,128)} %get-tuple-element.69.delta_ref, f32[32,16,16]{2,1,0:T(8,128)} %bitcast.85, ...), custom_call_target="tpu_custom_call" | custom-call | tf_op jit(solution)/shard_map/pallas_call | solution.py:104
  265.3 3.1 %add_add_fusion.1.rest_0_ = f32[16,32,384]{2,1,0:T(8,128)} fusion(f32[16,32,384]{2,1,0:T(8,128)S(1)} %collective-permute-done.8, f32[16,32,384]{2,1,0:T(8,128)} %collective-permute-done.9, f32[16,32,384]{2,1,0:T(8,128)S(1)} %collective-permute-done.10, f32[16,32,384]{2,1,0:T(8,128)} %copy-done.9, f32[16,32,384]{2,1,0:T(8,128)} %collective-permute-done.12, ...), kind=kLoop, calls=%fused_computation.26 | loop fusion | flops 2359296 | bytes 4939776 | tf_op jit(solution)/shard_map/add | solution.py:109
  268.3 7.0 %shard_map.128 = (f32[16,32,384]{2,1,0:T(8,128)}, f32[16,32,384]{2,1,0:T(8,128)}) custom-call(f32[16,384]{1,0:T(8,128)} %get-tuple-element.54.neg_rate_ref, f32[1,384]{1,0:T(1,128)} %get-tuple-element.74.skip_ref, bf16[16,32,384]{2,1,0:T(8,128)(2,1)} %copy-done.2, f32[16,32,384]{2,1,0:T(8,128)} %get-tuple-element.36.delta_ref, f32[16,32,16]{2,1,0:T(8,128)} %bitcast.81, ...), custom_call_target="tpu_custom_call" | custom-call | tf_op jit(solution)/shard_map/pallas_call | solution.py:104
  275.3 2.6 add_add_fusion.rest_0_
  277.9 7.0 %shard_map.130 = (f32[16,32,384]{2,1,0:T(8,128)}, f32[16,32,384]{2,1,0:T(8,128)}) custom-call(f32[16,384]{1,0:T(8,128)} %get-tuple-element.55.neg_rate_ref, f32[1,384]{1,0:T(1,128)} %get-tuple-element.75.skip_ref, bf16[16,32,384]{2,1,0:T(8,128)(2,1)} %copy-done.2, f32[16,32,384]{2,1,0:T(8,128)} %get-tuple-element.71.delta_ref, f32[16,32,16]{2,1,0:T(8,128)} %bitcast.77, ...), custom_call_target="tpu_custom_call" | custom-call | tf_op jit(solution)/shard_map/pallas_call | solution.py:104
  284.9 2.2 fusion.19
  (215 shorter events, 43.8 us)
Async XLA Ops:
  3.8 7.4 %collective-permute-start = (bf16[1,16,384]{2,1,0:T(8,128)(2,1)S(1)}, bf16[1,16,384]{2,1,0:T(8,128)(2,1)S(1)}, u32[]{:S(2)}, u32[]{:S(2)}) collective-permute-start(bf16[1,16,384]{2,1,0:T(8,128)(2,1)S(1)} %get-tuple-element.42), channel_id=1, source_target_pairs={{0,32},{32,64},{64,96},{96,128},{128,160},{160,192},{192,224},{1,3... | collective-permute-start | bytes 36872 | tf_op jit(solution)/shard_map/ppermute | solution.py:15
  5.8 5.3 %collective-permute-start.1 = (bf16[1,16,384]{2,1,0:T(8,128)(2,1)S(1)}, bf16[1,16,384]{2,1,0:T(8,128)(2,1)S(1)}, u32[]{:S(2)}, u32[]{:S(2)}) collective-permute-start(bf16[1,16,384]{2,1,0:T(8,128)(2,1)S(1)} %get-tuple-element.43), channel_id=1, source_target_pairs={{32,0},{64,32},{96,64},{128,96},{160,128},{192,160},{224,192},{33,... | collective-permute-start | bytes 36872 | tf_op jit(solution)/shard_map/ppermute | solution.py:18
  11.3 10.1 %collective-permute-start.2 = (bf16[34,1,384]{2,1,0:T(2,128)(2,1)S(1)}, bf16[34,1,384]{2,1,0:T(2,128)(2,1)S(1)}, u32[]{:S(2)}, u32[]{:S(2)}) collective-permute-start(bf16[34,1,384]{2,1,0:T(2,128)(2,1)S(1)} %get-tuple-element.46), channel_id=1, source_target_pairs={{0,1},{1,2},{2,3},{3,4},{4,5},{5,6},{6,7},{7,8},{8,9},{9,10},{10,1... | collective-permute-start | bytes 78344 | tf_op jit(solution)/shard_map/ppermute | solution.py:15
  15.1 7.9 %collective-permute-start.3 = (bf16[34,1,384]{2,1,0:T(2,128)(2,1)S(1)}, bf16[34,1,384]{2,1,0:T(2,128)(2,1)S(1)}, u32[]{:S(2)}, u32[]{:S(2)}) collective-permute-start(bf16[34,1,384]{2,1,0:T(2,128)(2,1)S(1)} %get-tuple-element.47), channel_id=1, source_target_pairs={{1,0},{2,1},{3,2},{4,3},{5,4},{6,5},{7,6},{8,7},{9,8},{10,9},{11,1... | collective-permute-start | bytes 78344 | tf_op jit(solution)/shard_map/ppermute | solution.py:18
  24.2 31.5 %copy-start.1 = (bf16[32,16,384]{2,1,0:T(8,128)(2,1)}, bf16[32,16,384]{2,1,0:T(8,128)(2,1)S(1)}, u32[]{:S(2)}) copy-start(bf16[32,16,384]{2,1,0:T(8,128)(2,1)S(1)} %multiply_convert_fusion.x_ref) | copy-start | bytes 1179652
  27.5 29.7 %collective-permute-start.4 = (f32[32,384]{1,0:T(8,128)S(1)}, f32[32,384]{1,0:T(8,128)S(1)}, u32[]{:S(2)}, u32[]{:S(2)}) collective-permute-start(f32[32,384]{1,0:T(8,128)S(1)} %get-tuple-element.35), channel_id=1, source_target_pairs={{0,1},{1,2},{2,3},{3,4},{4,5},{5,6},{6,7},{7,8},{8,9},{9,10},{10,1... | collective-permute-start | bytes 147464 | tf_op jit(solution)/shard_map/ppermute | solution.py:122
  36.6 54.6 %collective-permute-start.8 = (f32[16,32,384]{2,1,0:T(8,128)}, f32[16,32,384]{2,1,0:T(8,128)S(1)}, u32[]{:S(2)}, u32[]{:S(2)}) collective-permute-start(f32[16,32,384]{2,1,0:T(8,128)} %shard_map.127), channel_id=1, source_target_pairs={{0,1},{1,2},{2,3},{3,4},{4,5},{5,6},{6,7},{7,8},{8,9},{9,10},{10,1... | collective-permute-start | bytes 2359304 | tf_op jit(solution)/shard_map/ppermute | solution.py:122
  41.4 22.7 %collective-permute-start.13 = (f32[32,384]{1,0:T(8,128)S(1)}, f32[32,384]{1,0:T(8,128)S(1)}, u32[]{:S(2)}, u32[]{:S(2)}) collective-permute-start(f32[32,384]{1,0:T(8,128)S(1)} %get-tuple-element.70), channel_id=1, source_target_pairs={{1,0},{2,1},{3,2},{4,3},{5,4},{6,5},{7,6},{8,7},{9,8},{10,9},{11,1... | collective-permute-start | bytes 147464 | tf_op jit(solution)/shard_map/ppermute | solution.py:122
  51.6 41.3 %collective-permute-start.17 = (f32[16,32,384]{2,1,0:T(8,128)}, f32[16,32,384]{2,1,0:T(8,128)S(1)}, u32[]{:S(2)}, u32[]{:S(2)}) collective-permute-start(f32[16,32,384]{2,1,0:T(8,128)} %shard_map.129), channel_id=1, source_target_pairs={{1,0},{2,1},{3,2},{4,3},{5,4},{6,5},{7,6},{8,7},{9,8},{10,9},{11,1... | collective-permute-start | bytes 2359304 | tf_op jit(solution)/shard_map/ppermute | solution.py:122
  57.3 14.8 %copy-start.32 = (f32[32,384]{1,0:T(8,128)}, f32[32,384]{1,0:T(8,128)S(1)}, u32[]{:S(2)}) copy-start(f32[32,384]{1,0:T(8,128)S(1)} %add.250) | copy-start | bytes 147460
  57.3 9.4 %collective-permute-start.5 = (f32[32,384]{1,0:T(8,128)S(1)}, f32[32,384]{1,0:T(8,128)S(1)}, u32[]{:S(2)}, u32[]{:S(2)}) collective-permute-start(f32[32,384]{1,0:T(8,128)S(1)} %add.250), channel_id=1, source_target_pairs={{0,2},{1,3},{2,4},{3,5},{4,6},{5,7},{6,8},{7,9},{8,10},{9,11},{10,... | collective-permute-start | bytes 147464 | tf_op jit(solution)/shard_map/ppermute | solution.py:122
  62.1 30.7 %copy-start.36 = (f32[16,384]{1,0:T(8,128)}, f32[16,384]{1,0:T(8,128)S(1)}, u32[]{:S(2)}) copy-start(f32[16,384]{1,0:T(8,128)S(1)} %get-tuple-element.68) | copy-start | bytes 73732
  62.1 30.7 %copy-start.38 = (f32[16,384]{1,0:T(8,128)}, f32[16,384]{1,0:T(8,128)S(1)}, u32[]{:S(2)}) copy-start(f32[16,384]{1,0:T(8,128)S(1)} %get-tuple-element.28) | copy-start | bytes 73732
  62.1 30.5 %copy-start.7 = (f32[16,32,384]{2,1,0:T(8,128)S(1)}, f32[16,32,384]{2,1,0:T(8,128)}, u32[]{:S(2)}) copy-start(f32[16,32,384]{2,1,0:T(8,128)} %shard_map.127) | copy-start | bytes 2359300
  62.1 30.6 %copy-start.15 = (f32[16,384]{1,0:T(8,128)S(1)}, f32[16,384]{1,0:T(8,128)}, u32[]{:S(2)}) copy-start(f32[16,384]{1,0:T(8,128)} %get-tuple-element.54.neg_rate_ref) | copy-start | bytes 73732
  62.1 10.0 %collective-permute-start.27 = (f32[16,384]{1,0:T(8,128)S(1)}, f32[16,384]{1,0:T(8,128)S(1)}, u32[]{:S(2)}, u32[]{:S(2)}) collective-permute-start(f32[16,384]{1,0:T(8,128)S(1)} %get-tuple-element.28), channel_id=1, source_target_pairs={{32,0},{64,32},{96,64},{128,96},{160,128},{192,160},{224,192},{33,... | collective-permute-start | bytes 73736 | tf_op jit(solution)/shard_map/ppermute | solution.py:122
  64.2 71.4 %copy-start.26 = (f32[32,384]{1,0:T(8,128)}, f32[32,384]{1,0:T(8,128)S(1)}, u32[]{:S(2)}) copy-start(f32[32,384]{1,0:T(8,128)S(1)} %collective-permute-done.13) | copy-start | bytes 147460
  64.2 13.2 %collective-permute-start.22 = (f32[16,384]{1,0:T(8,128)S(1)}, f32[16,384]{1,0:T(8,128)S(1)}, u32[]{:S(2)}, u32[]{:S(2)}) collective-permute-start(f32[16,384]{1,0:T(8,128)S(1)} %get-tuple-element.68), channel_id=1, source_target_pairs={{0,32},{32,64},{64,96},{96,128},{128,160},{160,192},{192,224},{1,3... | collective-permute-start | bytes 73736 | tf_op jit(solution)/shard_map/ppermute | solution.py:122
  66.6 26.2 %copy-start.34 = (f32[32,384]{1,0:T(8,128)}, f32[32,384]{1,0:T(8,128)S(1)}, u32[]{:S(2)}) copy-start(f32[32,384]{1,0:T(8,128)S(1)} %add.268) | copy-start | bytes 147460
  66.7 24.5 %copy-start.44 = (f32[32,384]{1,0:T(8,128)}, f32[32,384]{1,0:T(8,128)S(1)}, u32[]{:S(2)}) copy-start(f32[32,384]{1,0:T(8,128)S(1)} %collective-permute-done.5) | copy-start | bytes 147460
  66.7 13.3 %collective-permute-start.14 = (f32[32,384]{1,0:T(8,128)S(1)}, f32[32,384]{1,0:T(8,128)S(1)}, u32[]{:S(2)}, u32[]{:S(2)}) collective-permute-start(f32[32,384]{1,0:T(8,128)S(1)} %add.268), channel_id=1, source_target_pairs={{2,0},{3,1},{4,2},{5,3},{6,4},{7,5},{8,6},{9,7},{10,8},{11,9},{12,... | collective-permute-start | bytes 147464 | tf_op jit(solution)/shard_map/ppermute | solution.py:122
  72.1 19.1 %copy-start.30 = (f32[32,384]{1,0:T(8,128)}, f32[32,384]{1,0:T(8,128)S(1)}, u32[]{:S(2)}) copy-start(f32[32,384]{1,0:T(8,128)S(1)} %add.251) | copy-start | bytes 147460
  72.1 19.1 %copy-start.42 = (f32[16,384]{1,0:T(8,128)}, f32[16,384]{1,0:T(8,128)S(1)}, u32[]{:S(2)}) copy-start(f32[16,384]{1,0:T(8,128)S(1)} %collective-permute-done.27) | copy-start | bytes 73732
  72.1 12.4 %collective-permute-start.6 = (f32[32,384]{1,0:T(8,128)S(1)}, f32[32,384]{1,0:T(8,128)S(1)}, u32[]{:S(2)}, u32[]{:S(2)}) collective-permute-start(f32[32,384]{1,0:T(8,128)S(1)} %add.251), channel_id=1, source_target_pairs={{0,4},{1,5},{2,6},{3,7},{4,8},{5,9},{6,10},{7,11},{8,12},{9,13},{1... | collective-permute-start | bytes 147464 | tf_op jit(solution)/shard_map/ppermute | solution.py:122
  77.4 15.4 %copy-start.49 = (f32[16,384]{1,0:T(8,128)}, f32[16,384]{1,0:T(8,128)S(1)}, u32[]{:S(2)}) copy-start(f32[16,384]{1,0:T(8,128)S(1)} %add.297) | copy-start | bytes 73732
  77.5 18.5 %collective-permute-start.28 = (f32[16,384]{1,0:T(8,128)S(1)}, f32[16,384]{1,0:T(8,128)}, u32[]{:S(2)}, u32[]{:S(2)}) collective-permute-start(f32[16,384]{1,0:T(8,128)S(1)} %add.297), channel_id=1, source_target_pairs={{64,0},{96,32},{128,64},{160,96},{192,128},{224,160},{65,1},{97,33... | collective-permute-start | bytes 73736 | tf_op jit(solution)/shard_map/ppermute | solution.py:122
  80.0 42.7 %collective-permute-start.23 = (f32[16,384]{1,0:T(8,128)}, f32[16,384]{1,0:T(8,128)}, u32[]{:S(2)}, u32[]{:S(2)}) collective-permute-start(f32[16,384]{1,0:T(8,128)} %add.287), channel_id=1, source_target_pairs={{0,64},{32,96},{64,128},{96,160},{128,192},{160,224},{1,65},{33,97... | collective-permute-start | bytes 73736 | tf_op jit(solution)/shard_map/ppermute | solution.py:122
  84.6 41.5 %collective-permute-start.15 = (f32[32,384]{1,0:T(8,128)}, f32[32,384]{1,0:T(8,128)}, u32[]{:S(2)}, u32[]{:S(2)}) collective-permute-start(f32[32,384]{1,0:T(8,128)} %add.269), channel_id=1, source_target_pairs={{4,0},{5,1},{6,2},{7,3},{8,4},{9,5},{10,6},{11,7},{12,8},{13,9},{1... | collective-permute-start | bytes 147464 | tf_op jit(solution)/shard_map/ppermute | solution.py:122
  91.2 38.1 %collective-permute-start.7 = (f32[32,384]{1,0:T(8,128)}, f32[32,384]{1,0:T(8,128)}, u32[]{:S(2)}, u32[]{:S(2)}) collective-permute-start(f32[32,384]{1,0:T(8,128)} %add.252), channel_id=1, source_target_pairs={{0,8},{1,9},{2,10},{3,11},{4,12},{5,13},{6,14},{7,15},{8,16},{9,17... | collective-permute-start | bytes 147464 | tf_op jit(solution)/shard_map/ppermute | solution.py:122
  92.9 44.2 %collective-permute-start.9 = (f32[16,32,384]{2,1,0:T(8,128)S(1)}, f32[16,32,384]{2,1,0:T(8,128)}, u32[]{:S(2)}, u32[]{:S(2)}) collective-permute-start(f32[16,32,384]{2,1,0:T(8,128)S(1)} %multiply_add_fusion.7), channel_id=1, source_target_pairs={{0,2},{1,3},{2,4},{3,5},{4,6},{5,7},{6,8},{7,9},{8,10},{9,11},{10,... | collective-permute-start | bytes 2359304 | tf_op jit(solution)/shard_map/ppermute | solution.py:122
  95.9 46.1 %collective-permute-start.18 = (f32[16,32,384]{2,1,0:T(8,128)}, f32[16,32,384]{2,1,0:T(8,128)S(1)}, u32[]{:S(2)}, u32[]{:S(2)}) collective-permute-start(f32[16,32,384]{2,1,0:T(8,128)} %multiply_add_fusion.3), channel_id=1, source_target_pairs={{2,0},{3,1},{4,2},{5,3},{6,4},{7,5},{8,6},{9,7},{10,8},{11,9},{12,... | collective-permute-start | bytes 2359304 | tf_op jit(solution)/shard_map/ppermute | solution.py:122
  122.0 15.1 %copy-start.33 = (f32[32,384]{1,0:T(8,128)S(1)}, f32[32,384]{1,0:T(8,128)}, u32[]{:S(2)}) copy-start(f32[32,384]{1,0:T(8,128)} %copy-done.32) | copy-start | bytes 147460
  122.7 27.9 %collective-permute-start.29 = (f32[16,16,384]{2,1,0:T(8,128)}, f32[16,16,384]{2,1,0:T(8,128)S(1)}, u32[]{:S(2)}, u32[]{:S(2)}) collective-permute-start(f32[16,16,384]{2,1,0:T(8,128)} %shard_map.133), channel_id=1, source_target_pairs={{32,0},{64,32},{96,64},{128,96},{160,128},{192,160},{224,192},{33,... | collective-permute-start | bytes 1179656 | tf_op jit(solution)/shard_map/ppermute | solution.py:122
  126.0 27.8 %collective-permute-start.24 = (f32[16,16,384]{2,1,0:T(8,128)}, f32[16,16,384]{2,1,0:T(8,128)S(1)}, u32[]{:S(2)}, u32[]{:S(2)}) collective-permute-start(f32[16,16,384]{2,1,0:T(8,128)} %shard_map.131), channel_id=1, source_target_pairs={{0,32},{32,64},{64,96},{96,128},{128,160},{160,192},{192,224},{1,3... | collective-permute-start | bytes 1179656 | tf_op jit(solution)/shard_map/ppermute | solution.py:122
  129.3 6.3 %collective-permute-start.16 = (f32[32,384]{1,0:T(8,128)S(1)}, f32[32,384]{1,0:T(8,128)S(1)}, u32[]{:S(2)}, u32[]{:S(2)}) collective-permute-start(f32[32,384]{1,0:T(8,128)S(1)} %add.270), channel_id=1, source_target_pairs={{8,0},{9,1},{10,2},{11,3},{12,4},{13,5},{14,6},{15,7},{16,8},{17,9... | collective-permute-start | bytes 147464 | tf_op jit(solution)/shard_map/ppermute | solution.py:122
  138.4 37.8 %collective-permute-start.10 = (f32[16,32,384]{2,1,0:T(8,128)S(1)}, f32[16,32,384]{2,1,0:T(8,128)S(1)}, u32[]{:S(2)}, u32[]{:S(2)}) collective-permute-start(f32[16,32,384]{2,1,0:T(8,128)S(1)} %multiply_add_fusion.6), channel_id=1, source_target_pairs={{0,4},{1,5},{2,6},{3,7},{4,8},{5,9},{6,10},{7,11},{8,12},{9,13},{1... | collective-permute-start | bytes 2359304 | tf_op jit(solution)/shard_map/ppermute | solution.py:122
  143.4 50.0 %collective-permute-start.19 = (f32[16,32,384]{2,1,0:T(8,128)S(1)}, f32[16,32,384]{2,1,0:T(8,128)S(1)}, u32[]{:S(2)}, u32[]{:S(2)}) collective-permute-start(f32[16,32,384]{2,1,0:T(8,128)S(1)} %multiply_add_fusion.2), channel_id=1, source_target_pairs={{4,0},{5,1},{6,2},{7,3},{8,4},{9,5},{10,6},{11,7},{12,8},{13,9},{1... | collective-permute-start | bytes 2359304 | tf_op jit(solution)/shard_map/ppermute | solution.py:122
  150.8 25.4 %copy-start.31 = (f32[32,384]{1,0:T(8,128)S(1)}, f32[32,384]{1,0:T(8,128)}, u32[]{:S(2)}) copy-start(f32[32,384]{1,0:T(8,128)} %copy-done.30) | copy-start | bytes 147460
  150.8 62.2 %collective-permute-start.30 = (f32[16,16,384]{2,1,0:T(8,128)S(1)}, f32[16,16,384]{2,1,0:T(8,128)S(1)}, u32[]{:S(2)}, u32[]{:S(2)}) collective-permute-start(f32[16,16,384]{2,1,0:T(8,128)S(1)} %multiply_add_fusion.9), channel_id=1, source_target_pairs={{64,0},{96,32},{128,64},{160,96},{192,128},{224,160},{65,1},{97,33... | collective-permute-start | bytes 1179656 | tf_op jit(solution)/shard_map/ppermute | solution.py:122
  153.9 60.5 %collective-permute-start.25 = (f32[16,16,384]{2,1,0:T(8,128)S(1)}, f32[16,16,384]{2,1,0:T(8,128)S(1)}, u32[]{:S(2)}, u32[]{:S(2)}) collective-permute-start(f32[16,16,384]{2,1,0:T(8,128)S(1)} %multiply_add_fusion.11), channel_id=1, source_target_pairs={{0,64},{32,96},{64,128},{96,160},{128,192},{160,224},{1,65},{33,97... | collective-permute-start | bytes 1179656 | tf_op jit(solution)/shard_map/ppermute | solution.py:122
  176.4 36.6 %copy-start.50 = (f32[16,384]{1,0:T(8,128)S(1)}, f32[16,384]{1,0:T(8,128)}, u32[]{:S(2)}) copy-start(f32[16,384]{1,0:T(8,128)} %copy-done.49) | copy-start | bytes 73732
  176.4 46.4 %collective-permute-start.11 = (f32[16,32,384]{2,1,0:T(8,128)S(1)}, f32[16,32,384]{2,1,0:T(8,128)S(1)}, u32[]{:S(2)}, u32[]{:S(2)}) collective-permute-start(f32[16,32,384]{2,1,0:T(8,128)S(1)} %multiply_add_fusion.5), channel_id=1, source_target_pairs={{0,8},{1,9},{2,10},{3,11},{4,12},{5,13},{6,14},{7,15},{8,16},{9,17... | collective-permute-start | bytes 2359304 | tf_op jit(solution)/shard_map/ppermute | solution.py:122
  194.4 36.0 %collective-permute-start.20 = (f32[16,32,384]{2,1,0:T(8,128)S(1)}, f32[16,32,384]{2,1,0:T(8,128)S(1)}, u32[]{:S(2)}, u32[]{:S(2)}) collective-permute-start(f32[16,32,384]{2,1,0:T(8,128)S(1)} %multiply_add_fusion.1), channel_id=1, source_target_pairs={{8,0},{9,1},{10,2},{11,3},{12,4},{13,5},{14,6},{15,7},{16,8},{17,9... | collective-permute-start | bytes 2359304 | tf_op jit(solution)/shard_map/ppermute | solution.py:122
  213.1 33.1 %collective-permute-start.31 = (f32[16,16,384]{2,1,0:T(8,128)S(1)}, f32[16,16,384]{2,1,0:T(8,128)S(1)}, u32[]{:S(2)}, u32[]{:S(2)}) collective-permute-start(f32[16,16,384]{2,1,0:T(8,128)S(1)} %multiply_add_fusion.8), channel_id=1, source_target_pairs={{128,0},{160,32},{192,64},{224,96},{129,1},{161,33},{193,65},{225,... | collective-permute-start | bytes 1179656 | tf_op jit(solution)/shard_map/ppermute | solution.py:122
  216.0 39.2 %collective-permute-start.26 = (f32[16,16,384]{2,1,0:T(8,128)}, f32[16,16,384]{2,1,0:T(8,128)}, u32[]{:S(2)}, u32[]{:S(2)}) collective-permute-start(f32[16,16,384]{2,1,0:T(8,128)} %multiply_add_fusion.10), channel_id=1, source_target_pairs={{0,128},{32,160},{64,192},{96,224},{1,129},{33,161},{65,193},{97,2... | collective-permute-start | bytes 1179656 | tf_op jit(solution)/shard_map/ppermute | solution.py:122
  224.7 21.5 %copy-start.43 = (f32[16,384]{1,0:T(8,128)S(1)}, f32[16,384]{1,0:T(8,128)}, u32[]{:S(2)}) copy-start(f32[16,384]{1,0:T(8,128)} %copy-done.42) | copy-start | bytes 73732
  224.7 40.6 %collective-permute-start.12 = (f32[16,32,384]{2,1,0:T(8,128)}, f32[16,32,384]{2,1,0:T(8,128)}, u32[]{:S(2)}, u32[]{:S(2)}) collective-permute-start(f32[16,32,384]{2,1,0:T(8,128)} %multiply_add_fusion.4), channel_id=1, source_target_pairs={{0,16},{1,17},{2,18},{3,19},{4,20},{5,21},{6,22},{7,23},{8,24},{9,... | collective-permute-start | bytes 2359304 | tf_op jit(solution)/shard_map/ppermute | solution.py:122
  231.6 43.7 %collective-permute-start.21 = (f32[16,32,384]{2,1,0:T(8,128)}, f32[16,32,384]{2,1,0:T(8,128)}, u32[]{:S(2)}, u32[]{:S(2)}) collective-permute-start(f32[16,32,384]{2,1,0:T(8,128)} %multiply_add_fusion), channel_id=1, source_target_pairs={{16,0},{17,1},{18,2},{19,3},{20,4},{21,5},{22,6},{23,7},{24,8},{25... | collective-permute-start | bytes 2359304 | tf_op jit(solution)/shard_map/ppermute | solution.py:122
  (42 other events, 265.8 us)
where the time goes:
time: 292 us; the launch traced here: 289 us
  starting transfers between devices  140 us (48%)
  Pallas kernels  52.5 us (18%)
  waiting for transfers between devices  40.7 us (14%)
  other arithmetic  36.7 us (13%)
  local copies, waits for them, and re-layouts  13.1 us (4%)
  matrix products  4.88 us (2%)
    ppermute x28, starting transfers between devices, carried_in(): got = tuple((lax.ppermute(a, axis, pairs) for a in inclusive))  124 us
    pallas_call x8, Pallas kernels, run_scan(): return pl.pallas_call(kernel, out_shape=tuple(out_shape))(*args)  52.5 us
    ppermute x28, waiting for transfers between devices, carried_in(): got = tuple((lax.ppermute(a, axis, pairs) for a in inclusive))  39 us
    add x28, other arithmetic, combine(): return (earlier[0] + later[0], decay * earlier[1] + later[1])  26.4 us
    ppermute x2, starting transfers between devices, padded_2(): lax.ppermute(lax.slice_in_dim(block, 0, width, axis=dim), axis, backward)  9.76 us
    slice x8, local copies, waits for them, and re-layouts, direction_inputs(): readout = projections[:, rank + nstate:].reshape(length, seqs, nstate)  6.18 us
    ppermute x2, starting transfers between devices, padded_2(): lax.ppermute(lax.slice_in_dim(block, block.shape[dim] - width, None, axis...  5.88 us
  transfers between devices with their start and end apart: 32, of which 5 were waited for; matrix products, arithmetic and copies ran while one was open for 14% of the time, Pallas kernels for 16%

commit v1 on v0

--- a/solution.py
+++ b/solution.py
@@ -9,7 +9,7 @@
 
 def padded_2(block, sides, width):
     for axis, dim in sides:
-        count = lax.axis_size(axis)
+        count = axis_count(axis)
         forward = [(i, i + 1) for i in range(count - 1)]
         backward = [(target, source) for source, target in forward]
         low = lax.ppermute(
@@ -18,6 +18,15 @@
         high = lax.ppermute(lax.slice_in_dim(block, 0, width, axis=dim), axis, backward)
         block = jnp.concatenate([low, block, high], axis=dim)
     return block
+
+
+def axis_count(axis):
+    if isinstance(axis, tuple):
+        count = 1
+        for name in axis:
+            count *= lax.axis_size(name)
+        return count
+    return lax.axis_size(axis)
 
 
 def layer_norm(values, gain):
@@ -65,7 +74,7 @@
     else:
         state_ref[...] = jnp.zeros(state_ref.shape, state_ref.dtype)
 
-    def step(i, carry):
+    def step(i, summed):
         t = length - 1 - i if reverse else i
         delta = delta_ref[t]
         x_wide = x_ref[t].astype(jnp.float32)
@@ -83,15 +92,16 @@
                 total = total + readout[:, n : n + 1] * state
         if with_y:
             y_ref[t] = total + skip_ref[...] * x_wide
-        return carry
-
-    lax.fori_loop(0, length, step, 0)
+        return summed + delta
+
+    summed = lax.fori_loop(0, length, step, jnp.zeros(state_ref.shape[1:], jnp.float32))
+    state_ref[nstate] = summed
 
 
 def run_scan(seq_x, delta, entry, readout, neg_rate, skip, init, reverse, with_y):
     length, seqs, inner = delta.shape
     nstate = neg_rate.shape[0]
-    state_shape = jax.ShapeDtypeStruct((nstate, seqs, inner), jnp.float32)
+    state_shape = jax.ShapeDtypeStruct((nstate + 1, seqs, inner), jnp.float32)
     out_shape = [state_shape]
     if with_y:
         out_shape = [jax.ShapeDtypeStruct((length, seqs, inner), jnp.float32), state_shape]
@@ -105,13 +115,15 @@
 
 
 def combine(earlier, later, neg_rate):
-    decay = jnp.exp(later[0][None] * neg_rate[:, None, :])
-    return (earlier[0] + later[0], decay * earlier[1] + later[1])
-
-
-def carried_in(total, end_state, neg_rate, axis, reverse):
+    nstate = neg_rate.shape[0]
+    decay = jnp.exp(later[nstate][None] * neg_rate[:, None, :])
+    state = decay * earlier[:nstate] + later[:nstate]
+    return jnp.concatenate([state, (earlier[nstate] + later[nstate])[None]], axis=0)
+
+
+def carried_in(packed, neg_rate, axis, reverse):
     count = lax.axis_size(axis)
-    inclusive = (total, end_state)
+    inclusive = packed
     exclusive = None
     shift = 1
     while shift < count:
@@ -119,14 +131,14 @@
             pairs = [(i + shift, i) for i in range(count - shift)]
         else:
             pairs = [(i, i + shift) for i in range(count - shift)]
-        got = tuple(lax.ppermute(a, axis, pairs) for a in inclusive)
+        got = lax.ppermute(inclusive, axis, pairs)
         exclusive = got if exclusive is None else combine(got, exclusive, neg_rate)
         if 2 * shift < count:
             inclusive = combine(got, inclusive, neg_rate)
         shift *= 2
     if exclusive is None:
-        return jnp.zeros_like(end_state)
-    return exclusive[1]
+        return jnp.zeros_like(packed)
+    return exclusive
 
 
 def direction(seq_x, seq_mask, k, proj_weight, dt_weight, dt_bias, a_rate, skip_d, axis, reverse):
@@ -134,9 +146,8 @@
         seq_x, seq_mask, proj_weight[k], dt_weight[k], dt_bias[k]
     )
     neg_rate = -jnp.transpose(a_rate[k])
-    (end_state,) = run_scan(seq_x, delta, entry, readout, neg_rate, skip_d[k], None, reverse, False)
-    total = jnp.sum(delta, axis=0)
-    init = carried_in(total, end_state, neg_rate, axis, reverse)
+    (packed,) = run_scan(seq_x, delta, entry, readout, neg_rate, skip_d[k], None, reverse, False)
+    init = carried_in(packed, neg_rate, axis, reverse)
     y, _ = run_scan(seq_x, delta, entry, readout, neg_rate, skip_d[k], init, reverse, True)
     return y
 
@@ -165,14 +176,17 @@
     projected = projected.astype(jnp.bfloat16).reshape(rows_here, cols_here, 2 * inner)
     inner_part = projected[:, :, :inner]
     gate_part = projected[:, :, inner:]
-    padded = padded_2(inner_part, (("row", 0), ("col", 1)), 1)
+    padded = padded_2(inner_part, (("row", 0), (("cx", "cz"), 1)), 1)
     conv_out = conv_silu(padded, conv_weight, conv_bias, rows_here, cols_here)
     tissue_wide = tissue.astype(jnp.float32)
-    conv_t = jnp.transpose(conv_out, (1, 0, 2))
-    tissue_t = jnp.transpose(tissue_wide)
+    band_x = lax.all_to_all(conv_out, "cz", 0, 1, tiled=True)
+    band_mask = lax.all_to_all(tissue_wide, "cz", 0, 1, tiled=True)
+    conv_t = jnp.transpose(band_x, (1, 0, 2))
+    tissue_t = jnp.transpose(band_mask)
     common = (proj_weight, dt_weight, dt_bias, a_rate, skip_d)
-    along_rows = direction(conv_t, tissue_t, 0, *common, "col", False)
-    along_rows = along_rows + direction(conv_t, tissue_t, 2, *common, "col", True)
+    along_rows = direction(conv_t, tissue_t, 0, *common, "cx", False)
+    along_rows = along_rows + direction(conv_t, tissue_t, 2, *common, "cx", True)
+    along_rows = lax.all_to_all(along_rows, "cz", 0, 1, tiled=True)
     along_cols = direction(conv_out, tissue_wide, 1, *common, "row", False)
     along_cols = along_cols + direction(conv_out, tissue_wide, 3, *common, "row", True)
     mixed_sum = jnp.transpose(along_rows, (1, 0, 2)) + along_cols
@@ -187,12 +201,17 @@
 
 
 def solution(mesh):
+    cols = mesh.shape["col"]
+    group = 8 if cols % 8 == 0 else cols
+    grid = mesh.devices.reshape(mesh.shape["row"], cols // group, group)
+    mesh = jax.sharding.Mesh(grid, ("row", "cx", "cz"))
+    col = ("cx", "cz")
     return jax.shard_map(
         local,
         mesh=mesh,
         in_specs=(
-            P("row", "col", None),
-            P("row", "col"),
+            P("row", col, None),
+            P("row", col),
             P(),
             P(),
             P(),
@@ -205,6 +224,6 @@
             P(),
             P(),
         ),
-        out_specs=P("row", "col", None),
+        out_specs=P("row", col, None),
         check_vma=False,
     )

time: 292 us -> 229 us (0.78)
  starting transfers between devices: 140 us -> 54.9 us
  Pallas kernels: 52.5 us -> 93.8 us
  waiting for transfers between devices: 40.7 us -> 6.8 us
  blocking collectives: 0 us -> 14.1 us
  other arithmetic: 36.7 us -> 28.6 us
  matrix products: 4.88 us -> 10.3 us
  local copies, waits for them, and re-layouts: 13.1 us -> 18 us
    ppermute x28 -> x10, starting transfers between devices: 124 us -> 30.2 us  [carried_in(): got = lax.ppermute(inclusive, axis, pairs)]
    pallas_call x8, Pallas kernels: 52.5 us -> 93.8 us  [run_scan(): return pl.pallas_call(kernel, out_shape=tuple(out_shape))(*args)]
    ppermute x28 -> x10, waiting for transfers between devices: 39 us -> 4.97 us  [carried_in(): got = lax.ppermute(inclusive, axis, pairs)]
    add x28 -> x15, other arithmetic: 26.4 us -> 11.1 us  [the longest x10 6.64 us: combine(): state = decay * earlier[:nstate] + later[:nstate]]
    all_to_all x0 -> x1, blocking collectives: none -> 14.1 us  [local(): band_mask = lax.all_to_all(tissue_wide, 'cz', 0, 1, tiled=True)]
    all_to_all x0 -> x2, starting transfers between devices: none -> 10.3 us  [the longest x1 6.84 us: local(): along_rows = lax.all_to_all(along_rows, 'cz', 0, 1, tiled=True)]
    mul x0 -> x8, other arithmetic: none -> 5.92 us  [the longest x2 3.71 us: direction_inputs(): delta = delta.reshape(length, seqs, inner) * seq_mask[:, :, None]]
    concatenate x0 -> x10, other arithmetic: none -> 5.24 us  [combine(): jnp.concatenate([state, (earlier[nstate] + later[nstate])[None]], axis=0)]
  transfers between devices with their start and end apart: 32 -> 16, of which waited for: 5 -> 5; matrix products, arithmetic and copies ran while one was open for 14% -> 18% of each run, Pallas kernels for 16% -> 39%
where the time goes in v1:
time: 229 us; the launch traced here: 227 us
  Pallas kernels  93.8 us (41%)
  starting transfers between devices  54.9 us (24%)
  other arithmetic  28.6 us (12%)
  local copies, waits for them, and re-layouts  18 us (8%)
  blocking collectives  14.1 us (6%)
  matrix products  10.3 us (4%)
  waiting for transfers between devices  6.8 us (3%)
    pallas_call x8, Pallas kernels, run_scan(): return pl.pallas_call(kernel, out_shape=tuple(out_shape))(*args)  93.8 us
    ppermute x10, starting transfers between devices, carried_in(): got = lax.ppermute(inclusive, axis, pairs)  30.2 us
    all_to_all x1, blocking collectives, local(): band_mask = lax.all_to_all(tissue_wide, 'cz', 0, 1, tiled=True)  14.1 us
    ppermute x2, starting transfers between devices, padded_2(): lax.ppermute(lax.slice_in_dim(block, 0, width, axis=dim), axis, backward)  8.18 us
    all_to_all x1, starting transfers between devices, local(): along_rows = lax.all_to_all(along_rows, 'cz', 0, 1, tiled=True)  6.84 us
    add x10, other arithmetic, combine(): state = decay * earlier[:nstate] + later[:nstate]  6.64 us
    ppermute x2, starting transfers between devices, padded_2(): lax.ppermute(lax.slice_in_dim(block, block.shape[dim] - width, None, axis...  6.23 us
    concatenate x10, other arithmetic, combine(): jnp.concatenate([state, (earlier[nstate] + later[nstate])[None]], axis=0)  5.24 us
  transfers between devices with their start and end apart: 16, of which 5 were waited for; matrix products, arithmetic and copies ran while one was open for 18% of the time, Pallas kernels for 39%

profile of v1, /device:TPU:14, one launch (start us, length us, event | category | flops | bytes accessed | tf_op | source)
XLA Modules:
  0.0 227.2 jit_solution(10991940138487615780)
XLA Ops:
  0.0 1.2 convert_reduce_fusion
  1.2 1.2 fusion.9
  3.8 2.1 collective-permute-start.1
  5.8 2.4 %collective-permute-start = (bf16[1,16,384]{2,1,0:T(8,128)(2,1)S(1)}, bf16[1,16,384]{2,1,0:T(8,128)(2,1)S(1)}, u32[]{:S(2)}, u32[]{:S(2)}) collective-permute-start(bf16[1,16,384]{2,1,0:T(8,128)(2,1)S(1)} %get-tuple-element.32), channel_id=1, source_target_pairs={{0,32},{32,64},{64,96},{96,128},{128,160},{160,192},{192,224},{1,3... | collective-permute-start | bytes 36872 | tf_op jit(solution)/shard_map/ppermute | solution.py:15
  11.3 3.8 %collective-permute-start.2 = (bf16[34,1,384]{2,1,0:T(2,128)(2,1)S(1)}, bf16[34,1,384]{2,1,0:T(2,128)(2,1)S(1)}, u32[]{:S(2)}, u32[]{:S(2)}) collective-permute-start(bf16[34,1,384]{2,1,0:T(2,128)(2,1)S(1)} %get-tuple-element.42), channel_id=1, source_target_pairs={{0,1},{1,2},{2,3},{3,4},{4,5},{5,6},{6,7},{7,8},{8,9},{9,10},{10,1... | collective-permute-start | bytes 78344 | tf_op jit(solution)/shard_map/ppermute | solution.py:15
  15.1 6.1 %collective-permute-start.3 = (bf16[34,1,384]{2,1,0:T(2,128)(2,1)S(1)}, bf16[34,1,384]{2,1,0:T(2,128)(2,1)S(1)}, u32[]{:S(2)}, u32[]{:S(2)}) collective-permute-start(bf16[34,1,384]{2,1,0:T(2,128)(2,1)S(1)} %get-tuple-element.43), channel_id=1, source_target_pairs={{1,0},{2,1},{3,2},{4,3},{5,4},{6,5},{7,6},{8,7},{9,8},{10,9},{11,1... | collective-permute-start | bytes 78344 | tf_op jit(solution)/shard_map/ppermute | solution.py:18
  21.4 1.7 collective-permute-done.3
  23.5 1.5 multiply_convert_fusion.x_ref
  25.1 1.2 fusion.18
  26.3 1.2 fusion.19
  30.5 1.4 broadcast_multiply_fusion
  31.9 6.1 %shard_map.131 = f32[17,16,384]{2,1,0:T(8,128)} custom-call(f32[16,384]{1,0:T(8,128)} %get-tuple-element.59.neg_rate_ref, f32[1,384]{1,0:T(1,128)} %get-tuple-element.77.skip_ref, bf16[32,16,384]{2,1,0:T(8,128)(2,1)} %multiply_convert_fusion.x_ref, f32[32,16,384]{2,1,0:T(8,128)} %get-tuple-element.73.delta_ref, f32[32,16,16]{2,1,0:T(8,128)} %bitcast.106, ...), custom_call_target="tpu_custom_call" | custom-call | tf_op jit(solution)/shard_map/pallas_call | solution.py:114
  38.0 2.2 collective-permute-start.8
  40.2 14.1 %all_to_all.55 = f32[8,4,16]{2,1,0:T(4,128)S(1)} all-to-all(f32[8,4,16]{2,1,0:T(4,128)S(1)} %bitcast.131), channel_id=1, replica_groups=mesh['row'=8,'cx'=4,'cz'=8] {'cz'}, dimensions={0} | all-to-all | bytes 4096 | tf_op jit(solution)/shard_map/all_to_all | solution.py:183
  55.1 3.5 %all-to-all-start = ((bf16[32,16,384]{2,1,0:T(8,128)(2,1)}), bf16[32,16,384]{2,1,0:T(8,128)(2,1)S(1)}, u32[]{:S(2)}, u32[]{:S(2)}) async-start(bf16[32,16,384]{2,1,0:T(8,128)(2,1)} %multiply_convert_fusion.x_ref), calls=%async_computation | async-start | bytes 786432 | tf_op jit(solution)/shard_map/all_to_all | solution.py:182
  60.3 6.1 %shard_map.133 = f32[17,16,384]{2,1,0:T(8,128)} custom-call(f32[16,384]{1,0:T(8,128)} %get-tuple-element.56.neg_rate_ref, f32[1,384]{1,0:T(1,128)} %get-tuple-element.74.skip_ref, bf16[32,16,384]{2,1,0:T(8,128)(2,1)} %multiply_convert_fusion.x_ref, f32[32,16,384]{2,1,0:T(8,128)} %get-tuple-element.72.delta_ref, f32[32,16,16]{2,1,0:T(8,128)} %bitcast.110, ...), custom_call_target="tpu_custom_call" | custom-call | tf_op jit(solution)/shard_map/pallas_call | solution.py:114
  66.4 2.2 collective-permute-start.11
  69.5 3.4 %collective-permute-start.9 = (f32[17,16,384]{2,1,0:T(8,128)}, f32[17,16,384]{2,1,0:T(8,128)}, u32[]{:S(2)}, u32[]{:S(2)}) collective-permute-start(f32[17,16,384]{2,1,0:T(8,128)} %pad_maximum_fusion.1), channel_id=1, source_target_pairs={{0,64},{32,96},{64,128},{96,160},{128,192},{160,224},{1,65},{33,97... | collective-permute-start | bytes 1253384 | tf_op jit(solution)/shard_map/ppermute | solution.py:134
  72.9 1.5 collective-permute-done.11
  75.3 1.9 collective-permute-start.12
  78.4 1.5 compare_select_fusion.2
  79.9 1.4 reshape.99
  81.2 1.1 fusion.21
  83.0 2.2 compare_select_fusion.3
  85.2 1.4 reshape.96
  86.6 1.6 copy.52
  88.2 1.6 copy.53
  89.8 2.3 %broadcast_multiply_fusion.2 = (f32[128,4,384]{2,1,0:T(4,128)}, f32[128,4,384]{2,1,0:T(4,128)}) fusion(f32[128,4,384]{2,1,0:T(4,128)S(1)} %reshape.99, f32[128,4]{1,0:T(8,128)} %copy.51, f32[128,4,384]{2,1,0:T(4,128)S(1)} %reshape.96), kind=kLoop, calls=%fused_computation.49 | loop fusion | flops 393216 | bytes 3147776 | tf_op jit(solution)/shard_map/mul | solution.py:59
  92.2 14.4 %shard_map.127 = f32[17,4,384]{2,1,0:T(4,128)} custom-call(f32[16,384]{1,0:T(8,128)} %get-tuple-element.58.neg_rate_ref, f32[1,384]{1,0:T(1,128)} %get-tuple-element.76.skip_ref, bf16[128,4,384]{2,1,0:T(4,128)(2,1)} %bitcast.100, f32[128,4,384]{2,1,0:T(4,128)} %get-tuple-element.67.delta_ref, f32[128,4,16]{2,1,0:T(4,128)} %bitcast.118, f32[128,4,16]{2,1,0:T(4,128)} %bitcast.120), custom_call_target="tpu_custom_call" | custom-call | tf_op jit(solution)/shard_map/pallas_call | solution.py:114
  106.6 1.3 collective-permute-start.4
  109.6 14.5 %shard_map.129 = f32[17,4,384]{2,1,0:T(4,128)} custom-call(f32[16,384]{1,0:T(8,128)} %get-tuple-element.57.neg_rate_ref, f32[1,384]{1,0:T(1,128)} %get-tuple-element.75.skip_ref, bf16[128,4,384]{2,1,0:T(4,128)(2,1)} %bitcast.101, f32[128,4,384]{2,1,0:T(4,128)} %get-tuple-element.66.delta_ref, f32[128,4,16]{2,1,0:T(4,128)} %bitcast.114, f32[128,4,16]{2,1,0:T(4,128)} %bitcast.116), custom_call_target="tpu_custom_call" | custom-call | tf_op jit(solution)/shard_map/pallas_call | solution.py:114
  124.1 4.5 %collective-permute-start.6 = (f32[17,4,384]{2,1,0:T(4,128)}, f32[17,4,384]{2,1,0:T(4,128)S(1)}, u32[]{:S(2)}, u32[]{:S(2)}) collective-permute-start(f32[17,4,384]{2,1,0:T(4,128)} %shard_map.129), channel_id=1, source_target_pairs={{8,0},{16,8},{24,16},{9,1},{17,9},{25,17},{10,2},{18,10},{26,18},{... | collective-permute-start | bytes 313352 | tf_op jit(solution)/shard_map/ppermute | solution.py:134
  128.8 1.3 collective-permute-start.5
  130.1 1.4 collective-permute-done.6
  133.8 5.8 %collective-permute-start.7 = (f32[17,4,384]{2,1,0:T(4,128)}, f32[17,4,384]{2,1,0:T(4,128)}, u32[]{:S(2)}, u32[]{:S(2)}) collective-permute-start(f32[17,4,384]{2,1,0:T(4,128)} %pad_maximum_fusion.11), channel_id=1, source_target_pairs={{16,0},{24,8},{17,1},{25,9},{18,2},{26,10},{19,3},{27,11},{20,4},{... | collective-permute-start | bytes 313352 | tf_op jit(solution)/shard_map/ppermute | solution.py:134
  141.4 6.3 %collective-permute-start.10 = (f32[17,16,384]{2,1,0:T(8,128)S(1)}, f32[17,16,384]{2,1,0:T(8,128)S(1)}, u32[]{:S(2)}, u32[]{:S(2)}) collective-permute-start(f32[17,16,384]{2,1,0:T(8,128)S(1)} %pad_maximum_fusion.2), channel_id=1, source_target_pairs={{0,128},{32,160},{64,192},{96,224},{1,129},{33,161},{65,193},{97,2... | collective-permute-start | bytes 1253384 | tf_op jit(solution)/shard_map/ppermute | solution.py:134
  147.7 1.1 multiply_add_fusion
  149.6 18.3 %shard_map.128 = (f32[128,4,384]{2,1,0:T(4,128)}, f32[17,4,384]{2,1,0:T(4,128)}) custom-call(f32[16,384]{1,0:T(8,128)} %get-tuple-element.58.neg_rate_ref, f32[1,384]{1,0:T(1,128)} %get-tuple-element.76.skip_ref, bf16[128,4,384]{2,1,0:T(4,128)(2,1)} %bitcast.102, f32[128,4,384]{2,1,0:T(4,128)} %get-tuple-element.67.delta_ref, f32[128,4,16]{2,1,0:T(4,128)} %bitcast.119, ...), custom_call_target="tpu_custom_call" | custom-call | tf_op jit(solution)/shard_map/pallas_call | solution.py:114
  170.2 18.5 %shard_map.130 = (f32[128,4,384]{2,1,0:T(4,128)}, f32[17,4,384]{2,1,0:T(4,128)}) custom-call(f32[16,384]{1,0:T(8,128)} %get-tuple-element.57.neg_rate_ref, f32[1,384]{1,0:T(1,128)} %get-tuple-element.75.skip_ref, bf16[128,4,384]{2,1,0:T(4,128)(2,1)} %bitcast.103, f32[128,4,384]{2,1,0:T(4,128)} %get-tuple-element.66.delta_ref, f32[128,4,16]{2,1,0:T(4,128)} %bitcast.115, ...), custom_call_target="tpu_custom_call" | custom-call | tf_op jit(solution)/shard_map/pallas_call | solution.py:114
  188.6 2.2 add.230
  190.9 6.8 %all-to-all-start.2 = ((f32[128,4,384]{2,1,0:T(4,128)}), f32[128,4,384]{2,1,0:T(4,128)S(1)}, u32[]{:S(2)}, u32[]{:S(2)}) async-start(f32[128,4,384]{2,1,0:T(4,128)} %add.230), calls=%async_computation.2 | async-start | bytes 1572864 | tf_op jit(solution)/shard_map/all_to_all | solution.py:189
  198.6 1.3 collective-permute-start.13
  200.6 1.2 fusion.13
  202.6 8.0 %shard_map.132 = (f32[32,16,384]{2,1,0:T(8,128)}, f32[17,16,384]{2,1,0:T(8,128)}) custom-call(f32[16,384]{1,0:T(8,128)} %get-tuple-element.59.neg_rate_ref, f32[1,384]{1,0:T(1,128)} %get-tuple-element.77.skip_ref, bf16[32,16,384]{2,1,0:T(8,128)(2,1)} %multiply_convert_fusion.x_ref, f32[32,16,384]{2,1,0:T(8,128)} %get-tuple-element.73.delta_ref, ...), custom_call_target="tpu_custom_call" | custom-call | tf_op jit(solution)/shard_map/pallas_call | solution.py:114
  210.5 2.1 collective-permute-done.13
  213.4 1.2 fusion.12
  215.3 8.0 %shard_map.134 = (f32[32,16,384]{2,1,0:T(8,128)}, f32[17,16,384]{2,1,0:T(8,128)}) custom-call(f32[16,384]{1,0:T(8,128)} %get-tuple-element.56.neg_rate_ref, f32[1,384]{1,0:T(1,128)} %get-tuple-element.74.skip_ref, bf16[32,16,384]{2,1,0:T(8,128)(2,1)} %multiply_convert_fusion.x_ref, f32[32,16,384]{2,1,0:T(8,128)} %get-tuple-element.72.delta_ref, ...), custom_call_target="tpu_custom_call" | custom-call | tf_op jit(solution)/shard_map/pallas_call | solution.py:114
  226.0 1.2 fusion.1
  (136 shorter events, 29.3 us)
Async XLA Ops:
  0.0 3.3 %copy-start = (bf16[192,768]{1,0:T(8,128)(2,1)S(1)}, bf16[192,768]{1,0:T(8,128)(2,1)}, u32[]{:S(2)}) copy-start(bf16[192,768]{1,0:T(8,128)(2,1)} %param.16) | copy-start | bytes 884740
  0.0 2.4 %copy-start.2 = (bf16[32,16,192]{2,1,0:T(8,128)(2,1)S(1)}, bf16[32,16,192]{2,1,0:T(8,128)(2,1)}, u32[]{:S(2)}) copy-start(bf16[32,16,192]{2,1,0:T(8,128)(2,1)} %param.13) | copy-start | bytes 589828
  3.3 4.9 %copy-start.20 = (f32[4,384,16]{1,2,0:T(8,128)S(1)}, f32[4,384,16]{1,2,0:T(8,128)}, u32[]{:S(2)}) copy-start(f32[4,384,16]{1,2,0:T(8,128)} %param.22) | copy-start | bytes 294916
  3.3 5.6 %copy-start.25 = (f32[4,384]{1,0:T(4,128)S(1)}, f32[4,384]{1,0:T(4,128)}, u32[]{:S(2)}) copy-start(f32[4,384]{1,0:T(4,128)} %param.23) | copy-start | bytes 18436
  3.3 6.2 %copy-start.16 = (bf16[4,384,44]{1,0,2:T(4,128)(2,1)S(1)}, bf16[4,384,44]{1,0,2:T(4,128)(2,1)}, u32[]{:S(2)}) copy-start(bf16[4,384,44]{1,0,2:T(4,128)(2,1)} %param.19) | copy-start | bytes 405508
  3.4 7.0 %copy-start.19 = (bf16[4,12,384]{2,0,1:T(4,128)(2,1)S(1)}, bf16[4,12,384]{2,0,1:T(4,128)(2,1)}, u32[]{:S(2)}) copy-start(bf16[4,12,384]{2,0,1:T(4,128)(2,1)} %param.20) | copy-start | bytes 110596
  3.7 7.4 %copy-start.3 = (bf16[512,768]{1,0:T(8,128)(2,1)}, bf16[512,768]{1,0:T(8,128)(2,1)S(1)}, u32[]{:S(2)}) copy-start(bf16[512,768]{1,0:T(8,128)(2,1)S(1)} %convolution_convert_fusion) | copy-start | bytes 2359300
  3.7 7.3 %copy-start.21 = (bf16[3,3,384]{2,1,0:T(4,128)(2,1)S(1)}, bf16[3,3,384]{2,1,0:T(4,128)(2,1)}, u32[]{:S(2)}) copy-start(bf16[3,3,384]{2,1,0:T(4,128)(2,1)} %param.17) | copy-start | bytes 20740
  3.8 7.4 %collective-permute-start.1 = (bf16[1,16,384]{2,1,0:T(8,128)(2,1)S(1)}, bf16[1,16,384]{2,1,0:T(8,128)(2,1)S(1)}, u32[]{:S(2)}, u32[]{:S(2)}) collective-permute-start(bf16[1,16,384]{2,1,0:T(8,128)(2,1)S(1)} %get-tuple-element.33), channel_id=1, source_target_pairs={{32,0},{64,32},{96,64},{128,96},{160,128},{192,160},{224,192},{33,... | collective-permute-start | bytes 36872 | tf_op jit(solution)/shard_map/ppermute | solution.py:18
  5.8 5.3 %collective-permute-start = (bf16[1,16,384]{2,1,0:T(8,128)(2,1)S(1)}, bf16[1,16,384]{2,1,0:T(8,128)(2,1)S(1)}, u32[]{:S(2)}, u32[]{:S(2)}) collective-permute-start(bf16[1,16,384]{2,1,0:T(8,128)(2,1)S(1)} %get-tuple-element.32), channel_id=1, source_target_pairs={{0,32},{32,64},{64,96},{96,128},{128,160},{160,192},{192,224},{1,3... | collective-permute-start | bytes 36872 | tf_op jit(solution)/shard_map/ppermute | solution.py:15
  10.4 10.9 %copy-start.24 = (f32[4,384]{1,0:T(4,128)S(1)}, f32[4,384]{1,0:T(4,128)}, u32[]{:S(2)}) copy-start(f32[4,384]{1,0:T(4,128)} %param.21) | copy-start | bytes 18436
  10.4 10.9 %copy-start.23 = (s32[32,16]{0,1:T(8,128)S(1)}, s32[32,16]{0,1:T(8,128)}, u32[]{:S(2)}) copy-start(s32[32,16]{0,1:T(8,128)} %param.14) | copy-start | bytes 6148
  11.3 10.2 %collective-permute-start.2 = (bf16[34,1,384]{2,1,0:T(2,128)(2,1)S(1)}, bf16[34,1,384]{2,1,0:T(2,128)(2,1)S(1)}, u32[]{:S(2)}, u32[]{:S(2)}) collective-permute-start(bf16[34,1,384]{2,1,0:T(2,128)(2,1)S(1)} %get-tuple-element.42), channel_id=1, source_target_pairs={{0,1},{1,2},{2,3},{3,4},{4,5},{5,6},{6,7},{7,8},{8,9},{9,10},{10,1... | collective-permute-start | bytes 78344 | tf_op jit(solution)/shard_map/ppermute | solution.py:15
  15.1 8.1 %collective-permute-start.3 = (bf16[34,1,384]{2,1,0:T(2,128)(2,1)S(1)}, bf16[34,1,384]{2,1,0:T(2,128)(2,1)S(1)}, u32[]{:S(2)}, u32[]{:S(2)}) collective-permute-start(bf16[34,1,384]{2,1,0:T(2,128)(2,1)S(1)} %get-tuple-element.43), channel_id=1, source_target_pairs={{1,0},{2,1},{3,2},{4,3},{5,4},{6,5},{7,6},{8,7},{9,8},{10,9},{11,1... | collective-permute-start | bytes 78344 | tf_op jit(solution)/shard_map/ppermute | solution.py:18
  21.4 2.2 copy-start.26
  38.0 30.6 %collective-permute-start.8 = (f32[17,16,384]{2,1,0:T(8,128)}, f32[17,16,384]{2,1,0:T(8,128)S(1)}, u32[]{:S(2)}, u32[]{:S(2)}) collective-permute-start(f32[17,16,384]{2,1,0:T(8,128)} %shard_map.131), channel_id=1, source_target_pairs={{0,32},{32,64},{64,96},{96,128},{128,160},{160,192},{192,224},{1,3... | collective-permute-start | bytes 1253384 | tf_op jit(solution)/shard_map/ppermute | solution.py:134
  55.1 22.1 %all-to-all-start = ((bf16[32,16,384]{2,1,0:T(8,128)(2,1)}), bf16[32,16,384]{2,1,0:T(8,128)(2,1)S(1)}, u32[]{:S(2)}, u32[]{:S(2)}) async-start(bf16[32,16,384]{2,1,0:T(8,128)(2,1)} %multiply_convert_fusion.x_ref), calls=%async_computation | async-start | bytes 786432 | tf_op jit(solution)/shard_map/all_to_all | solution.py:182
  60.3 8.3 %copy-start.7 = (f32[17,16,384]{2,1,0:T(8,128)S(1)}, f32[17,16,384]{2,1,0:T(8,128)}, u32[]{:S(2)}) copy-start(f32[17,16,384]{2,1,0:T(8,128)} %shard_map.131) | copy-start | bytes 1253380
  60.3 8.3 %copy-start.10 = (f32[16,384]{1,0:T(8,128)S(1)}, f32[16,384]{1,0:T(8,128)}, u32[]{:S(2)}) copy-start(f32[16,384]{1,0:T(8,128)} %get-tuple-element.59.neg_rate_ref) | copy-start | bytes 73732
  66.4 8.0 %collective-permute-start.11 = (f32[17,16,384]{2,1,0:T(8,128)}, f32[17,16,384]{2,1,0:T(8,128)S(1)}, u32[]{:S(2)}, u32[]{:S(2)}) collective-permute-start(f32[17,16,384]{2,1,0:T(8,128)} %shard_map.133), channel_id=1, source_target_pairs={{32,0},{64,32},{96,64},{128,96},{160,128},{192,160},{224,192},{33,... | collective-permute-start | bytes 1253384 | tf_op jit(solution)/shard_map/ppermute | solution.py:134
  68.6 0.9 copy-start.5
  68.6 5.8 %copy-start.8 = (f32[17,16,384]{2,1,0:T(8,128)S(1)}, f32[17,16,384]{2,1,0:T(8,128)}, u32[]{:S(2)}) copy-start(f32[17,16,384]{2,1,0:T(8,128)} %shard_map.133) | copy-start | bytes 1253380
  68.6 5.8 %copy-start.9 = (f32[16,384]{1,0:T(8,128)S(1)}, f32[16,384]{1,0:T(8,128)}, u32[]{:S(2)}) copy-start(f32[16,384]{1,0:T(8,128)} %get-tuple-element.56.neg_rate_ref) | copy-start | bytes 73732
  69.5 70.0 %collective-permute-start.9 = (f32[17,16,384]{2,1,0:T(8,128)}, f32[17,16,384]{2,1,0:T(8,128)}, u32[]{:S(2)}, u32[]{:S(2)}) collective-permute-start(f32[17,16,384]{2,1,0:T(8,128)} %pad_maximum_fusion.1), channel_id=1, source_target_pairs={{0,64},{32,96},{64,128},{96,160},{128,192},{160,224},{1,65},{33,97... | collective-permute-start | bytes 1253384 | tf_op jit(solution)/shard_map/ppermute | solution.py:134
  75.3 72.4 %collective-permute-start.12 = (f32[17,16,384]{2,1,0:T(8,128)}, f32[17,16,384]{2,1,0:T(8,128)}, u32[]{:S(2)}, u32[]{:S(2)}) collective-permute-start(f32[17,16,384]{2,1,0:T(8,128)} %pad_maximum_fusion.4), channel_id=1, source_target_pairs={{64,0},{96,32},{128,64},{160,96},{192,128},{224,160},{65,1},{97,33... | collective-permute-start | bytes 1253384 | tf_op jit(solution)/shard_map/ppermute | solution.py:134
  77.2 0.9 copy-start.18
  77.4 2.5 %copy-start.1 = (bf16[4,8,16,384]{3,0,2,1:T(4,128)(2,1)}, bf16[4,8,16,384]{3,0,2,1:T(4,128)(2,1)S(1)}, u32[]{:S(2)}) copy-start(bf16[4,8,16,384]{3,0,2,1:T(4,128)(2,1)S(1)} %copy.47) | copy-start | bytes 1179652
  77.4 0.9 copy-start.22
  106.6 22.1 %collective-permute-start.4 = (f32[17,4,384]{2,1,0:T(4,128)}, f32[17,4,384]{2,1,0:T(4,128)S(1)}, u32[]{:S(2)}, u32[]{:S(2)}) collective-permute-start(f32[17,4,384]{2,1,0:T(4,128)} %shard_map.127), channel_id=1, source_target_pairs={{0,8},{8,16},{16,24},{1,9},{9,17},{17,25},{2,10},{10,18},{18,26},{... | collective-permute-start | bytes 313352 | tf_op jit(solution)/shard_map/ppermute | solution.py:134
  109.6 19.1 %copy-start.17 = (f32[17,4,384]{2,1,0:T(4,128)S(1)}, f32[17,4,384]{2,1,0:T(4,128)}, u32[]{:S(2)}) copy-start(f32[17,4,384]{2,1,0:T(4,128)} %shard_map.127) | copy-start | bytes 313348
  109.6 19.1 %copy-start.15 = (f32[16,384]{1,0:T(8,128)S(1)}, f32[16,384]{1,0:T(8,128)}, u32[]{:S(2)}) copy-start(f32[16,384]{1,0:T(8,128)} %get-tuple-element.58.neg_rate_ref) | copy-start | bytes 73732
  109.6 22.6 %copy-start.14 = (f32[16,384]{1,0:T(8,128)S(1)}, f32[16,384]{1,0:T(8,128)}, u32[]{:S(2)}) copy-start(f32[16,384]{1,0:T(8,128)} %get-tuple-element.57.neg_rate_ref) | copy-start | bytes 73732
  124.1 7.3 %collective-permute-start.6 = (f32[17,4,384]{2,1,0:T(4,128)}, f32[17,4,384]{2,1,0:T(4,128)S(1)}, u32[]{:S(2)}, u32[]{:S(2)}) collective-permute-start(f32[17,4,384]{2,1,0:T(4,128)} %shard_map.129), channel_id=1, source_target_pairs={{8,0},{16,8},{24,16},{9,1},{17,9},{25,17},{10,2},{18,10},{26,18},{... | collective-permute-start | bytes 313352 | tf_op jit(solution)/shard_map/ppermute | solution.py:134
  128.8 20.0 %collective-permute-start.5 = (f32[17,4,384]{2,1,0:T(4,128)S(1)}, f32[17,4,384]{2,1,0:T(4,128)S(1)}, u32[]{:S(2)}, u32[]{:S(2)}) collective-permute-start(f32[17,4,384]{2,1,0:T(4,128)S(1)} %pad_maximum_fusion.9), channel_id=1, source_target_pairs={{0,16},{8,24},{1,17},{9,25},{2,18},{10,26},{3,19},{11,27},{4,20},{... | collective-permute-start | bytes 313352 | tf_op jit(solution)/shard_map/ppermute | solution.py:134
  133.8 34.1 %collective-permute-start.7 = (f32[17,4,384]{2,1,0:T(4,128)}, f32[17,4,384]{2,1,0:T(4,128)}, u32[]{:S(2)}, u32[]{:S(2)}) collective-permute-start(f32[17,4,384]{2,1,0:T(4,128)} %pad_maximum_fusion.11), channel_id=1, source_target_pairs={{16,0},{24,8},{17,1},{25,9},{18,2},{26,10},{19,3},{27,11},{20,4},{... | collective-permute-start | bytes 313352 | tf_op jit(solution)/shard_map/ppermute | solution.py:134
  141.4 58.4 %collective-permute-start.10 = (f32[17,16,384]{2,1,0:T(8,128)S(1)}, f32[17,16,384]{2,1,0:T(8,128)S(1)}, u32[]{:S(2)}, u32[]{:S(2)}) collective-permute-start(f32[17,16,384]{2,1,0:T(8,128)S(1)} %pad_maximum_fusion.2), channel_id=1, source_target_pairs={{0,128},{32,160},{64,192},{96,224},{1,129},{33,161},{65,193},{97,2... | collective-permute-start | bytes 1253384 | tf_op jit(solution)/shard_map/ppermute | solution.py:134
  170.2 18.5 %copy-start.12 = (f32[128,4,384]{2,1,0:T(4,128)S(1)}, f32[128,4,384]{2,1,0:T(4,128)}, u32[]{:S(2)}) copy-start(f32[128,4,384]{2,1,0:T(4,128)} %get-tuple-element.9) | copy-start | bytes 2359300
  190.9 32.4 %all-to-all-start.2 = ((f32[128,4,384]{2,1,0:T(4,128)}), f32[128,4,384]{2,1,0:T(4,128)S(1)}, u32[]{:S(2)}, u32[]{:S(2)}) async-start(f32[128,4,384]{2,1,0:T(4,128)} %add.230), calls=%async_computation.2 | async-start | bytes 1572864 | tf_op jit(solution)/shard_map/all_to_all | solution.py:189
  197.7 2.1 copy-start.6
  198.6 14.1 %collective-permute-start.13 = (f32[17,16,384]{2,1,0:T(8,128)S(1)}, f32[17,16,384]{2,1,0:T(8,128)S(1)}, u32[]{:S(2)}, u32[]{:S(2)}) collective-permute-start(f32[17,16,384]{2,1,0:T(8,128)S(1)} %pad_maximum_fusion.5), channel_id=1, source_target_pairs={{128,0},{160,32},{192,64},{224,96},{129,1},{161,33},{193,65},{225,... | collective-permute-start | bytes 1253384 | tf_op jit(solution)/shard_map/ppermute | solution.py:134
  223.3 1.1 copy-start.11
  223.3 1.4 copy-start.13
  224.7 0.9 copy-start.27
  224.9 1.2 copy-start.4
  224.9 1.1 copy-start.28

commit v2 on v1

--- a/solution.py
+++ b/solution.py
@@ -84,7 +84,7 @@
         total = jnp.zeros_like(delta)
         for n in range(nstate):
             state = (
-                jnp.exp(delta * neg_rate_ref[pl.ds(n, 1), :]) * state_ref[n]
+                jnp.exp(delta * neg_rate_ref[n]) * state_ref[n]
                 + drive * entry[:, n : n + 1]
             )
             state_ref[n] = state
@@ -105,7 +105,7 @@
     out_shape = [state_shape]
     if with_y:
         out_shape = [jax.ShapeDtypeStruct((length, seqs, inner), jnp.float32), state_shape]
-    args = [neg_rate, skip.reshape(1, inner), seq_x, delta, entry, readout]
+    args = [neg_rate, skip, seq_x, delta, entry, readout]
     if init is not None:
         args.append(init)
     kernel = functools.partial(
@@ -141,15 +141,33 @@
     return exclusive
 
 
-def direction(seq_x, seq_mask, k, proj_weight, dt_weight, dt_bias, a_rate, skip_d, axis, reverse):
-    delta, entry, readout = direction_inputs(
-        seq_x, seq_mask, proj_weight[k], dt_weight[k], dt_bias[k]
-    )
-    neg_rate = -jnp.transpose(a_rate[k])
-    (packed,) = run_scan(seq_x, delta, entry, readout, neg_rate, skip_d[k], None, reverse, False)
-    init = carried_in(packed, neg_rate, axis, reverse)
-    y, _ = run_scan(seq_x, delta, entry, readout, neg_rate, skip_d[k], init, reverse, True)
-    return y
+def flipped(array):
+    return array[::-1]
+
+
+def rows_of(value, seqs):
+    return jnp.broadcast_to(value[..., None, :], value.shape[:-1] + (seqs, value.shape[-1]))
+
+
+def direction_pair(seq_x, seq_mask, ahead, back, proj_weight, dt_weight, dt_bias, a_rate, skip_d,
+                   axis):
+    length, seqs, inner = seq_x.shape
+    nstate = a_rate.shape[2]
+    fwd = direction_inputs(seq_x, seq_mask, proj_weight[ahead], dt_weight[ahead], dt_bias[ahead])
+    bwd = direction_inputs(seq_x, seq_mask, proj_weight[back], dt_weight[back], dt_bias[back])
+    both = [jnp.concatenate([f, flipped(b)], axis=1) for f, b in zip(fwd, bwd)]
+    delta, entry, readout = both
+    stacked_x = jnp.concatenate([seq_x, flipped(seq_x)], axis=1)
+    neg_fwd = -jnp.transpose(a_rate[ahead])
+    neg_bwd = -jnp.transpose(a_rate[back])
+    neg_rate = jnp.concatenate([rows_of(neg_fwd, seqs), rows_of(neg_bwd, seqs)], axis=1)
+    skip = jnp.concatenate([rows_of(skip_d[ahead], seqs), rows_of(skip_d[back], seqs)], axis=0)
+    (packed,) = run_scan(stacked_x, delta, entry, readout, neg_rate, skip, None, False, False)
+    init_fwd = carried_in(packed[:, :seqs], neg_fwd, axis, False)
+    init_bwd = carried_in(packed[:, seqs:], neg_bwd, axis, True)
+    init = jnp.concatenate([init_fwd, init_bwd], axis=1)
+    y, _ = run_scan(stacked_x, delta, entry, readout, neg_rate, skip, init, False, True)
+    return y[:, :seqs] + flipped(y[:, seqs:])
 
 
 def local(
@@ -179,16 +197,19 @@
     padded = padded_2(inner_part, (("row", 0), (("cx", "cz"), 1)), 1)
     conv_out = conv_silu(padded, conv_weight, conv_bias, rows_here, cols_here)
     tissue_wide = tissue.astype(jnp.float32)
-    band_x = lax.all_to_all(conv_out, "cz", 0, 1, tiled=True)
-    band_mask = lax.all_to_all(tissue_wide, "cz", 0, 1, tiled=True)
+    group = lax.axis_size("cz")
+    mask_lane = jnp.pad(tissue.astype(jnp.bfloat16), ((0, 0), (0, inner - cols_here)))
+    sent = jnp.concatenate([conv_out, mask_lane[:, None, :]], axis=1)
+    band = lax.all_to_all(sent, "cz", 0, 1, tiled=True)
+    band = band.reshape(rows_here // group, group, cols_here + 1, inner)
+    band_x = band[:, :, :cols_here, :].reshape(rows_here // group, group * cols_here, inner)
+    band_mask = band[:, :, cols_here, :cols_here].reshape(rows_here // group, group * cols_here)
     conv_t = jnp.transpose(band_x, (1, 0, 2))
-    tissue_t = jnp.transpose(band_mask)
+    tissue_t = jnp.transpose(band_mask).astype(jnp.float32)
     common = (proj_weight, dt_weight, dt_bias, a_rate, skip_d)
-    along_rows = direction(conv_t, tissue_t, 0, *common, "cx", False)
-    along_rows = along_rows + direction(conv_t, tissue_t, 2, *common, "cx", True)
+    along_rows = direction_pair(conv_t, tissue_t, 0, 2, *common, "cx")
     along_rows = lax.all_to_all(along_rows, "cz", 0, 1, tiled=True)
-    along_cols = direction(conv_out, tissue_wide, 1, *common, "row", False)
-    along_cols = along_cols + direction(conv_out, tissue_wide, 3, *common, "row", True)
+    along_cols = direction_pair(conv_out, tissue_wide, 1, 3, *common, "row")
     mixed_sum = jnp.transpose(along_rows, (1, 0, 2)) + along_cols
     mixed = (layer_norm(mixed_sum, out_gain) * jax.nn.silu(gate_part.astype(jnp.float32))).astype(
         jnp.bfloat16

time: 229 us -> 205 us (0.90)
  Pallas kernels: 93.8 us -> 54.5 us
  waiting for transfers between devices: 6.8 us -> 24.1 us
  blocking collectives: 14.1 us -> 0 us
  local copies, waits for them, and re-layouts: 18 us -> 27.4 us
  other arithmetic: 28.6 us -> 34.9 us
  matrix products: 10.3 us -> 6.64 us
    pallas_call x8 -> x4, Pallas kernels: 93.8 us -> 54.5 us  [run_scan(): return pl.pallas_call(kernel, out_shape=tuple(out_shape))(*args)]
    concatenate x0 -> x13, other arithmetic: none -> 14.3 us  [the longest x4 6.45 us: direction_pair(): both = [jnp.concatenate([f, flipped(b)], axis=1) for f, b in zip(fwd, bwd)]]
    all_to_all x1 -> x0, blocking collectives: 14.1 us -> none  [local(): band_mask = lax.all_to_all(tissue_wide, 'cz', 0, 1, tiled=True)]
    all_to_all x1, waiting for transfers between devices: 0.01 us -> 12 us  [local(): band = lax.all_to_all(sent, 'cz', 0, 1, tiled=True)]
    slice x4 -> x10, local copies, waits for them, and re-layouts: 2.15 us -> 9.14 us  [the longest x2 3.22 us: direction_pair(): init_fwd = carried_in(packed[:, :seqs], neg_fwd, axis, False)]
    ppermute x10, waiting for transfers between devices: 4.97 us -> 10.8 us  [carried_in(): got = lax.ppermute(inclusive, axis, pairs)]
    rev x0 -> x8, local copies, waits for them, and re-layouts: none -> 4.52 us  [flipped(): return array[::-1]]
    concatenate x10 -> x6, other arithmetic: 5.24 us -> 1.69 us  [combine(): jnp.concatenate([state, (earlier[nstate] + later[nstate])[None]], axis=0)]
  transfers between devices with their start and end apart: 16 -> 16, of which waited for: 5 -> 4; matrix products, arithmetic and copies ran while one was open for 18% -> 26% of each run, Pallas kernels for 39% -> 23%
where the time goes in v2:
time: 205 us; the launch traced here: 202 us
  Pallas kernels  54.5 us (27%)
  starting transfers between devices  53.6 us (26%)
  other arithmetic  34.9 us (17%)
  local copies, waits for them, and re-layouts  27.4 us (13%)
  waiting for transfers between devices  24.1 us (12%)
  matrix products  6.64 us (3%)
    pallas_call x4, Pallas kernels, run_scan(): return pl.pallas_call(kernel, out_shape=tuple(out_shape))(*args)  54.5 us
    ppermute x10, starting transfers between devices, carried_in(): got = lax.ppermute(inclusive, axis, pairs)  28.9 us
    all_to_all x1, waiting for transfers between devices, local(): band = lax.all_to_all(sent, 'cz', 0, 1, tiled=True)  12 us
    ppermute x10, waiting for transfers between devices, carried_in(): got = lax.ppermute(inclusive, axis, pairs)  10.8 us
    ppermute x2, starting transfers between devices, padded_2(): lax.ppermute(lax.slice_in_dim(block, 0, width, axis=dim), axis, backward)  8.04 us
    all_to_all x1, starting transfers between devices, local(): band = lax.all_to_all(sent, 'cz', 0, 1, tiled=True)  6.76 us
    concatenate x4, other arithmetic, direction_pair(): both = [jnp.concatenate([f, flipped(b)], axis=1) for f, b in zip(fwd, bwd)]  6.45 us
    ppermute x2, starting transfers between devices, padded_2(): lax.ppermute(lax.slice_in_dim(block, block.shape[dim] - width, None, axis...  6.24 us
  transfers between devices with their start and end apart: 16, of which 4 were waited for; matrix products, arithmetic and copies ran while one was open for 26% of the time, Pallas kernels for 23%

profile of v2, /device:TPU:14, one launch (start us, length us, event | category | flops | bytes accessed | tf_op | source)
XLA Modules:
  0.0 202.1 jit_solution(1357009614099452522)
XLA Ops:
  0.0 1.1 convert_reduce_fusion
  1.2 1.2 fusion.9
  2.4 1.2 fusion.11
  4.0 1.9 collective-permute-start.1
  5.9 2.4 %collective-permute-start = (bf16[1,16,384]{2,1,0:T(8,128)(2,1)S(1)}, bf16[1,16,384]{2,1,0:T(8,128)(2,1)S(1)}, u32[]{:S(2)}, u32[]{:S(2)}) collective-permute-start(bf16[1,16,384]{2,1,0:T(8,128)(2,1)S(1)} %get-tuple-element.38), channel_id=1, source_target_pairs={{0,32},{32,64},{64,96},{96,128},{128,160},{160,192},{192,224},{1,3... | collective-permute-start | bytes 36872 | tf_op jit(solution)/shard_map/ppermute | solution.py:15
  13.6 3.8 %collective-permute-start.2 = (bf16[34,1,384]{2,1,0:T(2,128)(2,1)S(1)}, bf16[34,1,384]{2,1,0:T(2,128)(2,1)S(1)}, u32[]{:S(2)}, u32[]{:S(2)}) collective-permute-start(bf16[34,1,384]{2,1,0:T(2,128)(2,1)S(1)} %get-tuple-element.44), channel_id=1, source_target_pairs={{0,1},{1,2},{2,3},{3,4},{4,5},{5,6},{6,7},{7,8},{8,9},{9,10},{10,1... | collective-permute-start | bytes 78344 | tf_op jit(solution)/shard_map/ppermute | solution.py:15
  17.4 6.1 %collective-permute-start.3 = (bf16[34,1,384]{2,1,0:T(2,128)(2,1)S(1)}, bf16[34,1,384]{2,1,0:T(2,128)(2,1)S(1)}, u32[]{:S(2)}, u32[]{:S(2)}) collective-permute-start(bf16[34,1,384]{2,1,0:T(2,128)(2,1)S(1)} %get-tuple-element.45), channel_id=1, source_target_pairs={{1,0},{2,1},{3,2},{4,3},{5,4},{6,5},{7,6},{8,7},{9,8},{10,9},{11,1... | collective-permute-start | bytes 78344 | tf_op jit(solution)/shard_map/ppermute | solution.py:18
  24.3 1.3 collective-permute-done.3
  30.3 1.4 pad_maximum_fusion.1.delta_ref
  31.7 1.2 pad_maximum_fusion.9
  32.9 8.6 %shard_map.129 = f32[17,32,384]{2,1,0:T(8,128)} custom-call(f32[16,32,384]{2,1,0:T(8,128)} %pad_maximum_fusion.3.neg_rate_ref, f32[32,384]{1,0:T(8,128)} %pad_maximum_fusion.23.skip_ref, bf16[32,32,384]{2,1,0:T(8,128)(2,1)} %pad_maximum_fusion.4.x_ref, f32[32,32,384]{2,1,0:T(8,128)} %pad_maximum_fusion.1.delta_ref, ...), custom_call_target="tpu_custom_call" | custom-call | tf_op jit(solution)/shard_map/pallas_call | solution.py:114
  41.5 2.1 %fusion.25 = (f32[17,16,384]{2,1,0:T(8,128)}, f32[17,16,384]{2,1,0:T(8,128)}) fusion(f32[17,32,384]{2,1,0:T(8,128)} %shard_map.129), kind=kLoop, calls=%fused_computation.144 | loop fusion | bytes 1671168 | tf_op jit(solution)/shard_map/slice | solution.py:166
  43.6 2.3 %collective-permute-start.11 = (f32[17,16,384]{2,1,0:T(8,128)}, f32[17,16,384]{2,1,0:T(8,128)S(1)}, u32[]{:S(2)}, u32[]{:S(2)}) collective-permute-start(f32[17,16,384]{2,1,0:T(8,128)} %get-tuple-element.35), channel_id=1, source_target_pairs={{32,0},{64,32},{96,64},{128,96},{160,128},{192,160},{224,192},{33,... | collective-permute-start | bytes 1253384 | tf_op jit(solution)/shard_map/ppermute | solution.py:134
  45.9 2.0 %collective-permute-start.8 = (f32[17,16,384]{2,1,0:T(8,128)}, f32[17,16,384]{2,1,0:T(8,128)S(1)}, u32[]{:S(2)}, u32[]{:S(2)}) collective-permute-start(f32[17,16,384]{2,1,0:T(8,128)} %get-tuple-element.34), channel_id=1, source_target_pairs={{0,32},{32,64},{64,96},{96,128},{128,160},{160,192},{192,224},{1,3... | collective-permute-start | bytes 1253384 | tf_op jit(solution)/shard_map/ppermute | solution.py:134
  50.5 6.8 %all-to-all-start = ((bf16[32,17,384]{2,1,0:T(8,128)(2,1)}), bf16[32,17,384]{2,1,0:T(8,128)(2,1)S(1)}, u32[]{:S(2)}, u32[]{:S(2)}) async-start(bf16[32,17,384]{2,1,0:T(8,128)(2,1)} %pad_maximum_fusion.6), calls=%async_computation | async-start | bytes 1179648 | tf_op jit(solution)/shard_map/all_to_all | solution.py:203
  58.9 2.4 %collective-permute-start.12 = (f32[17,16,384]{2,1,0:T(8,128)}, f32[17,16,384]{2,1,0:T(8,128)}, u32[]{:S(2)}, u32[]{:S(2)}) collective-permute-start(f32[17,16,384]{2,1,0:T(8,128)} %pad_maximum_fusion.13), channel_id=1, source_target_pairs={{64,0},{96,32},{128,64},{160,96},{192,128},{224,160},{65,1},{97,33... | collective-permute-start | bytes 1253384 | tf_op jit(solution)/shard_map/ppermute | solution.py:134
  62.1 3.5 %collective-permute-start.9 = (f32[17,16,384]{2,1,0:T(8,128)}, f32[17,16,384]{2,1,0:T(8,128)}, u32[]{:S(2)}, u32[]{:S(2)}) collective-permute-start(f32[17,16,384]{2,1,0:T(8,128)} %pad_maximum_fusion.11), channel_id=1, source_target_pairs={{0,64},{32,96},{64,128},{96,160},{128,192},{160,224},{1,65},{33,97... | collective-permute-start | bytes 1253384 | tf_op jit(solution)/shard_map/ppermute | solution.py:134
  65.6 12.0 %all-to-all-done = bf16[32,17,384]{2,1,0:T(8,128)(2,1)S(1)} async-done(((bf16[32,17,384]{2,1,0:T(8,128)(2,1)}), bf16[32,17,384]{2,1,0:T(8,128)(2,1)S(1)}, u32[]{:S(2)}, u32[]{:S(2)}) %all-to-all-start) | async-done | bytes 417824 | tf_op jit(solution)/shard_map/all_to_all | solution.py:203
  79.8 1.5 compare_select_fusion.3
  81.4 1.4 reshape.101
  84.4 1.5 compare_select_fusion.2
  85.9 1.4 reshape.102
  87.3 1.6 copy.146
  88.9 1.7 rev.32
  90.6 1.6 copy.145
  92.2 1.6 copy.148
  93.8 1.7 rev.33
  95.5 1.6 copy.147
  97.1 2.5 %broadcast_multiply_fusion.3 = (f32[128,4,384]{2,1,0:T(4,128)}, f32[128,4,384]{2,1,0:T(4,128)}) fusion(f32[128,4,384]{2,1,0:T(4,128)S(1)} %reshape.101, f32[128,4]{1,0:T(8,128)} %copy.142, f32[128,4,384]{2,1,0:T(4,128)S(1)} %reshape.102), kind=kLoop, calls=%fused_computation.61 | loop fusion | flops 393216 | bytes 3147776 | tf_op jit(solution)/shard_map/mul | solution.py:59
  99.6 1.2 pad_maximum_fusion.7
  100.8 1.3 pad_maximum_fusion.2.x_ref
  102.2 2.6 %pad_maximum_fusion.delta_ref = f32[128,8,384]{2,1,0:T(8,128)} fusion(f32[128,4,384]{2,1,0:T(4,128)S(1)} %rev.31, f32[128,4,384]{2,1,0:T(4,128)} %get-tuple-element.72), kind=kLoop, calls=%fused_computation.4 | loop fusion | flops 393216 | bytes 3145728 | tf_op jit(solution)/shard_map/concatenate | solution.py:158
  104.8 15.0 %shard_map.127 = f32[17,8,384]{2,1,0:T(8,128)} custom-call(f32[16,8,384]{2,1,0:T(8,128)} %pad_maximum_fusion.17.neg_rate_ref, f32[8,384]{1,0:T(8,128)} %pad_maximum_fusion.24.skip_ref, bf16[128,8,384]{2,1,0:T(8,128)(2,1)} %pad_maximum_fusion.2.x_ref, f32[128,8,384]{2,1,0:T(8,128)} %pad_maximum_fusion.delta_ref, f32[128,8,16]{2,1,0:T(8,128)} %get-tuple-element.82.entry_ref, ...), custom_call_target="tpu_custom_call" | custom-call | tf_op jit(solution)/shard_map/pallas_call | solution.py:114
  120.9 1.3 collective-permute-start.4
  122.2 4.6 %collective-permute-start.6 = (f32[17,4,384]{2,1,0:T(4,128)S(1)}, f32[17,4,384]{2,1,0:T(4,128)S(1)}, u32[]{:S(2)}, u32[]{:S(2)}) collective-permute-start(f32[17,4,384]{2,1,0:T(4,128)S(1)} %get-tuple-element.53), channel_id=1, source_target_pairs={{8,0},{16,8},{24,16},{9,1},{17,9},{25,17},{10,2},{18,10},{26,18},{... | collective-permute-start | bytes 313352 | tf_op jit(solution)/shard_map/ppermute | solution.py:134
  128.7 1.3 collective-permute-start.13
  130.2 4.2 %collective-permute-start.7 = (f32[17,4,384]{2,1,0:T(4,128)S(1)}, f32[17,4,384]{2,1,0:T(4,128)S(1)}, u32[]{:S(2)}, u32[]{:S(2)}) collective-permute-start(f32[17,4,384]{2,1,0:T(4,128)S(1)} %pad_maximum_fusion.19), channel_id=1, source_target_pairs={{16,0},{24,8},{17,1},{25,9},{18,2},{26,10},{19,3},{27,11},{20,4},{... | collective-permute-start | bytes 313352 | tf_op jit(solution)/shard_map/ppermute | solution.py:134
  134.4 1.5 collective-permute-start.5
  137.8 4.7 %collective-permute-done.5 = f32[17,4,384]{2,1,0:T(4,128)S(1)} collective-permute-done((f32[17,4,384]{2,1,0:T(4,128)S(1)}, f32[17,4,384]{2,1,0:T(4,128)S(1)}, u32[]{:S(2)}, u32[]{:S(2)}) %collective-permute-start.5) | collective-permute-done | bytes 104480 | tf_op jit(solution)/shard_map/ppermute | solution.py:134
  143.3 19.1 %shard_map.128 = (f32[128,8,384]{2,1,0:T(8,128)}, f32[17,8,384]{2,1,0:T(8,128)}) custom-call(f32[16,8,384]{2,1,0:T(8,128)} %pad_maximum_fusion.17.neg_rate_ref, f32[8,384]{1,0:T(8,128)} %pad_maximum_fusion.24.skip_ref, bf16[128,8,384]{2,1,0:T(8,128)(2,1)} %pad_maximum_fusion.2.x_ref, f32[128,8,384]{2,1,0:T(8,128)} %pad_maximum_fusion.delta_ref, ...), custom_call_target="tpu_custom_call" | custom-call | tf_op jit(solution)/shard_map/pallas_call | solution.py:114
  162.4 1.7 slice.376
  165.4 3.7 %all-to-all-start.1 = ((f32[128,4,384]{2,1,0:T(4,128)}), f32[128,4,384]{2,1,0:T(4,128)S(1)}, u32[]{:S(2)}, u32[]{:S(2)}) async-start(f32[128,4,384]{2,1,0:T(4,128)} %reverse_add_fusion), calls=%async_computation.1 | async-start | bytes 1572864 | tf_op jit(solution)/shard_map/all_to_all | solution.py:211
  169.1 5.9 %collective-permute-start.10 = (f32[17,16,384]{2,1,0:T(8,128)S(1)}, f32[17,16,384]{2,1,0:T(8,128)S(1)}, u32[]{:S(2)}, u32[]{:S(2)}) collective-permute-start(f32[17,16,384]{2,1,0:T(8,128)S(1)} %pad_maximum_fusion.12), channel_id=1, source_target_pairs={{0,128},{32,160},{64,192},{96,224},{1,129},{33,161},{65,193},{97,2... | collective-permute-start | bytes 1253384 | tf_op jit(solution)/shard_map/ppermute | solution.py:134
  175.8 6.1 %collective-permute-done.10 = f32[17,16,384]{2,1,0:T(8,128)S(1)} collective-permute-done((f32[17,16,384]{2,1,0:T(8,128)S(1)}, f32[17,16,384]{2,1,0:T(8,128)S(1)}, u32[]{:S(2)}, u32[]{:S(2)}) %collective-permute-start.10) | collective-permute-done | bytes 417824 | tf_op jit(solution)/shard_map/ppermute | solution.py:134
  182.7 1.3 fusion.12
  186.1 11.8 %shard_map.130 = (f32[32,32,384]{2,1,0:T(8,128)}, f32[17,32,384]{2,1,0:T(8,128)}) custom-call(f32[16,32,384]{2,1,0:T(8,128)} %pad_maximum_fusion.3.neg_rate_ref, f32[32,384]{1,0:T(8,128)} %pad_maximum_fusion.23.skip_ref, bf16[32,32,384]{2,1,0:T(8,128)(2,1)} %pad_maximum_fusion.4.x_ref, f32[32,32,384]{2,1,0:T(8,128)} %pad_maximum_fusion.1.delta_ref, ...), custom_call_target="tpu_custom_call" | custom-call | tf_op jit(solution)/shard_map/pallas_call | solution.py:114
  197.9 1.3 slice.412
  200.9 1.2 fusion.1
  (189 shorter events, 32.2 us)
Async XLA Ops:
  0.0 3.6 %copy-start = (bf16[192,768]{1,0:T(8,128)(2,1)S(1)}, bf16[192,768]{1,0:T(8,128)(2,1)}, u32[]{:S(2)}) copy-start(bf16[192,768]{1,0:T(8,128)(2,1)} %param.16) | copy-start | bytes 884740
  0.0 8.3 %copy-start.26 = (f32[4,384,16]{1,2,0:T(8,128)S(1)}, f32[4,384,16]{1,2,0:T(8,128)}, u32[]{:S(2)}) copy-start(f32[4,384,16]{1,2,0:T(8,128)} %param.22) | copy-start | bytes 294916
  0.0 9.0 %copy-start.36 = (f32[4,384]{1,0:T(4,128)S(1)}, f32[4,384]{1,0:T(4,128)}, u32[]{:S(2)}) copy-start(f32[4,384]{1,0:T(4,128)} %param.23) | copy-start | bytes 18436
  0.0 9.6 %copy-start.29 = (bf16[3,3,384]{2,1,0:T(4,128)(2,1)S(1)}, bf16[3,3,384]{2,1,0:T(4,128)(2,1)}, u32[]{:S(2)}) copy-start(bf16[3,3,384]{2,1,0:T(4,128)(2,1)} %param.17) | copy-start | bytes 20740
  0.0 9.6 %copy-start.16 = (bf16[4,384,44]{1,0,2:T(4,128)(2,1)S(1)}, bf16[4,384,44]{1,0,2:T(4,128)(2,1)}, u32[]{:S(2)}) copy-start(bf16[4,384,44]{1,0,2:T(4,128)(2,1)} %param.19) | copy-start | bytes 405508
  1.2 9.3 %copy-start.25 = (bf16[4,12,384]{2,0,1:T(4,128)(2,1)S(1)}, bf16[4,12,384]{2,0,1:T(4,128)(2,1)}, u32[]{:S(2)}) copy-start(bf16[4,12,384]{2,0,1:T(4,128)(2,1)} %param.20) | copy-start | bytes 110596
  1.2 9.9 %copy-start.33 = (s32[32,16]{0,1:T(8,128)S(1)}, s32[32,16]{0,1:T(8,128)}, u32[]{:S(2)}) copy-start(s32[32,16]{0,1:T(8,128)} %param.14) | copy-start | bytes 6148
  4.0 9.5 %copy-start.5 = (bf16[512,768]{1,0:T(8,128)(2,1)}, bf16[512,768]{1,0:T(8,128)(2,1)S(1)}, u32[]{:S(2)}) copy-start(bf16[512,768]{1,0:T(8,128)(2,1)S(1)} %convolution_convert_fusion) | copy-start | bytes 2359300
  4.0 9.5 %collective-permute-start.1 = (bf16[1,16,384]{2,1,0:T(8,128)(2,1)S(1)}, bf16[1,16,384]{2,1,0:T(8,128)(2,1)S(1)}, u32[]{:S(2)}, u32[]{:S(2)}) collective-permute-start(bf16[1,16,384]{2,1,0:T(8,128)(2,1)S(1)} %get-tuple-element.39), channel_id=1, source_target_pairs={{32,0},{64,32},{96,64},{128,96},{160,128},{192,160},{224,192},{33,... | collective-permute-start | bytes 36872 | tf_op jit(solution)/shard_map/ppermute | solution.py:18
  5.9 7.6 %collective-permute-start = (bf16[1,16,384]{2,1,0:T(8,128)(2,1)S(1)}, bf16[1,16,384]{2,1,0:T(8,128)(2,1)S(1)}, u32[]{:S(2)}, u32[]{:S(2)}) collective-permute-start(bf16[1,16,384]{2,1,0:T(8,128)(2,1)S(1)} %get-tuple-element.38), channel_id=1, source_target_pairs={{0,32},{32,64},{64,96},{96,128},{128,160},{160,192},{192,224},{1,3... | collective-permute-start | bytes 36872 | tf_op jit(solution)/shard_map/ppermute | solution.py:15
  11.8 11.8 %copy-start.37 = (f32[4,384]{1,0:T(4,128)S(1)}, f32[4,384]{1,0:T(4,128)}, u32[]{:S(2)}) copy-start(f32[4,384]{1,0:T(4,128)} %param.21) | copy-start | bytes 18436
  13.4 12.4 %copy-start.38 = (f32[384]{0:T(512)S(1)}, f32[384]{0:T(512)}, u32[]{:S(2)}) copy-start(f32[384]{0:T(512)} %param.18) | copy-start | bytes 4612
  13.6 10.7 %collective-permute-start.2 = (bf16[34,1,384]{2,1,0:T(2,128)(2,1)S(1)}, bf16[34,1,384]{2,1,0:T(2,128)(2,1)S(1)}, u32[]{:S(2)}, u32[]{:S(2)}) collective-permute-start(bf16[34,1,384]{2,1,0:T(2,128)(2,1)S(1)} %get-tuple-element.44), channel_id=1, source_target_pairs={{0,1},{1,2},{2,3},{3,4},{4,5},{5,6},{6,7},{7,8},{8,9},{9,10},{10,1... | collective-permute-start | bytes 78344 | tf_op jit(solution)/shard_map/ppermute | solution.py:15
  17.4 8.1 %collective-permute-start.3 = (bf16[34,1,384]{2,1,0:T(2,128)(2,1)S(1)}, bf16[34,1,384]{2,1,0:T(2,128)(2,1)S(1)}, u32[]{:S(2)}, u32[]{:S(2)}) collective-permute-start(bf16[34,1,384]{2,1,0:T(2,128)(2,1)S(1)} %get-tuple-element.45), channel_id=1, source_target_pairs={{1,0},{2,1},{3,2},{4,3},{5,4},{6,5},{7,6},{8,7},{9,8},{10,9},{11,1... | collective-permute-start | bytes 78344 | tf_op jit(solution)/shard_map/ppermute | solution.py:18
  41.5 6.5 %copy-start.32 = (bf16[32,16]{0,1:T(8,128)(2,1)S(1)}, bf16[32,16]{0,1:T(8,128)(2,1)}, u32[]{:S(2)}) copy-start(bf16[32,16]{0,1:T(8,128)(2,1)} %get-tuple-element.80) | copy-start | bytes 3076
  41.5 6.6 %copy-start.35 = (f32[384]{0:T(512)S(1)}, f32[384]{0:T(512)}, u32[]{:S(2)}) copy-start(f32[384]{0:T(512)} %get-tuple-element.23) | copy-start | bytes 4612
  41.5 6.7 %copy-start.34 = (f32[384]{0:T(512)S(1)}, f32[384]{0:T(512)}, u32[]{:S(2)}) copy-start(f32[384]{0:T(512)} %get-tuple-element.22) | copy-start | bytes 4612
  41.5 7.3 %copy-start.17 = (f32[16,384]{1,0:T(8,128)S(1)}, f32[16,384]{1,0:T(8,128)}, u32[]{:S(2)}) copy-start(f32[16,384]{1,0:T(8,128)} %get-tuple-element.65) | copy-start | bytes 73732
  43.6 13.6 %collective-permute-start.11 = (f32[17,16,384]{2,1,0:T(8,128)}, f32[17,16,384]{2,1,0:T(8,128)S(1)}, u32[]{:S(2)}, u32[]{:S(2)}) collective-permute-start(f32[17,16,384]{2,1,0:T(8,128)} %get-tuple-element.35), channel_id=1, source_target_pairs={{32,0},{64,32},{96,64},{128,96},{160,128},{192,160},{224,192},{33,... | collective-permute-start | bytes 1253384 | tf_op jit(solution)/shard_map/ppermute | solution.py:134
  45.9 11.3 %collective-permute-start.8 = (f32[17,16,384]{2,1,0:T(8,128)}, f32[17,16,384]{2,1,0:T(8,128)S(1)}, u32[]{:S(2)}, u32[]{:S(2)}) collective-permute-start(f32[17,16,384]{2,1,0:T(8,128)} %get-tuple-element.34), channel_id=1, source_target_pairs={{0,32},{32,64},{64,96},{96,128},{128,160},{160,192},{192,224},{1,3... | collective-permute-start | bytes 1253384 | tf_op jit(solution)/shard_map/ppermute | solution.py:134
  47.9 9.3 %copy-start.1 = (f32[17,32,384]{2,1,0:T(8,128)S(1)}, f32[17,32,384]{2,1,0:T(8,128)}, u32[]{:S(2)}) copy-start(f32[17,32,384]{2,1,0:T(8,128)} %shard_map.129) | copy-start | bytes 2506756
  50.5 27.1 %all-to-all-start = ((bf16[32,17,384]{2,1,0:T(8,128)(2,1)}), bf16[32,17,384]{2,1,0:T(8,128)(2,1)S(1)}, u32[]{:S(2)}, u32[]{:S(2)}) async-start(bf16[32,17,384]{2,1,0:T(8,128)(2,1)} %pad_maximum_fusion.6), calls=%async_computation | async-start | bytes 1179648 | tf_op jit(solution)/shard_map/all_to_all | solution.py:203
  58.0 3.3 %copy-start.19 = (f32[1,16,384]{2,1,0:T(8,128)}, f32[1,16,384]{2,1,0:T(8,128)S(1)}, u32[]{:S(2)}) copy-start(f32[1,16,384]{2,1,0:T(8,128)S(1)} %get-tuple-element.31) | copy-start | bytes 73732
  58.9 67.9 %collective-permute-start.12 = (f32[17,16,384]{2,1,0:T(8,128)}, f32[17,16,384]{2,1,0:T(8,128)}, u32[]{:S(2)}, u32[]{:S(2)}) collective-permute-start(f32[17,16,384]{2,1,0:T(8,128)} %pad_maximum_fusion.13), channel_id=1, source_target_pairs={{64,0},{96,32},{128,64},{160,96},{192,128},{224,160},{65,1},{97,33... | collective-permute-start | bytes 1253384 | tf_op jit(solution)/shard_map/ppermute | solution.py:134
  62.1 73.8 %collective-permute-start.9 = (f32[17,16,384]{2,1,0:T(8,128)}, f32[17,16,384]{2,1,0:T(8,128)}, u32[]{:S(2)}, u32[]{:S(2)}) collective-permute-start(f32[17,16,384]{2,1,0:T(8,128)} %pad_maximum_fusion.11), channel_id=1, source_target_pairs={{0,64},{32,96},{64,128},{96,160},{128,192},{160,224},{1,65},{33,97... | collective-permute-start | bytes 1253384 | tf_op jit(solution)/shard_map/ppermute | solution.py:134
  77.8 2.1 %copy-start.31 = (bf16[1,12,384]{2,0,1:T(2,128)(2,1)S(1)}, bf16[1,12,384]{2,0,1:T(2,128)(2,1)}, u32[]{:S(2)}) copy-start(bf16[1,12,384]{2,0,1:T(2,128)(2,1)} %get-tuple-element.74) | copy-start | bytes 27652
  79.8 3.7 %copy-start.23 = (bf16[1,384,44]{1,0,2:T(2,128)(2,1)S(1)}, bf16[1,384,44]{1,0,2:T(2,128)(2,1)}, u32[]{:S(2)}) copy-start(bf16[1,384,44]{1,0,2:T(2,128)(2,1)} %get-tuple-element.56) | copy-start | bytes 101380
  81.4 3.1 %copy-start.30 = (bf16[1,12,384]{2,0,1:T(2,128)(2,1)S(1)}, bf16[1,12,384]{2,0,1:T(2,128)(2,1)}, u32[]{:S(2)}) copy-start(bf16[1,12,384]{2,0,1:T(2,128)(2,1)} %get-tuple-element.76) | copy-start | bytes 27652
  81.4 3.1 %copy-start.39 = (f32[384]{0:T(512)S(1)}, f32[384]{0:T(512)}, u32[]{:S(2)}) copy-start(f32[384]{0:T(512)} %get-tuple-element.19) | copy-start | bytes 4612
  97.1 2.5 %copy-start.12 = (f32[128,4,16]{2,1,0:T(4,128)S(1)}, f32[128,4,16]{2,1,0:T(4,128)}, u32[]{:S(2)}) copy-start(f32[128,4,16]{2,1,0:T(4,128)} %rev.32) | copy-start | bytes 98308
  97.1 2.5 %copy-start.13 = (f32[512,16]{1,0:T(8,128)S(1)}, f32[512,16]{1,0:T(8,128)}, u32[]{:S(2)}) copy-start(f32[512,16]{1,0:T(8,128)} %copy.145) | copy-start | bytes 98308
  97.1 2.5 %copy-start.14 = (f32[128,4,16]{2,1,0:T(4,128)S(1)}, f32[128,4,16]{2,1,0:T(4,128)}, u32[]{:S(2)}) copy-start(f32[128,4,16]{2,1,0:T(4,128)} %rev.33) | copy-start | bytes 98308
  97.1 2.5 %copy-start.15 = (f32[512,16]{1,0:T(8,128)S(1)}, f32[512,16]{1,0:T(8,128)}, u32[]{:S(2)}) copy-start(f32[512,16]{1,0:T(8,128)} %copy.147) | copy-start | bytes 98308
  99.6 2.6 %copy-start.2 = (f32[128,4,384]{2,1,0:T(4,128)S(1)}, f32[128,4,384]{2,1,0:T(4,128)}, u32[]{:S(2)}) copy-start(f32[128,4,384]{2,1,0:T(4,128)} %get-tuple-element.73) | copy-start | bytes 2359300
  104.8 22.0 %copy-start.22 = (f32[1,16,384]{2,1,0:T(8,128)S(1)}, f32[1,16,384]{2,1,0:T(8,128)}, u32[]{:S(2)}) copy-start(f32[1,16,384]{2,1,0:T(8,128)} %copy-done.21) | copy-start | bytes 73732
  119.8 10.2 %copy-start.4 = (f32[17,8,384]{2,1,0:T(8,128)S(1)}, f32[17,8,384]{2,1,0:T(8,128)}, u32[]{:S(2)}) copy-start(f32[17,8,384]{2,1,0:T(8,128)} %shard_map.127) | copy-start | bytes 626692
  119.8 10.2 %copy-start.18 = (f32[16,384]{1,0:T(8,128)S(1)}, f32[16,384]{1,0:T(8,128)}, u32[]{:S(2)}) copy-start(f32[16,384]{1,0:T(8,128)} %get-tuple-element.65) | copy-start | bytes 73732
  120.9 9.0 %collective-permute-start.4 = (f32[17,4,384]{2,1,0:T(4,128)S(1)}, f32[17,4,384]{2,1,0:T(4,128)S(1)}, u32[]{:S(2)}, u32[]{:S(2)}) collective-permute-start(f32[17,4,384]{2,1,0:T(4,128)S(1)} %get-tuple-element.52), channel_id=1, source_target_pairs={{0,8},{8,16},{16,24},{1,9},{9,17},{17,25},{2,10},{10,18},{18,26},{... | collective-permute-start | bytes 313352 | tf_op jit(solution)/shard_map/ppermute | solution.py:134
  122.2 7.8 %collective-permute-start.6 = (f32[17,4,384]{2,1,0:T(4,128)S(1)}, f32[17,4,384]{2,1,0:T(4,128)S(1)}, u32[]{:S(2)}, u32[]{:S(2)}) collective-permute-start(f32[17,4,384]{2,1,0:T(4,128)S(1)} %get-tuple-element.53), channel_id=1, source_target_pairs={{8,0},{16,8},{24,16},{9,1},{17,9},{25,17},{10,2},{18,10},{26,18},{... | collective-permute-start | bytes 313352 | tf_op jit(solution)/shard_map/ppermute | solution.py:134
  127.6 8.4 %copy-start.20 = (f32[1,16,384]{2,1,0:T(8,128)S(1)}, f32[1,16,384]{2,1,0:T(8,128)}, u32[]{:S(2)}) copy-start(f32[1,16,384]{2,1,0:T(8,128)} %copy-done.19) | copy-start | bytes 73732
  128.7 46.4 %collective-permute-start.13 = (f32[17,16,384]{2,1,0:T(8,128)S(1)}, f32[17,16,384]{2,1,0:T(8,128)}, u32[]{:S(2)}, u32[]{:S(2)}) collective-permute-start(f32[17,16,384]{2,1,0:T(8,128)S(1)} %pad_maximum_fusion.14), channel_id=1, source_target_pairs={{128,0},{160,32},{192,64},{224,96},{129,1},{161,33},{193,65},{225,... | collective-permute-start | bytes 1253384 | tf_op jit(solution)/shard_map/ppermute | solution.py:134
  130.2 7.6 %collective-permute-start.7 = (f32[17,4,384]{2,1,0:T(4,128)S(1)}, f32[17,4,384]{2,1,0:T(4,128)S(1)}, u32[]{:S(2)}, u32[]{:S(2)}) collective-permute-start(f32[17,4,384]{2,1,0:T(4,128)S(1)} %pad_maximum_fusion.19), channel_id=1, source_target_pairs={{16,0},{24,8},{17,1},{25,9},{18,2},{26,10},{19,3},{27,11},{20,4},{... | collective-permute-start | bytes 313352 | tf_op jit(solution)/shard_map/ppermute | solution.py:134
  134.4 8.1 %collective-permute-start.5 = (f32[17,4,384]{2,1,0:T(4,128)S(1)}, f32[17,4,384]{2,1,0:T(4,128)S(1)}, u32[]{:S(2)}, u32[]{:S(2)}) collective-permute-start(f32[17,4,384]{2,1,0:T(4,128)S(1)} %pad_maximum_fusion.18), channel_id=1, source_target_pairs={{0,16},{8,24},{1,17},{9,25},{2,18},{10,26},{3,19},{11,27},{4,20},{... | collective-permute-start | bytes 313352 | tf_op jit(solution)/shard_map/ppermute | solution.py:134
  165.4 9.7 %copy-start.8 = (f32[17,16,384]{2,1,0:T(8,128)S(1)}, f32[17,16,384]{2,1,0:T(8,128)}, u32[]{:S(2)}) copy-start(f32[17,16,384]{2,1,0:T(8,128)} %copy-done.7) | copy-start | bytes 1253380
  165.4 17.3 %copy-start.28 = (f32[16,384]{1,0:T(8,128)S(1)}, f32[16,384]{1,0:T(8,128)}, u32[]{:S(2)}) copy-start(f32[16,384]{1,0:T(8,128)} %get-tuple-element.40) | copy-start | bytes 73732
  165.4 33.8 %all-to-all-start.1 = ((f32[128,4,384]{2,1,0:T(4,128)}), f32[128,4,384]{2,1,0:T(4,128)S(1)}, u32[]{:S(2)}, u32[]{:S(2)}) async-start(f32[128,4,384]{2,1,0:T(4,128)} %reverse_add_fusion), calls=%async_computation.1 | async-start | bytes 1572864 | tf_op jit(solution)/shard_map/all_to_all | solution.py:211
  169.1 14.8 %copy-start.27 = (f32[16,384]{1,0:T(8,128)S(1)}, f32[16,384]{1,0:T(8,128)}, u32[]{:S(2)}) copy-start(f32[16,384]{1,0:T(8,128)} %get-tuple-element.41) | copy-start | bytes 73732
  169.1 12.8 %collective-permute-start.10 = (f32[17,16,384]{2,1,0:T(8,128)S(1)}, f32[17,16,384]{2,1,0:T(8,128)S(1)}, u32[]{:S(2)}, u32[]{:S(2)}) collective-permute-start(f32[17,16,384]{2,1,0:T(8,128)S(1)} %pad_maximum_fusion.12), channel_id=1, source_target_pairs={{0,128},{32,160},{64,192},{96,224},{1,129},{33,161},{65,193},{97,2... | collective-permute-start | bytes 1253384 | tf_op jit(solution)/shard_map/ppermute | solution.py:134
  (11 other events, 15.3 us)

commit v3 on v2

--- a/solution.py
+++ b/solution.py
@@ -149,15 +149,36 @@
     return jnp.broadcast_to(value[..., None, :], value.shape[:-1] + (seqs, value.shape[-1]))
 
 
+def pair_inputs(stacked_x, stacked_mask, ahead, back, proj_weight, dt_weight, dt_bias, seqs):
+    rank = dt_weight.shape[1]
+    length, both_seqs, inner = stacked_x.shape
+    flat = stacked_x.reshape(length * both_seqs, inner)
+    weights = jnp.concatenate([proj_weight[ahead], proj_weight[back]], axis=1)
+    width = proj_weight.shape[2]
+    projections = jnp.dot(flat, weights, preferred_element_type=jnp.float32)
+    projections = projections.reshape(length, both_seqs, 2 * width)
+    is_fwd = (lax.broadcasted_iota(jnp.int32, (1, both_seqs, 1), 1) < seqs)
+    chosen = jnp.where(is_fwd, projections[:, :, :width], projections[:, :, width:])
+    rate_low = chosen[:, :, :rank].astype(jnp.bfloat16).reshape(length * both_seqs, rank)
+    step_fwd = jnp.dot(rate_low, dt_weight[ahead], preferred_element_type=jnp.float32)
+    step_bwd = jnp.dot(rate_low, dt_weight[back], preferred_element_type=jnp.float32)
+    step_fwd = step_fwd.reshape(length, both_seqs, inner) + dt_bias[ahead]
+    step_bwd = step_bwd.reshape(length, both_seqs, inner) + dt_bias[back]
+    delta = jax.nn.softplus(jnp.where(is_fwd, step_fwd, step_bwd)) * stacked_mask[:, :, None]
+    nstate = (width - rank) // 2
+    entry = chosen[:, :, rank : rank + nstate]
+    readout = chosen[:, :, rank + nstate :]
+    return (delta, entry, readout)
+
+
 def direction_pair(seq_x, seq_mask, ahead, back, proj_weight, dt_weight, dt_bias, a_rate, skip_d,
                    axis):
     length, seqs, inner = seq_x.shape
-    nstate = a_rate.shape[2]
-    fwd = direction_inputs(seq_x, seq_mask, proj_weight[ahead], dt_weight[ahead], dt_bias[ahead])
-    bwd = direction_inputs(seq_x, seq_mask, proj_weight[back], dt_weight[back], dt_bias[back])
-    both = [jnp.concatenate([f, flipped(b)], axis=1) for f, b in zip(fwd, bwd)]
-    delta, entry, readout = both
     stacked_x = jnp.concatenate([seq_x, flipped(seq_x)], axis=1)
+    stacked_mask = jnp.concatenate([seq_mask, flipped(seq_mask)], axis=1)
+    delta, entry, readout = pair_inputs(
+        stacked_x, stacked_mask, ahead, back, proj_weight, dt_weight, dt_bias, seqs
+    )
     neg_fwd = -jnp.transpose(a_rate[ahead])
     neg_bwd = -jnp.transpose(a_rate[back])
     neg_rate = jnp.concatenate([rows_of(neg_fwd, seqs), rows_of(neg_bwd, seqs)], axis=1)

time: 205 us -> 186 us (0.907)
  local copies, waits for them, and re-layouts: 27.4 us -> 14.7 us
  other arithmetic: 34.9 us -> 26 us
    concatenate x4 -> x2, other arithmetic: 6.45 us -> 0.02 us  [direction_pair(): stacked_mask = jnp.concatenate([seq_mask, flipped(seq_mask)], axis=1)]
    slice x15 -> x5, local copies, waits for them, and re-layouts: 10.3 us -> 4.15 us  [the longest x2 2.69 us: pair_inputs(): readout = chosen[:, :, rank + nstate:]]
    rev x8 -> x4, local copies, waits for them, and re-layouts: 4.52 us -> 0.35 us  [flipped(): return array[::-1]]
    reshape x3 -> x0, local copies, waits for them, and re-layouts: 2.83 us -> none  [the longest x2 2.73 us: direction_inputs(): delta = delta.reshape(length, seqs, inner) * seq_mask[:, :, None]]
    mul x2 -> x0, other arithmetic: 2.63 us -> none  [direction_inputs(): delta = delta.reshape(length, seqs, inner) * seq_mask[:, :, None]]
    dot_general x8 -> x6, matrix products: 5.11 us -> 6.17 us  [the longest x2 4.66 us: pair_inputs(): jnp.dot(rate_low, dt_weight[back], preferred_element_type=jnp.float32)]
  transfers between devices with their start and end apart: 16 -> 16, of which waited for: 4 -> 5; matrix products, arithmetic and copies ran while one was open for 26% -> 17% of each run, Pallas kernels for 23% -> 25%
where the time goes in v3:
time: 186 us; the launch traced here: 183 us
  Pallas kernels  54.5 us (29%)
  starting transfers between devices  54.2 us (29%)
  other arithmetic  26 us (14%)
  waiting for transfers between devices  24.8 us (13%)
  local copies, waits for them, and re-layouts  14.7 us (8%)
  matrix products  7.71 us (4%)
    pallas_call x4, Pallas kernels, run_scan(): return pl.pallas_call(kernel, out_shape=tuple(out_shape))(*args)  54.5 us
    ppermute x10, starting transfers between devices, carried_in(): got = lax.ppermute(inclusive, axis, pairs)  29.6 us
    ppermute x10, waiting for transfers between devices, carried_in(): got = lax.ppermute(inclusive, axis, pairs)  12.2 us
    all_to_all x1, waiting for transfers between devices, local(): band = lax.all_to_all(sent, 'cz', 0, 1, tiled=True)  10.9 us
    ppermute x2, starting transfers between devices, padded_2(): lax.ppermute(lax.slice_in_dim(block, 0, width, axis=dim), axis, backward)  8.04 us
    all_to_all x1, starting transfers between devices, local(): band = lax.all_to_all(sent, 'cz', 0, 1, tiled=True)  6.76 us
    ppermute x2, starting transfers between devices, padded_2(): lax.ppermute(lax.slice_in_dim(block, block.shape[dim] - width, None, axis...  6.23 us
    add x8, other arithmetic, combine(): state = decay * earlier[:nstate] + later[:nstate]  5.23 us
  transfers between devices with their start and end apart: 16, of which 5 were waited for; matrix products, arithmetic and copies ran while one was open for 17% of the time, Pallas kernels for 25%

profile of v3, /device:TPU:14, one launch (start us, length us, event | category | flops | bytes accessed | tf_op | source)
XLA Modules:
  0.0 182.6 jit_solution(14087288212808026964)
XLA Ops:
  0.0 1.1 convert_reduce_fusion
  1.2 1.2 fusion.11
  2.5 1.2 fusion.13
  4.0 1.9 %collective-permute-start.1 = (bf16[1,16,384]{2,1,0:T(8,128)(2,1)S(1)}, bf16[1,16,384]{2,1,0:T(8,128)(2,1)S(1)}, u32[]{:S(2)}, u32[]{:S(2)}) collective-permute-start(bf16[1,16,384]{2,1,0:T(8,128)(2,1)S(1)} %get-tuple-element.39), channel_id=1, source_target_pairs={{32,0},{64,32},{96,64},{128,96},{160,128},{192,160},{224,192},{33,... | collective-permute-start | bytes 36872 | tf_op jit(solution)/shard_map/ppermute | solution.py:18
  5.9 2.4 %collective-permute-start = (bf16[1,16,384]{2,1,0:T(8,128)(2,1)S(1)}, bf16[1,16,384]{2,1,0:T(8,128)(2,1)S(1)}, u32[]{:S(2)}, u32[]{:S(2)}) collective-permute-start(bf16[1,16,384]{2,1,0:T(8,128)(2,1)S(1)} %get-tuple-element.38), channel_id=1, source_target_pairs={{0,32},{32,64},{64,96},{96,128},{128,160},{160,192},{192,224},{1,3... | collective-permute-start | bytes 36872 | tf_op jit(solution)/shard_map/ppermute | solution.py:15
  10.2 1.0 pad_maximum_fusion.1.neg_rate_ref
  13.3 3.8 %collective-permute-start.2 = (bf16[34,1,384]{2,1,0:T(2,128)(2,1)S(1)}, bf16[34,1,384]{2,1,0:T(2,128)(2,1)S(1)}, u32[]{:S(2)}, u32[]{:S(2)}) collective-permute-start(bf16[34,1,384]{2,1,0:T(2,128)(2,1)S(1)} %get-tuple-element.48), channel_id=1, source_target_pairs={{0,1},{1,2},{2,3},{3,4},{4,5},{5,6},{6,7},{7,8},{8,9},{9,10},{10,1... | collective-permute-start | bytes 78344 | tf_op jit(solution)/shard_map/ppermute | solution.py:15
  17.2 6.1 %collective-permute-start.3 = (bf16[34,1,384]{2,1,0:T(2,128)(2,1)S(1)}, bf16[34,1,384]{2,1,0:T(2,128)(2,1)S(1)}, u32[]{:S(2)}, u32[]{:S(2)}) collective-permute-start(bf16[34,1,384]{2,1,0:T(2,128)(2,1)S(1)} %get-tuple-element.49), channel_id=1, source_target_pairs={{1,0},{2,1},{3,2},{4,3},{5,4},{6,5},{7,6},{8,7},{9,8},{10,9},{11,1... | collective-permute-start | bytes 78344 | tf_op jit(solution)/shard_map/ppermute | solution.py:18
  23.6 1.7 collective-permute-done.3
  26.5 1.0 pad_maximum_fusion.2.x_ref
  28.0 1.3 fusion.36
  29.6 2.3 %fusion.1.delta_ref = f32[32,32,384]{2,1,0:T(8,128)} fusion(f32[32,32,384]{2,1,0:T(8,128)S(1)} %fusion.19, f32[32,32]{1,0:T(8,128)S(1)} %copy.82, f32[384]{0:T(512)S(1)} %get-tuple-element.20, f32[384]{0:T(512)S(1)} %get-tuple-element.21, pred[32]{0:T(512)(128)(4,1)S(1)} %iota_compare_fusion, f32[32,32,44]{2,1,0:T(8,128)S(1)} %slice_select_fusion, ...), kind=kOutput, calls=%fused_computation.3 | convolution fusion | flops 13369344 | bytes 3447296 | tf_op jit(solution)/shard_map/dot_general | solution.py:164
  32.0 8.6 %shard_map.129 = f32[17,32,384]{2,1,0:T(8,128)} custom-call(f32[16,32,384]{2,1,0:T(8,128)} %pad_maximum_fusion.1.neg_rate_ref, f32[32,384]{1,0:T(8,128)} %pad_maximum_fusion.17.skip_ref, bf16[32,32,384]{2,1,0:T(8,128)(2,1)} %pad_maximum_fusion.2.x_ref, f32[32,32,384]{2,1,0:T(8,128)} %fusion.1.delta_ref, f32[32,32,16]{2,1,0:T(8,128)} %get-tuple-element.43.entry_ref, ...), custom_call_target="tpu_custom_call" | custom-call | tf_op jit(solution)/shard_map/pallas_call | solution.py:114
  40.6 2.2 %fusion.33 = (f32[17,16,384]{2,1,0:T(8,128)}, f32[17,16,384]{2,1,0:T(8,128)}) fusion(f32[17,32,384]{2,1,0:T(8,128)} %shard_map.129), kind=kLoop, calls=%fused_computation.142 | loop fusion | bytes 1671168 | tf_op jit(solution)/shard_map/slice | solution.py:187
  42.7 2.4 %collective-permute-start.11 = (f32[17,16,384]{2,1,0:T(8,128)}, f32[17,16,384]{2,1,0:T(8,128)}, u32[]{:S(2)}, u32[]{:S(2)}) collective-permute-start(f32[17,16,384]{2,1,0:T(8,128)} %get-tuple-element.35), channel_id=1, source_target_pairs={{32,0},{64,32},{96,64},{128,96},{160,128},{192,160},{224,192},{33,... | collective-permute-start | bytes 1253384 | tf_op jit(solution)/shard_map/ppermute | solution.py:134
  45.2 2.0 %collective-permute-start.8 = (f32[17,16,384]{2,1,0:T(8,128)}, f32[17,16,384]{2,1,0:T(8,128)}, u32[]{:S(2)}, u32[]{:S(2)}) collective-permute-start(f32[17,16,384]{2,1,0:T(8,128)} %get-tuple-element.34), channel_id=1, source_target_pairs={{0,32},{32,64},{64,96},{96,128},{128,160},{160,192},{192,224},{1,3... | collective-permute-start | bytes 1253384 | tf_op jit(solution)/shard_map/ppermute | solution.py:134
  48.4 0.9 pad_maximum_fusion.4
  49.3 6.8 %all-to-all-start = ((bf16[32,17,384]{2,1,0:T(8,128)(2,1)}), bf16[32,17,384]{2,1,0:T(8,128)(2,1)S(1)}, u32[]{:S(2)}, u32[]{:S(2)}) async-start(bf16[32,17,384]{2,1,0:T(8,128)(2,1)} %pad_maximum_fusion.4), calls=%async_computation | async-start | bytes 1179648 | tf_op jit(solution)/shard_map/all_to_all | solution.py:224
  56.8 1.3 slice_add_fusion.1
  58.9 3.1 %collective-permute-start.12 = (f32[17,16,384]{2,1,0:T(8,128)}, f32[17,16,384]{2,1,0:T(8,128)}, u32[]{:S(2)}, u32[]{:S(2)}) collective-permute-start(f32[17,16,384]{2,1,0:T(8,128)} %pad_maximum_fusion.7), channel_id=1, source_target_pairs={{64,0},{96,32},{128,64},{160,96},{192,128},{224,160},{65,1},{97,33... | collective-permute-start | bytes 1253384 | tf_op jit(solution)/shard_map/ppermute | solution.py:134
  62.8 2.7 %collective-permute-start.9 = (f32[17,16,384]{2,1,0:T(8,128)}, f32[17,16,384]{2,1,0:T(8,128)S(1)}, u32[]{:S(2)}, u32[]{:S(2)}) collective-permute-start(f32[17,16,384]{2,1,0:T(8,128)} %pad_maximum_fusion.5), channel_id=1, source_target_pairs={{0,64},{32,96},{64,128},{96,160},{128,192},{160,224},{1,65},{33,97... | collective-permute-start | bytes 1253384 | tf_op jit(solution)/shard_map/ppermute | solution.py:134
  65.5 10.9 %all-to-all-done = bf16[32,17,384]{2,1,0:T(8,128)(2,1)S(1)} async-done(((bf16[32,17,384]{2,1,0:T(8,128)(2,1)}), bf16[32,17,384]{2,1,0:T(8,128)(2,1)S(1)}, u32[]{:S(2)}, u32[]{:S(2)}) %all-to-all-start) | async-done | bytes 417824 | tf_op jit(solution)/shard_map/all_to_all | solution.py:224
  78.6 2.3 %fusion.delta_ref = f32[128,8,384]{2,1,0:T(8,128)} fusion(f32[128,8,384]{2,1,0:T(8,128)S(1)} %fusion.18, f32[128,8]{1,0:T(8,128)S(1)} %copy.74, f32[384]{0:T(512)S(1)} %copy-done.17, f32[384]{0:T(512)S(1)} %copy-done.16, pred[8]{0:T(512)(128)(4,1)S(1)} %copy-done.18, f32[128,8,44]{2,1,0:T(8,128)S(1)} %slice_select_fusion.1, ...), kind=kOutput, calls=%fused_computation.2 | convolution fusion | flops 13369344 | bytes 3496448 | tf_op jit(solution)/shard_map/dot_general | solution.py:164
  80.9 1.4 fusion.35
  82.3 1.3 pad_maximum_fusion.x_ref
  83.5 15.0 %shard_map.127 = f32[17,8,384]{2,1,0:T(8,128)} custom-call(f32[16,8,384]{2,1,0:T(8,128)} %pad_maximum_fusion.11.neg_rate_ref, f32[8,384]{1,0:T(8,128)} %pad_maximum_fusion.19.skip_ref, bf16[128,8,384]{2,1,0:T(8,128)(2,1)} %pad_maximum_fusion.x_ref, f32[128,8,384]{2,1,0:T(8,128)} %fusion.delta_ref, f32[128,8,16]{2,1,0:T(8,128)} %get-tuple-element.41.entry_ref, ...), custom_call_target="tpu_custom_call" | custom-call | tf_op jit(solution)/shard_map/pallas_call | solution.py:114
  98.6 1.1 fusion.37
  99.7 1.3 collective-permute-start.4
  101.0 4.6 %collective-permute-start.6 = (f32[17,4,384]{2,1,0:T(4,128)S(1)}, f32[17,4,384]{2,1,0:T(4,128)S(1)}, u32[]{:S(2)}, u32[]{:S(2)}) collective-permute-start(f32[17,4,384]{2,1,0:T(4,128)S(1)} %get-tuple-element.57), channel_id=1, source_target_pairs={{8,0},{16,8},{24,16},{9,1},{17,9},{25,17},{10,2},{18,10},{26,18},{... | collective-permute-start | bytes 313352 | tf_op jit(solution)/shard_map/ppermute | solution.py:134
  106.3 1.1 multiply_add_fusion
  107.4 1.3 collective-permute-start.13
  108.9 4.2 %collective-permute-start.7 = (f32[17,4,384]{2,1,0:T(4,128)S(1)}, f32[17,4,384]{2,1,0:T(4,128)S(1)}, u32[]{:S(2)}, u32[]{:S(2)}) collective-permute-start(f32[17,4,384]{2,1,0:T(4,128)S(1)} %pad_maximum_fusion.13), channel_id=1, source_target_pairs={{16,0},{24,8},{17,1},{25,9},{18,2},{26,10},{19,3},{27,11},{20,4},{... | collective-permute-start | bytes 313352 | tf_op jit(solution)/shard_map/ppermute | solution.py:134
  113.2 1.3 collective-permute-start.5
  114.6 0.8 collective-permute-done.7
  115.4 5.8 %collective-permute-done.5 = f32[17,4,384]{2,1,0:T(4,128)S(1)} collective-permute-done((f32[17,4,384]{2,1,0:T(4,128)S(1)}, f32[17,4,384]{2,1,0:T(4,128)S(1)}, u32[]{:S(2)}, u32[]{:S(2)}) %collective-permute-start.5) | collective-permute-done | bytes 104480 | tf_op jit(solution)/shard_map/ppermute | solution.py:134
  122.0 19.1 %shard_map.128 = (f32[128,8,384]{2,1,0:T(8,128)}, f32[17,8,384]{2,1,0:T(8,128)}) custom-call(f32[16,8,384]{2,1,0:T(8,128)} %pad_maximum_fusion.11.neg_rate_ref, f32[8,384]{1,0:T(8,128)} %pad_maximum_fusion.19.skip_ref, bf16[128,8,384]{2,1,0:T(8,128)(2,1)} %pad_maximum_fusion.x_ref, f32[128,8,384]{2,1,0:T(8,128)} %fusion.delta_ref, ...), custom_call_target="tpu_custom_call" | custom-call | tf_op jit(solution)/shard_map/pallas_call | solution.py:114
  141.1 1.7 slice.367
  143.0 1.1 reverse_add_fusion
  144.1 3.5 %all-to-all-start.1 = ((f32[128,4,384]{2,1,0:T(4,128)}), f32[128,4,384]{2,1,0:T(4,128)S(1)}, u32[]{:S(2)}, u32[]{:S(2)}) async-start(f32[128,4,384]{2,1,0:T(4,128)} %reverse_add_fusion), calls=%async_computation.1 | async-start | bytes 1572864 | tf_op jit(solution)/shard_map/all_to_all | solution.py:232
  148.4 6.7 %collective-permute-start.10 = (f32[17,16,384]{2,1,0:T(8,128)}, f32[17,16,384]{2,1,0:T(8,128)}, u32[]{:S(2)}, u32[]{:S(2)}) collective-permute-start(f32[17,16,384]{2,1,0:T(8,128)} %pad_maximum_fusion.6), channel_id=1, source_target_pairs={{0,128},{32,160},{64,192},{96,224},{1,129},{33,161},{65,193},{97,2... | collective-permute-start | bytes 1253384 | tf_op jit(solution)/shard_map/ppermute | solution.py:134
  156.0 5.5 %collective-permute-done.10 = f32[17,16,384]{2,1,0:T(8,128)} collective-permute-done((f32[17,16,384]{2,1,0:T(8,128)}, f32[17,16,384]{2,1,0:T(8,128)}, u32[]{:S(2)}, u32[]{:S(2)}) %collective-permute-start.10) | collective-permute-done | bytes 417824 | tf_op jit(solution)/shard_map/ppermute | solution.py:134
  162.3 1.4 fusion.14
  163.6 1.3 fusion.15
  164.9 1.0 maximum_maximum_fusion.rest_0_
  165.9 11.8 %shard_map.130 = (f32[32,32,384]{2,1,0:T(8,128)}, f32[17,32,384]{2,1,0:T(8,128)}) custom-call(f32[16,32,384]{2,1,0:T(8,128)} %pad_maximum_fusion.1.neg_rate_ref, f32[32,384]{1,0:T(8,128)} %pad_maximum_fusion.17.skip_ref, bf16[32,32,384]{2,1,0:T(8,128)(2,1)} %pad_maximum_fusion.2.x_ref, f32[32,32,384]{2,1,0:T(8,128)} %fusion.1.delta_ref, ...), custom_call_target="tpu_custom_call" | custom-call | tf_op jit(solution)/shard_map/pallas_call | solution.py:114
  177.7 1.2 slice.402
  179.0 1.3 copy-done.4
  181.5 1.2 fusion.3
  (129 shorter events, 17.8 us)
Async XLA Ops:
  0.0 3.6 %copy-start = (bf16[192,768]{1,0:T(8,128)(2,1)S(1)}, bf16[192,768]{1,0:T(8,128)(2,1)}, u32[]{:S(2)}) copy-start(bf16[192,768]{1,0:T(8,128)(2,1)} %param.16) | copy-start | bytes 884740
  0.0 8.4 %copy-start.8 = (f32[4,384,16]{1,2,0:T(8,128)S(1)}, f32[4,384,16]{1,2,0:T(8,128)}, u32[]{:S(2)}) copy-start(f32[4,384,16]{1,2,0:T(8,128)} %param.22) | copy-start | bytes 294916
  0.0 8.4 %copy-start.13 = (f32[4,384]{1,0:T(4,128)S(1)}, f32[4,384]{1,0:T(4,128)}, u32[]{:S(2)}) copy-start(f32[4,384]{1,0:T(4,128)} %param.23) | copy-start | bytes 18436
  0.0 8.4 %copy-start.10 = (bf16[3,3,384]{2,1,0:T(4,128)(2,1)S(1)}, bf16[3,3,384]{2,1,0:T(4,128)(2,1)}, u32[]{:S(2)}) copy-start(bf16[3,3,384]{2,1,0:T(4,128)(2,1)} %param.17) | copy-start | bytes 20740
  0.0 8.5 %copy-start.6 = (bf16[4,384,44]{1,0,2:T(4,128)(2,1)S(1)}, bf16[4,384,44]{1,0,2:T(4,128)(2,1)}, u32[]{:S(2)}) copy-start(bf16[4,384,44]{1,0,2:T(4,128)(2,1)} %param.19) | copy-start | bytes 405508
  1.2 7.5 %copy-start.7 = (bf16[4,12,384]{2,0,1:T(4,128)(2,1)S(1)}, bf16[4,12,384]{2,0,1:T(4,128)(2,1)}, u32[]{:S(2)}) copy-start(bf16[4,12,384]{2,0,1:T(4,128)(2,1)} %param.20) | copy-start | bytes 110596
  1.2 8.2 %copy-start.12 = (s32[32,16]{0,1:T(8,128)S(1)}, s32[32,16]{0,1:T(8,128)}, u32[]{:S(2)}) copy-start(s32[32,16]{0,1:T(8,128)} %param.14) | copy-start | bytes 6148
  1.2 8.2 %copy-start.14 = (f32[4,384]{1,0:T(4,128)S(1)}, f32[4,384]{1,0:T(4,128)}, u32[]{:S(2)}) copy-start(f32[4,384]{1,0:T(4,128)} %param.21) | copy-start | bytes 18436
  4.0 9.2 %collective-permute-start.1 = (bf16[1,16,384]{2,1,0:T(8,128)(2,1)S(1)}, bf16[1,16,384]{2,1,0:T(8,128)(2,1)S(1)}, u32[]{:S(2)}, u32[]{:S(2)}) collective-permute-start(bf16[1,16,384]{2,1,0:T(8,128)(2,1)S(1)} %get-tuple-element.39), channel_id=1, source_target_pairs={{32,0},{64,32},{96,64},{128,96},{160,128},{192,160},{224,192},{33,... | collective-permute-start | bytes 36872 | tf_op jit(solution)/shard_map/ppermute | solution.py:18
  5.9 7.3 %collective-permute-start = (bf16[1,16,384]{2,1,0:T(8,128)(2,1)S(1)}, bf16[1,16,384]{2,1,0:T(8,128)(2,1)S(1)}, u32[]{:S(2)}, u32[]{:S(2)}) collective-permute-start(bf16[1,16,384]{2,1,0:T(8,128)(2,1)S(1)} %get-tuple-element.38), channel_id=1, source_target_pairs={{0,32},{32,64},{64,96},{96,128},{128,160},{160,192},{192,224},{1,3... | collective-permute-start | bytes 36872 | tf_op jit(solution)/shard_map/ppermute | solution.py:15
  13.2 12.4 %copy-start.15 = (f32[384]{0:T(512)S(1)}, f32[384]{0:T(512)}, u32[]{:S(2)}) copy-start(f32[384]{0:T(512)} %param.18) | copy-start | bytes 4612
  13.3 10.2 %collective-permute-start.2 = (bf16[34,1,384]{2,1,0:T(2,128)(2,1)S(1)}, bf16[34,1,384]{2,1,0:T(2,128)(2,1)S(1)}, u32[]{:S(2)}, u32[]{:S(2)}) collective-permute-start(bf16[34,1,384]{2,1,0:T(2,128)(2,1)S(1)} %get-tuple-element.48), channel_id=1, source_target_pairs={{0,1},{1,2},{2,3},{3,4},{4,5},{5,6},{6,7},{7,8},{8,9},{9,10},{10,1... | collective-permute-start | bytes 78344 | tf_op jit(solution)/shard_map/ppermute | solution.py:15
  17.2 8.1 %collective-permute-start.3 = (bf16[34,1,384]{2,1,0:T(2,128)(2,1)S(1)}, bf16[34,1,384]{2,1,0:T(2,128)(2,1)S(1)}, u32[]{:S(2)}, u32[]{:S(2)}) collective-permute-start(bf16[34,1,384]{2,1,0:T(2,128)(2,1)S(1)} %get-tuple-element.49), channel_id=1, source_target_pairs={{1,0},{2,1},{3,2},{4,3},{5,4},{6,5},{7,6},{8,7},{9,8},{10,9},{11,1... | collective-permute-start | bytes 78344 | tf_op jit(solution)/shard_map/ppermute | solution.py:18
  42.7 13.3 %copy-start.1 = (f32[17,32,384]{2,1,0:T(8,128)S(1)}, f32[17,32,384]{2,1,0:T(8,128)}, u32[]{:S(2)}) copy-start(f32[17,32,384]{2,1,0:T(8,128)} %shard_map.129) | copy-start | bytes 2506756
  42.7 13.3 %collective-permute-start.11 = (f32[17,16,384]{2,1,0:T(8,128)}, f32[17,16,384]{2,1,0:T(8,128)}, u32[]{:S(2)}, u32[]{:S(2)}) collective-permute-start(f32[17,16,384]{2,1,0:T(8,128)} %get-tuple-element.35), channel_id=1, source_target_pairs={{32,0},{64,32},{96,64},{128,96},{160,128},{192,160},{224,192},{33,... | collective-permute-start | bytes 1253384 | tf_op jit(solution)/shard_map/ppermute | solution.py:134
  45.2 10.9 %collective-permute-start.8 = (f32[17,16,384]{2,1,0:T(8,128)}, f32[17,16,384]{2,1,0:T(8,128)}, u32[]{:S(2)}, u32[]{:S(2)}) collective-permute-start(f32[17,16,384]{2,1,0:T(8,128)} %get-tuple-element.34), channel_id=1, source_target_pairs={{0,32},{32,64},{64,96},{96,128},{128,160},{160,192},{192,224},{1,3... | collective-permute-start | bytes 1253384 | tf_op jit(solution)/shard_map/ppermute | solution.py:134
  49.3 27.1 %all-to-all-start = ((bf16[32,17,384]{2,1,0:T(8,128)(2,1)}), bf16[32,17,384]{2,1,0:T(8,128)(2,1)S(1)}, u32[]{:S(2)}, u32[]{:S(2)}) async-start(bf16[32,17,384]{2,1,0:T(8,128)(2,1)} %pad_maximum_fusion.4), calls=%async_computation | async-start | bytes 1179648 | tf_op jit(solution)/shard_map/all_to_all | solution.py:224
  58.9 46.7 %collective-permute-start.12 = (f32[17,16,384]{2,1,0:T(8,128)}, f32[17,16,384]{2,1,0:T(8,128)}, u32[]{:S(2)}, u32[]{:S(2)}) collective-permute-start(f32[17,16,384]{2,1,0:T(8,128)} %pad_maximum_fusion.7), channel_id=1, source_target_pairs={{64,0},{96,32},{128,64},{160,96},{192,128},{224,160},{65,1},{97,33... | collective-permute-start | bytes 1253384 | tf_op jit(solution)/shard_map/ppermute | solution.py:134
  62.8 51.7 %collective-permute-start.9 = (f32[17,16,384]{2,1,0:T(8,128)}, f32[17,16,384]{2,1,0:T(8,128)S(1)}, u32[]{:S(2)}, u32[]{:S(2)}) collective-permute-start(f32[17,16,384]{2,1,0:T(8,128)} %pad_maximum_fusion.5), channel_id=1, source_target_pairs={{0,64},{32,96},{64,128},{96,160},{128,192},{160,224},{1,65},{33,97... | collective-permute-start | bytes 1253384 | tf_op jit(solution)/shard_map/ppermute | solution.py:134
  76.5 0.8 copy-start.9
  76.6 1.2 copy-start.18
  77.8 0.7 copy-start.11
  77.8 0.7 copy-start.16
  77.8 0.7 copy-start.17
  98.6 10.2 %copy-start.3 = (f32[17,8,384]{2,1,0:T(8,128)S(1)}, f32[17,8,384]{2,1,0:T(8,128)}, u32[]{:S(2)}) copy-start(f32[17,8,384]{2,1,0:T(8,128)} %shard_map.127) | copy-start | bytes 626692
  99.7 9.0 %collective-permute-start.4 = (f32[17,4,384]{2,1,0:T(4,128)S(1)}, f32[17,4,384]{2,1,0:T(4,128)S(1)}, u32[]{:S(2)}, u32[]{:S(2)}) collective-permute-start(f32[17,4,384]{2,1,0:T(4,128)S(1)} %get-tuple-element.56), channel_id=1, source_target_pairs={{0,8},{8,16},{16,24},{1,9},{9,17},{17,25},{2,10},{10,18},{18,26},{... | collective-permute-start | bytes 313352 | tf_op jit(solution)/shard_map/ppermute | solution.py:134
  101.0 7.7 %collective-permute-start.6 = (f32[17,4,384]{2,1,0:T(4,128)S(1)}, f32[17,4,384]{2,1,0:T(4,128)S(1)}, u32[]{:S(2)}, u32[]{:S(2)}) collective-permute-start(f32[17,4,384]{2,1,0:T(4,128)S(1)} %get-tuple-element.57), channel_id=1, source_target_pairs={{8,0},{16,8},{24,16},{9,1},{17,9},{25,17},{10,2},{18,10},{26,18},{... | collective-permute-start | bytes 313352 | tf_op jit(solution)/shard_map/ppermute | solution.py:134
  107.4 47.8 %collective-permute-start.13 = (f32[17,16,384]{2,1,0:T(8,128)S(1)}, f32[17,16,384]{2,1,0:T(8,128)}, u32[]{:S(2)}, u32[]{:S(2)}) collective-permute-start(f32[17,16,384]{2,1,0:T(8,128)S(1)} %pad_maximum_fusion.8), channel_id=1, source_target_pairs={{128,0},{160,32},{192,64},{224,96},{129,1},{161,33},{193,65},{225,... | collective-permute-start | bytes 1253384 | tf_op jit(solution)/shard_map/ppermute | solution.py:134
  108.9 6.5 %collective-permute-start.7 = (f32[17,4,384]{2,1,0:T(4,128)S(1)}, f32[17,4,384]{2,1,0:T(4,128)S(1)}, u32[]{:S(2)}, u32[]{:S(2)}) collective-permute-start(f32[17,4,384]{2,1,0:T(4,128)S(1)} %pad_maximum_fusion.13), channel_id=1, source_target_pairs={{16,0},{24,8},{17,1},{25,9},{18,2},{26,10},{19,3},{27,11},{20,4},{... | collective-permute-start | bytes 313352 | tf_op jit(solution)/shard_map/ppermute | solution.py:134
  113.2 8.1 %collective-permute-start.5 = (f32[17,4,384]{2,1,0:T(4,128)S(1)}, f32[17,4,384]{2,1,0:T(4,128)S(1)}, u32[]{:S(2)}, u32[]{:S(2)}) collective-permute-start(f32[17,4,384]{2,1,0:T(4,128)S(1)} %pad_maximum_fusion.12), channel_id=1, source_target_pairs={{0,16},{8,24},{1,17},{9,25},{2,18},{10,26},{3,19},{11,27},{4,20},{... | collective-permute-start | bytes 313352 | tf_op jit(solution)/shard_map/ppermute | solution.py:134
  141.1 1.9 %copy-start.5 = (f32[128,8,384]{2,1,0:T(8,128)S(1)}, f32[128,8,384]{2,1,0:T(8,128)}, u32[]{:S(2)}) copy-start(f32[128,8,384]{2,1,0:T(8,128)} %get-tuple-element.7) | copy-start | bytes 4718596
  144.1 34.8 %all-to-all-start.1 = ((f32[128,4,384]{2,1,0:T(4,128)}), f32[128,4,384]{2,1,0:T(4,128)S(1)}, u32[]{:S(2)}, u32[]{:S(2)}) async-start(f32[128,4,384]{2,1,0:T(4,128)} %reverse_add_fusion), calls=%async_computation.1 | async-start | bytes 1572864 | tf_op jit(solution)/shard_map/all_to_all | solution.py:232
  148.4 13.1 %collective-permute-start.10 = (f32[17,16,384]{2,1,0:T(8,128)}, f32[17,16,384]{2,1,0:T(8,128)}, u32[]{:S(2)}, u32[]{:S(2)}) collective-permute-start(f32[17,16,384]{2,1,0:T(8,128)} %pad_maximum_fusion.6), channel_id=1, source_target_pairs={{0,128},{32,160},{64,192},{96,224},{1,129},{33,161},{65,193},{97,2... | collective-permute-start | bytes 1253384 | tf_op jit(solution)/shard_map/ppermute | solution.py:134
  178.9 1.4 copy-start.4
  180.5 1.0 copy-start.2
  180.5 1.0 copy-start.19
  180.5 1.0 copy-start.20

commit v4 on v3

--- a/solution.py
+++ b/solution.py
@@ -69,12 +69,22 @@
     y_ref = rest.pop(0) if with_y else None
     state_ref = rest.pop(0)
     nstate = neg_rate_ref.shape[0]
-    if with_init:
-        state_ref[...] = init_ref[...]
+    slab = state_ref.shape[1:]
+    in_registers = slab[0] <= 8
+    if in_registers:
+        if with_init:
+            start = tuple(init_ref[n] for n in range(nstate))
+        else:
+            start = tuple(jnp.zeros(slab, jnp.float32) for _ in range(nstate))
     else:
-        state_ref[...] = jnp.zeros(state_ref.shape, state_ref.dtype)
-
-    def step(i, summed):
+        start = ()
+        if with_init:
+            state_ref[...] = init_ref[...]
+        else:
+            state_ref[...] = jnp.zeros(state_ref.shape, state_ref.dtype)
+
+    def step(i, carry):
+        summed, states = carry
         t = length - 1 - i if reverse else i
         delta = delta_ref[t]
         x_wide = x_ref[t].astype(jnp.float32)
@@ -82,19 +92,25 @@
         entry = entry_ref[t]
         readout = readout_ref[t]
         total = jnp.zeros_like(delta)
+        kept = []
         for n in range(nstate):
-            state = (
-                jnp.exp(delta * neg_rate_ref[n]) * state_ref[n]
-                + drive * entry[:, n : n + 1]
-            )
-            state_ref[n] = state
+            before = states[n] if in_registers else state_ref[n]
+            state = jnp.exp(delta * neg_rate_ref[n]) * before + drive * entry[:, n : n + 1]
+            if in_registers:
+                kept.append(state)
+            else:
+                state_ref[n] = state
             if with_y:
                 total = total + readout[:, n : n + 1] * state
         if with_y:
             y_ref[t] = total + skip_ref[...] * x_wide
-        return summed + delta
-
-    summed = lax.fori_loop(0, length, step, jnp.zeros(state_ref.shape[1:], jnp.float32))
+        return (summed + delta, tuple(kept))
+
+    summed, states = lax.fori_loop(
+        0, length, step, (jnp.zeros(slab, jnp.float32), start), unroll=4 if in_registers else 2
+    )
+    for n, state in enumerate(states):
+        state_ref[n] = state
     state_ref[nstate] = summed
 
 

time: 186 us -> 173 us (0.930)
  Pallas kernels: 54.5 us -> 41.6 us
    pallas_call x4, Pallas kernels: 54.5 us -> 41.6 us  [run_scan(): return pl.pallas_call(kernel, out_shape=tuple(out_shape))(*args)]
  transfers between devices with their start and end apart: 16 -> 16, of which waited for: 5 -> 5; matrix products, arithmetic and copies ran while one was open for 17% -> 19% of each run, Pallas kernels for 25% -> 20%
where the time goes in v4:
time: 173 us; the launch traced here: 170 us
  starting transfers between devices  54.4 us (31%)
  Pallas kernels  41.6 us (24%)
  other arithmetic  26 us (15%)
  waiting for transfers between devices  24.6 us (14%)
  local copies, waits for them, and re-layouts  14.7 us (8%)
  matrix products  7.71 us (4%)
    pallas_call x4, Pallas kernels, run_scan(): return pl.pallas_call(kernel, out_shape=tuple(out_shape))(*args)  41.6 us
    ppermute x10, starting transfers between devices, carried_in(): got = lax.ppermute(inclusive, axis, pairs)  29.8 us
    ppermute x10, waiting for transfers between devices, carried_in(): got = lax.ppermute(inclusive, axis, pairs)  12 us
    all_to_all x1, waiting for transfers between devices, local(): band = lax.all_to_all(sent, 'cz', 0, 1, tiled=True)  10.9 us
    ppermute x2, starting transfers between devices, padded_2(): lax.ppermute(lax.slice_in_dim(block, 0, width, axis=dim), axis, backward)  8.05 us
    all_to_all x1, starting transfers between devices, local(): band = lax.all_to_all(sent, 'cz', 0, 1, tiled=True)  6.76 us
    ppermute x2, starting transfers between devices, padded_2(): lax.ppermute(lax.slice_in_dim(block, block.shape[dim] - width, None, axis...  6.23 us
    add x8, other arithmetic, combine(): state = decay * earlier[:nstate] + later[:nstate]  5.23 us
  transfers between devices with their start and end apart: 16, of which 5 were waited for; matrix products, arithmetic and copies ran while one was open for 19% of the time, Pallas kernels for 20%

profile of v4, /device:TPU:14, one launch (start us, length us, event | category | flops | bytes accessed | tf_op | source)
XLA Modules:
  0.0 169.7 jit_solution(15871735126510862978)
XLA Ops:
  0.0 1.1 convert_reduce_fusion
  1.2 1.2 fusion.11
  2.5 1.2 fusion.13
  4.0 1.9 %collective-permute-start.1 = (bf16[1,16,384]{2,1,0:T(8,128)(2,1)S(1)}, bf16[1,16,384]{2,1,0:T(8,128)(2,1)S(1)}, u32[]{:S(2)}, u32[]{:S(2)}) collective-permute-start(bf16[1,16,384]{2,1,0:T(8,128)(2,1)S(1)} %get-tuple-element.39), channel_id=1, source_target_pairs={{32,0},{64,32},{96,64},{128,96},{160,128},{192,160},{224,192},{33,... | collective-permute-start | bytes 36872 | tf_op jit(solution)/shard_map/ppermute | solution.py:18
  5.9 2.4 %collective-permute-start = (bf16[1,16,384]{2,1,0:T(8,128)(2,1)S(1)}, bf16[1,16,384]{2,1,0:T(8,128)(2,1)S(1)}, u32[]{:S(2)}, u32[]{:S(2)}) collective-permute-start(bf16[1,16,384]{2,1,0:T(8,128)(2,1)S(1)} %get-tuple-element.38), channel_id=1, source_target_pairs={{0,32},{32,64},{64,96},{96,128},{128,160},{160,192},{192,224},{1,3... | collective-permute-start | bytes 36872 | tf_op jit(solution)/shard_map/ppermute | solution.py:15
  10.2 1.0 pad_maximum_fusion.1.neg_rate_ref
  13.3 3.8 %collective-permute-start.2 = (bf16[34,1,384]{2,1,0:T(2,128)(2,1)S(1)}, bf16[34,1,384]{2,1,0:T(2,128)(2,1)S(1)}, u32[]{:S(2)}, u32[]{:S(2)}) collective-permute-start(bf16[34,1,384]{2,1,0:T(2,128)(2,1)S(1)} %get-tuple-element.48), channel_id=1, source_target_pairs={{0,1},{1,2},{2,3},{3,4},{4,5},{5,6},{6,7},{7,8},{8,9},{9,10},{10,1... | collective-permute-start | bytes 78344 | tf_op jit(solution)/shard_map/ppermute | solution.py:15
  17.2 6.1 %collective-permute-start.3 = (bf16[34,1,384]{2,1,0:T(2,128)(2,1)S(1)}, bf16[34,1,384]{2,1,0:T(2,128)(2,1)S(1)}, u32[]{:S(2)}, u32[]{:S(2)}) collective-permute-start(bf16[34,1,384]{2,1,0:T(2,128)(2,1)S(1)} %get-tuple-element.49), channel_id=1, source_target_pairs={{1,0},{2,1},{3,2},{4,3},{5,4},{6,5},{7,6},{8,7},{9,8},{10,9},{11,1... | collective-permute-start | bytes 78344 | tf_op jit(solution)/shard_map/ppermute | solution.py:18
  23.6 1.7 %collective-permute-done.3 = bf16[34,1,384]{2,1,0:T(2,128)(2,1)S(1)} collective-permute-done((bf16[34,1,384]{2,1,0:T(2,128)(2,1)S(1)}, bf16[34,1,384]{2,1,0:T(2,128)(2,1)S(1)}, u32[]{:S(2)}, u32[]{:S(2)}) %collective-permute-start.3) | collective-permute-done | bytes 26144 | tf_op jit(solution)/shard_map/ppermute | solution.py:18
  26.5 1.0 pad_maximum_fusion.2.x_ref
  28.0 1.3 fusion.36
  29.6 2.3 %fusion.1.delta_ref = f32[32,32,384]{2,1,0:T(8,128)} fusion(f32[32,32,384]{2,1,0:T(8,128)S(1)} %fusion.19, f32[32,32]{1,0:T(8,128)S(1)} %copy.82, f32[384]{0:T(512)S(1)} %get-tuple-element.20, f32[384]{0:T(512)S(1)} %get-tuple-element.21, pred[32]{0:T(512)(128)(4,1)S(1)} %iota_compare_fusion, f32[32,32,44]{2,1,0:T(8,128)S(1)} %slice_select_fusion, ...), kind=kOutput, calls=%fused_computation.3 | convolution fusion | flops 13369344 | bytes 3447296 | tf_op jit(solution)/shard_map/dot_general | solution.py:180
  32.0 8.5 %shard_map.129 = f32[17,32,384]{2,1,0:T(8,128)} custom-call(f32[16,32,384]{2,1,0:T(8,128)} %pad_maximum_fusion.1.neg_rate_ref, f32[32,384]{1,0:T(8,128)} %pad_maximum_fusion.17.skip_ref, bf16[32,32,384]{2,1,0:T(8,128)(2,1)} %pad_maximum_fusion.2.x_ref, f32[32,32,384]{2,1,0:T(8,128)} %fusion.1.delta_ref, f32[32,32,16]{2,1,0:T(8,128)} %get-tuple-element.43.entry_ref, ...), custom_call_target="tpu_custom_call" | custom-call | tf_op jit(solution)/shard_map/pallas_call | solution.py:130
  40.4 2.2 %fusion.33 = (f32[17,16,384]{2,1,0:T(8,128)}, f32[17,16,384]{2,1,0:T(8,128)}) fusion(f32[17,32,384]{2,1,0:T(8,128)} %shard_map.129), kind=kLoop, calls=%fused_computation.142 | loop fusion | bytes 1671168 | tf_op jit(solution)/shard_map/slice | solution.py:203
  42.6 2.4 %collective-permute-start.11 = (f32[17,16,384]{2,1,0:T(8,128)}, f32[17,16,384]{2,1,0:T(8,128)}, u32[]{:S(2)}, u32[]{:S(2)}) collective-permute-start(f32[17,16,384]{2,1,0:T(8,128)} %get-tuple-element.35), channel_id=1, source_target_pairs={{32,0},{64,32},{96,64},{128,96},{160,128},{192,160},{224,192},{33,... | collective-permute-start | bytes 1253384 | tf_op jit(solution)/shard_map/ppermute | solution.py:150
  45.0 2.0 %collective-permute-start.8 = (f32[17,16,384]{2,1,0:T(8,128)}, f32[17,16,384]{2,1,0:T(8,128)}, u32[]{:S(2)}, u32[]{:S(2)}) collective-permute-start(f32[17,16,384]{2,1,0:T(8,128)} %get-tuple-element.34), channel_id=1, source_target_pairs={{0,32},{32,64},{64,96},{96,128},{128,160},{160,192},{192,224},{1,3... | collective-permute-start | bytes 1253384 | tf_op jit(solution)/shard_map/ppermute | solution.py:150
  48.2 0.9 pad_maximum_fusion.4
  49.1 6.8 %all-to-all-start = ((bf16[32,17,384]{2,1,0:T(8,128)(2,1)}), bf16[32,17,384]{2,1,0:T(8,128)(2,1)S(1)}, u32[]{:S(2)}, u32[]{:S(2)}) async-start(bf16[32,17,384]{2,1,0:T(8,128)(2,1)} %pad_maximum_fusion.4), calls=%async_computation | async-start | bytes 1179648 | tf_op jit(solution)/shard_map/all_to_all | solution.py:240
  56.7 1.3 slice_add_fusion.1
  58.7 3.1 %collective-permute-start.12 = (f32[17,16,384]{2,1,0:T(8,128)}, f32[17,16,384]{2,1,0:T(8,128)}, u32[]{:S(2)}, u32[]{:S(2)}) collective-permute-start(f32[17,16,384]{2,1,0:T(8,128)} %pad_maximum_fusion.7), channel_id=1, source_target_pairs={{64,0},{96,32},{128,64},{160,96},{192,128},{224,160},{65,1},{97,33... | collective-permute-start | bytes 1253384 | tf_op jit(solution)/shard_map/ppermute | solution.py:150
  62.6 2.7 %collective-permute-start.9 = (f32[17,16,384]{2,1,0:T(8,128)}, f32[17,16,384]{2,1,0:T(8,128)S(1)}, u32[]{:S(2)}, u32[]{:S(2)}) collective-permute-start(f32[17,16,384]{2,1,0:T(8,128)} %pad_maximum_fusion.5), channel_id=1, source_target_pairs={{0,64},{32,96},{64,128},{96,160},{128,192},{160,224},{1,65},{33,97... | collective-permute-start | bytes 1253384 | tf_op jit(solution)/shard_map/ppermute | solution.py:150
  65.3 10.9 %all-to-all-done = bf16[32,17,384]{2,1,0:T(8,128)(2,1)S(1)} async-done(((bf16[32,17,384]{2,1,0:T(8,128)(2,1)}), bf16[32,17,384]{2,1,0:T(8,128)(2,1)S(1)}, u32[]{:S(2)}, u32[]{:S(2)}) %all-to-all-start) | async-done | bytes 417824 | tf_op jit(solution)/shard_map/all_to_all | solution.py:240
  78.4 2.3 %fusion.delta_ref = f32[128,8,384]{2,1,0:T(8,128)} fusion(f32[128,8,384]{2,1,0:T(8,128)S(1)} %fusion.18, f32[128,8]{1,0:T(8,128)S(1)} %copy.74, f32[384]{0:T(512)S(1)} %copy-done.17, f32[384]{0:T(512)S(1)} %copy-done.16, pred[8]{0:T(512)(128)(4,1)S(1)} %copy-done.18, f32[128,8,44]{2,1,0:T(8,128)S(1)} %slice_select_fusion.1, ...), kind=kOutput, calls=%fused_computation.2 | convolution fusion | flops 13369344 | bytes 3496448 | tf_op jit(solution)/shard_map/dot_general | solution.py:180
  80.7 1.4 fusion.35
  82.1 1.3 pad_maximum_fusion.x_ref
  83.4 8.7 %shard_map.127 = f32[17,8,384]{2,1,0:T(8,128)} custom-call(f32[16,8,384]{2,1,0:T(8,128)} %pad_maximum_fusion.11.neg_rate_ref, f32[8,384]{1,0:T(8,128)} %pad_maximum_fusion.19.skip_ref, bf16[128,8,384]{2,1,0:T(8,128)(2,1)} %pad_maximum_fusion.x_ref, f32[128,8,384]{2,1,0:T(8,128)} %fusion.delta_ref, f32[128,8,16]{2,1,0:T(8,128)} %get-tuple-element.41.entry_ref, ...), custom_call_target="tpu_custom_call" | custom-call | tf_op jit(solution)/shard_map/pallas_call | solution.py:130
  92.1 1.1 fusion.37
  93.2 1.3 collective-permute-start.4
  94.5 4.6 %collective-permute-start.6 = (f32[17,4,384]{2,1,0:T(4,128)S(1)}, f32[17,4,384]{2,1,0:T(4,128)S(1)}, u32[]{:S(2)}, u32[]{:S(2)}) collective-permute-start(f32[17,4,384]{2,1,0:T(4,128)S(1)} %get-tuple-element.57), channel_id=1, source_target_pairs={{8,0},{16,8},{24,16},{9,1},{17,9},{25,17},{10,2},{18,10},{26,18},{... | collective-permute-start | bytes 313352 | tf_op jit(solution)/shard_map/ppermute | solution.py:150
  99.9 1.1 multiply_add_fusion
  101.0 1.3 collective-permute-start.13
  102.4 4.2 %collective-permute-start.7 = (f32[17,4,384]{2,1,0:T(4,128)S(1)}, f32[17,4,384]{2,1,0:T(4,128)S(1)}, u32[]{:S(2)}, u32[]{:S(2)}) collective-permute-start(f32[17,4,384]{2,1,0:T(4,128)S(1)} %pad_maximum_fusion.13), channel_id=1, source_target_pairs={{16,0},{24,8},{17,1},{25,9},{18,2},{26,10},{19,3},{27,11},{20,4},{... | collective-permute-start | bytes 313352 | tf_op jit(solution)/shard_map/ppermute | solution.py:150
  106.7 1.5 collective-permute-start.5
  109.0 5.8 %collective-permute-done.5 = f32[17,4,384]{2,1,0:T(4,128)S(1)} collective-permute-done((f32[17,4,384]{2,1,0:T(4,128)S(1)}, f32[17,4,384]{2,1,0:T(4,128)S(1)}, u32[]{:S(2)}, u32[]{:S(2)}) %collective-permute-start.5) | collective-permute-done | bytes 104480 | tf_op jit(solution)/shard_map/ppermute | solution.py:150
  115.6 12.7 %shard_map.128 = (f32[128,8,384]{2,1,0:T(8,128)}, f32[17,8,384]{2,1,0:T(8,128)}) custom-call(f32[16,8,384]{2,1,0:T(8,128)} %pad_maximum_fusion.11.neg_rate_ref, f32[8,384]{1,0:T(8,128)} %pad_maximum_fusion.19.skip_ref, bf16[128,8,384]{2,1,0:T(8,128)(2,1)} %pad_maximum_fusion.x_ref, f32[128,8,384]{2,1,0:T(8,128)} %fusion.delta_ref, ...), custom_call_target="tpu_custom_call" | custom-call | tf_op jit(solution)/shard_map/pallas_call | solution.py:130
  128.3 1.7 slice.367
  130.2 1.1 reverse_add_fusion
  131.2 3.5 %all-to-all-start.1 = ((f32[128,4,384]{2,1,0:T(4,128)}), f32[128,4,384]{2,1,0:T(4,128)S(1)}, u32[]{:S(2)}, u32[]{:S(2)}) async-start(f32[128,4,384]{2,1,0:T(4,128)} %reverse_add_fusion), calls=%async_computation.1 | async-start | bytes 1572864 | tf_op jit(solution)/shard_map/all_to_all | solution.py:248
  134.8 0.8 pad_maximum_fusion.6
  135.6 6.7 %collective-permute-start.10 = (f32[17,16,384]{2,1,0:T(8,128)}, f32[17,16,384]{2,1,0:T(8,128)}, u32[]{:S(2)}, u32[]{:S(2)}) collective-permute-start(f32[17,16,384]{2,1,0:T(8,128)} %pad_maximum_fusion.6), channel_id=1, source_target_pairs={{0,128},{32,160},{64,192},{96,224},{1,129},{33,161},{65,193},{97,2... | collective-permute-start | bytes 1253384 | tf_op jit(solution)/shard_map/ppermute | solution.py:150
  143.2 5.5 %collective-permute-done.10 = f32[17,16,384]{2,1,0:T(8,128)} collective-permute-done((f32[17,16,384]{2,1,0:T(8,128)}, f32[17,16,384]{2,1,0:T(8,128)}, u32[]{:S(2)}, u32[]{:S(2)}) %collective-permute-start.10) | collective-permute-done | bytes 417824 | tf_op jit(solution)/shard_map/ppermute | solution.py:150
  149.5 1.4 fusion.14
  150.8 1.3 fusion.15
  152.1 1.0 maximum_maximum_fusion.rest_0_
  153.1 11.7 %shard_map.130 = (f32[32,32,384]{2,1,0:T(8,128)}, f32[17,32,384]{2,1,0:T(8,128)}) custom-call(f32[16,32,384]{2,1,0:T(8,128)} %pad_maximum_fusion.1.neg_rate_ref, f32[32,384]{1,0:T(8,128)} %pad_maximum_fusion.17.skip_ref, bf16[32,32,384]{2,1,0:T(8,128)(2,1)} %pad_maximum_fusion.2.x_ref, f32[32,32,384]{2,1,0:T(8,128)} %fusion.1.delta_ref, ...), custom_call_target="tpu_custom_call" | custom-call | tf_op jit(solution)/shard_map/pallas_call | solution.py:130
  164.8 1.2 slice.402
  166.1 1.3 copy-done.4
  168.5 1.2 fusion.3
  (129 shorter events, 17.6 us)
Async XLA Ops:
  0.0 3.6 %copy-start = (bf16[192,768]{1,0:T(8,128)(2,1)S(1)}, bf16[192,768]{1,0:T(8,128)(2,1)}, u32[]{:S(2)}) copy-start(bf16[192,768]{1,0:T(8,128)(2,1)} %param.16) | copy-start | bytes 884740
  0.0 8.4 %copy-start.8 = (f32[4,384,16]{1,2,0:T(8,128)S(1)}, f32[4,384,16]{1,2,0:T(8,128)}, u32[]{:S(2)}) copy-start(f32[4,384,16]{1,2,0:T(8,128)} %param.22) | copy-start | bytes 294916
  0.0 8.4 %copy-start.13 = (f32[4,384]{1,0:T(4,128)S(1)}, f32[4,384]{1,0:T(4,128)}, u32[]{:S(2)}) copy-start(f32[4,384]{1,0:T(4,128)} %param.23) | copy-start | bytes 18436
  0.0 8.4 %copy-start.10 = (bf16[3,3,384]{2,1,0:T(4,128)(2,1)S(1)}, bf16[3,3,384]{2,1,0:T(4,128)(2,1)}, u32[]{:S(2)}) copy-start(bf16[3,3,384]{2,1,0:T(4,128)(2,1)} %param.17) | copy-start | bytes 20740
  0.0 8.5 %copy-start.6 = (bf16[4,384,44]{1,0,2:T(4,128)(2,1)S(1)}, bf16[4,384,44]{1,0,2:T(4,128)(2,1)}, u32[]{:S(2)}) copy-start(bf16[4,384,44]{1,0,2:T(4,128)(2,1)} %param.19) | copy-start | bytes 405508
  1.2 7.5 %copy-start.7 = (bf16[4,12,384]{2,0,1:T(4,128)(2,1)S(1)}, bf16[4,12,384]{2,0,1:T(4,128)(2,1)}, u32[]{:S(2)}) copy-start(bf16[4,12,384]{2,0,1:T(4,128)(2,1)} %param.20) | copy-start | bytes 110596
  1.2 8.2 %copy-start.12 = (s32[32,16]{0,1:T(8,128)S(1)}, s32[32,16]{0,1:T(8,128)}, u32[]{:S(2)}) copy-start(s32[32,16]{0,1:T(8,128)} %param.14) | copy-start | bytes 6148
  1.2 8.2 %copy-start.14 = (f32[4,384]{1,0:T(4,128)S(1)}, f32[4,384]{1,0:T(4,128)}, u32[]{:S(2)}) copy-start(f32[4,384]{1,0:T(4,128)} %param.21) | copy-start | bytes 18436
  4.0 9.2 %collective-permute-start.1 = (bf16[1,16,384]{2,1,0:T(8,128)(2,1)S(1)}, bf16[1,16,384]{2,1,0:T(8,128)(2,1)S(1)}, u32[]{:S(2)}, u32[]{:S(2)}) collective-permute-start(bf16[1,16,384]{2,1,0:T(8,128)(2,1)S(1)} %get-tuple-element.39), channel_id=1, source_target_pairs={{32,0},{64,32},{96,64},{128,96},{160,128},{192,160},{224,192},{33,... | collective-permute-start | bytes 36872 | tf_op jit(solution)/shard_map/ppermute | solution.py:18
  5.9 7.3 %collective-permute-start = (bf16[1,16,384]{2,1,0:T(8,128)(2,1)S(1)}, bf16[1,16,384]{2,1,0:T(8,128)(2,1)S(1)}, u32[]{:S(2)}, u32[]{:S(2)}) collective-permute-start(bf16[1,16,384]{2,1,0:T(8,128)(2,1)S(1)} %get-tuple-element.38), channel_id=1, source_target_pairs={{0,32},{32,64},{64,96},{96,128},{128,160},{160,192},{192,224},{1,3... | collective-permute-start | bytes 36872 | tf_op jit(solution)/shard_map/ppermute | solution.py:15
  13.2 12.4 %copy-start.15 = (f32[384]{0:T(512)S(1)}, f32[384]{0:T(512)}, u32[]{:S(2)}) copy-start(f32[384]{0:T(512)} %param.18) | copy-start | bytes 4612
  13.3 10.2 %collective-permute-start.2 = (bf16[34,1,384]{2,1,0:T(2,128)(2,1)S(1)}, bf16[34,1,384]{2,1,0:T(2,128)(2,1)S(1)}, u32[]{:S(2)}, u32[]{:S(2)}) collective-permute-start(bf16[34,1,384]{2,1,0:T(2,128)(2,1)S(1)} %get-tuple-element.48), channel_id=1, source_target_pairs={{0,1},{1,2},{2,3},{3,4},{4,5},{5,6},{6,7},{7,8},{8,9},{9,10},{10,1... | collective-permute-start | bytes 78344 | tf_op jit(solution)/shard_map/ppermute | solution.py:15
  17.2 8.1 %collective-permute-start.3 = (bf16[34,1,384]{2,1,0:T(2,128)(2,1)S(1)}, bf16[34,1,384]{2,1,0:T(2,128)(2,1)S(1)}, u32[]{:S(2)}, u32[]{:S(2)}) collective-permute-start(bf16[34,1,384]{2,1,0:T(2,128)(2,1)S(1)} %get-tuple-element.49), channel_id=1, source_target_pairs={{1,0},{2,1},{3,2},{4,3},{5,4},{6,5},{7,6},{8,7},{9,8},{10,9},{11,1... | collective-permute-start | bytes 78344 | tf_op jit(solution)/shard_map/ppermute | solution.py:18
  42.6 13.3 %copy-start.1 = (f32[17,32,384]{2,1,0:T(8,128)S(1)}, f32[17,32,384]{2,1,0:T(8,128)}, u32[]{:S(2)}) copy-start(f32[17,32,384]{2,1,0:T(8,128)} %shard_map.129) | copy-start | bytes 2506756
  42.6 13.3 %collective-permute-start.11 = (f32[17,16,384]{2,1,0:T(8,128)}, f32[17,16,384]{2,1,0:T(8,128)}, u32[]{:S(2)}, u32[]{:S(2)}) collective-permute-start(f32[17,16,384]{2,1,0:T(8,128)} %get-tuple-element.35), channel_id=1, source_target_pairs={{32,0},{64,32},{96,64},{128,96},{160,128},{192,160},{224,192},{33,... | collective-permute-start | bytes 1253384 | tf_op jit(solution)/shard_map/ppermute | solution.py:150
  45.0 10.9 %collective-permute-start.8 = (f32[17,16,384]{2,1,0:T(8,128)}, f32[17,16,384]{2,1,0:T(8,128)}, u32[]{:S(2)}, u32[]{:S(2)}) collective-permute-start(f32[17,16,384]{2,1,0:T(8,128)} %get-tuple-element.34), channel_id=1, source_target_pairs={{0,32},{32,64},{64,96},{96,128},{128,160},{160,192},{192,224},{1,3... | collective-permute-start | bytes 1253384 | tf_op jit(solution)/shard_map/ppermute | solution.py:150
  49.1 27.1 %all-to-all-start = ((bf16[32,17,384]{2,1,0:T(8,128)(2,1)}), bf16[32,17,384]{2,1,0:T(8,128)(2,1)S(1)}, u32[]{:S(2)}, u32[]{:S(2)}) async-start(bf16[32,17,384]{2,1,0:T(8,128)(2,1)} %pad_maximum_fusion.4), calls=%async_computation | async-start | bytes 1179648 | tf_op jit(solution)/shard_map/all_to_all | solution.py:240
  58.7 40.4 %collective-permute-start.12 = (f32[17,16,384]{2,1,0:T(8,128)}, f32[17,16,384]{2,1,0:T(8,128)}, u32[]{:S(2)}, u32[]{:S(2)}) collective-permute-start(f32[17,16,384]{2,1,0:T(8,128)} %pad_maximum_fusion.7), channel_id=1, source_target_pairs={{64,0},{96,32},{128,64},{160,96},{192,128},{224,160},{65,1},{97,33... | collective-permute-start | bytes 1253384 | tf_op jit(solution)/shard_map/ppermute | solution.py:150
  62.6 45.6 %collective-permute-start.9 = (f32[17,16,384]{2,1,0:T(8,128)}, f32[17,16,384]{2,1,0:T(8,128)S(1)}, u32[]{:S(2)}, u32[]{:S(2)}) collective-permute-start(f32[17,16,384]{2,1,0:T(8,128)} %pad_maximum_fusion.5), channel_id=1, source_target_pairs={{0,64},{32,96},{64,128},{96,160},{128,192},{160,224},{1,65},{33,97... | collective-permute-start | bytes 1253384 | tf_op jit(solution)/shard_map/ppermute | solution.py:150
  76.4 0.8 copy-start.9
  76.5 1.2 copy-start.18
  77.7 0.7 copy-start.11
  77.7 0.7 copy-start.16
  77.7 0.7 copy-start.17
  92.1 10.2 %copy-start.3 = (f32[17,8,384]{2,1,0:T(8,128)S(1)}, f32[17,8,384]{2,1,0:T(8,128)}, u32[]{:S(2)}) copy-start(f32[17,8,384]{2,1,0:T(8,128)} %shard_map.127) | copy-start | bytes 626692
  93.2 9.0 %collective-permute-start.4 = (f32[17,4,384]{2,1,0:T(4,128)S(1)}, f32[17,4,384]{2,1,0:T(4,128)S(1)}, u32[]{:S(2)}, u32[]{:S(2)}) collective-permute-start(f32[17,4,384]{2,1,0:T(4,128)S(1)} %get-tuple-element.56), channel_id=1, source_target_pairs={{0,8},{8,16},{16,24},{1,9},{9,17},{17,25},{2,10},{10,18},{18,26},{... | collective-permute-start | bytes 313352 | tf_op jit(solution)/shard_map/ppermute | solution.py:150
  94.5 7.7 %collective-permute-start.6 = (f32[17,4,384]{2,1,0:T(4,128)S(1)}, f32[17,4,384]{2,1,0:T(4,128)S(1)}, u32[]{:S(2)}, u32[]{:S(2)}) collective-permute-start(f32[17,4,384]{2,1,0:T(4,128)S(1)} %get-tuple-element.57), channel_id=1, source_target_pairs={{8,0},{16,8},{24,16},{9,1},{17,9},{25,17},{10,2},{18,10},{26,18},{... | collective-permute-start | bytes 313352 | tf_op jit(solution)/shard_map/ppermute | solution.py:150
  101.0 41.4 %collective-permute-start.13 = (f32[17,16,384]{2,1,0:T(8,128)S(1)}, f32[17,16,384]{2,1,0:T(8,128)}, u32[]{:S(2)}, u32[]{:S(2)}) collective-permute-start(f32[17,16,384]{2,1,0:T(8,128)S(1)} %pad_maximum_fusion.8), channel_id=1, source_target_pairs={{128,0},{160,32},{192,64},{224,96},{129,1},{161,33},{193,65},{225,... | collective-permute-start | bytes 1253384 | tf_op jit(solution)/shard_map/ppermute | solution.py:150
  102.4 6.5 %collective-permute-start.7 = (f32[17,4,384]{2,1,0:T(4,128)S(1)}, f32[17,4,384]{2,1,0:T(4,128)S(1)}, u32[]{:S(2)}, u32[]{:S(2)}) collective-permute-start(f32[17,4,384]{2,1,0:T(4,128)S(1)} %pad_maximum_fusion.13), channel_id=1, source_target_pairs={{16,0},{24,8},{17,1},{25,9},{18,2},{26,10},{19,3},{27,11},{20,4},{... | collective-permute-start | bytes 313352 | tf_op jit(solution)/shard_map/ppermute | solution.py:150
  106.7 8.1 %collective-permute-start.5 = (f32[17,4,384]{2,1,0:T(4,128)S(1)}, f32[17,4,384]{2,1,0:T(4,128)S(1)}, u32[]{:S(2)}, u32[]{:S(2)}) collective-permute-start(f32[17,4,384]{2,1,0:T(4,128)S(1)} %pad_maximum_fusion.12), channel_id=1, source_target_pairs={{0,16},{8,24},{1,17},{9,25},{2,18},{10,26},{3,19},{11,27},{4,20},{... | collective-permute-start | bytes 313352 | tf_op jit(solution)/shard_map/ppermute | solution.py:150
  128.3 1.9 %copy-start.5 = (f32[128,8,384]{2,1,0:T(8,128)S(1)}, f32[128,8,384]{2,1,0:T(8,128)}, u32[]{:S(2)}) copy-start(f32[128,8,384]{2,1,0:T(8,128)} %get-tuple-element.7) | copy-start | bytes 4718596
  131.2 34.7 %all-to-all-start.1 = ((f32[128,4,384]{2,1,0:T(4,128)}), f32[128,4,384]{2,1,0:T(4,128)S(1)}, u32[]{:S(2)}, u32[]{:S(2)}) async-start(f32[128,4,384]{2,1,0:T(4,128)} %reverse_add_fusion), calls=%async_computation.1 | async-start | bytes 1572864 | tf_op jit(solution)/shard_map/all_to_all | solution.py:248
  135.6 13.1 %collective-permute-start.10 = (f32[17,16,384]{2,1,0:T(8,128)}, f32[17,16,384]{2,1,0:T(8,128)}, u32[]{:S(2)}, u32[]{:S(2)}) collective-permute-start(f32[17,16,384]{2,1,0:T(8,128)} %pad_maximum_fusion.6), channel_id=1, source_target_pairs={{0,128},{32,160},{64,192},{96,224},{1,129},{33,161},{65,193},{97,2... | collective-permute-start | bytes 1253384 | tf_op jit(solution)/shard_map/ppermute | solution.py:150
  166.0 1.4 copy-start.4
  167.6 1.0 copy-start.2
  167.6 1.0 copy-start.19
  167.6 1.0 copy-start.20

commit v5 on v4

--- a/solution.py
+++ b/solution.py
@@ -44,22 +44,6 @@
                 offset_row, offset_col
             ].astype(jnp.float32)
     return jax.nn.silu(summed).astype(jnp.bfloat16)
-
-
-def direction_inputs(seq_x, seq_mask, proj_one, dtw_one, dtb_one):
-    rank = dtw_one.shape[0]
-    nstate = (proj_one.shape[1] - rank) // 2
-    length, seqs, inner = seq_x.shape
-    flat = seq_x.reshape(length * seqs, inner)
-    projections = jnp.dot(flat, proj_one, preferred_element_type=jnp.float32)
-    rate_low = projections[:, :rank].astype(jnp.bfloat16)
-    delta = jax.nn.softplus(
-        jnp.dot(rate_low, dtw_one, preferred_element_type=jnp.float32) + dtb_one
-    )
-    delta = delta.reshape(length, seqs, inner) * seq_mask[:, :, None]
-    entry = projections[:, rank : rank + nstate].reshape(length, seqs, nstate)
-    readout = projections[:, rank + nstate :].reshape(length, seqs, nstate)
-    return (delta, entry, readout)
 
 
 def scan_kernel(neg_rate_ref, skip_ref, x_ref, delta_ref, entry_ref, readout_ref, *rest,
@@ -189,7 +173,7 @@
 
 def direction_pair(seq_x, seq_mask, ahead, back, proj_weight, dt_weight, dt_bias, a_rate, skip_d,
                    axis):
-    length, seqs, inner = seq_x.shape
+    _, seqs, _ = seq_x.shape
     stacked_x = jnp.concatenate([seq_x, flipped(seq_x)], axis=1)
     stacked_mask = jnp.concatenate([seq_mask, flipped(seq_mask)], axis=1)
     delta, entry, readout = pair_inputs(
@@ -207,7 +191,7 @@
     return y[:, :seqs] + flipped(y[:, seqs:])
 
 
-def local(
+def block(
     tokens,
     tissue,
     ln_gain,
@@ -265,7 +249,7 @@
     mesh = jax.sharding.Mesh(grid, ("row", "cx", "cz"))
     col = ("cx", "cz")
     return jax.shard_map(
-        local,
+        block,
         mesh=mesh,
         in_specs=(
             P("row", col, None),

time: 173 us -> 173 us (level)
  no operation moved by 1% of the time
where the time goes in v5:
time: 173 us; the launch traced here: 170 us
  starting transfers between devices  54.4 us (31%)
  Pallas kernels  41.6 us (24%)
  other arithmetic  26 us (15%)
  waiting for transfers between devices  24.6 us (14%)
  local copies, waits for them, and re-layouts  14.7 us (8%)
  matrix products  7.71 us (4%)
    pallas_call x4, Pallas kernels, run_scan(): return pl.pallas_call(kernel, out_shape=tuple(out_shape))(*args)  41.6 us
    ppermute x10, starting transfers between devices, carried_in(): got = lax.ppermute(inclusive, axis, pairs)  29.8 us
    ppermute x10, waiting for transfers between devices, carried_in(): got = lax.ppermute(inclusive, axis, pairs)  12 us
    all_to_all x1, waiting for transfers between devices, block(): band = lax.all_to_all(sent, 'cz', 0, 1, tiled=True)  10.9 us
    ppermute x2, starting transfers between devices, padded_2(): lax.ppermute(lax.slice_in_dim(block, 0, width, axis=dim), axis, backward)  8.05 us
    all_to_all x1, starting transfers between devices, block(): band = lax.all_to_all(sent, 'cz', 0, 1, tiled=True)  6.76 us
    ppermute x2, starting transfers between devices, padded_2(): lax.ppermute(lax.slice_in_dim(block, block.shape[dim] - width, None, axis...  6.23 us
    add x8, other arithmetic, combine(): state = decay * earlier[:nstate] + later[:nstate]  5.23 us
  transfers between devices with their start and end apart: 16, of which 5 were waited for; matrix products, arithmetic and copies ran while one was open for 19% of the time, Pallas kernels for 20%

profile of v5, /device:TPU:14, one launch (start us, length us, event | category | flops | bytes accessed | tf_op | source)
XLA Modules:
  0.0 169.7 jit_solution(15871735126510862978)
XLA Ops:
  0.0 1.1 convert_reduce_fusion
  1.2 1.2 fusion.11
  2.5 1.2 fusion.13
  4.0 1.9 %collective-permute-start.1 = (bf16[1,16,384]{2,1,0:T(8,128)(2,1)S(1)}, bf16[1,16,384]{2,1,0:T(8,128)(2,1)S(1)}, u32[]{:S(2)}, u32[]{:S(2)}) collective-permute-start(bf16[1,16,384]{2,1,0:T(8,128)(2,1)S(1)} %get-tuple-element.39), channel_id=1, source_target_pairs={{32,0},{64,32},{96,64},{128,96},{160,128},{192,160},{224,192},{33,... | collective-permute-start | bytes 36872 | tf_op jit(solution)/shard_map/ppermute | solution.py:18
  5.9 2.4 %collective-permute-start = (bf16[1,16,384]{2,1,0:T(8,128)(2,1)S(1)}, bf16[1,16,384]{2,1,0:T(8,128)(2,1)S(1)}, u32[]{:S(2)}, u32[]{:S(2)}) collective-permute-start(bf16[1,16,384]{2,1,0:T(8,128)(2,1)S(1)} %get-tuple-element.38), channel_id=1, source_target_pairs={{0,32},{32,64},{64,96},{96,128},{128,160},{160,192},{192,224},{1,3... | collective-permute-start | bytes 36872 | tf_op jit(solution)/shard_map/ppermute | solution.py:15
  10.2 1.0 pad_maximum_fusion.1.neg_rate_ref
  13.3 3.8 %collective-permute-start.2 = (bf16[34,1,384]{2,1,0:T(2,128)(2,1)S(1)}, bf16[34,1,384]{2,1,0:T(2,128)(2,1)S(1)}, u32[]{:S(2)}, u32[]{:S(2)}) collective-permute-start(bf16[34,1,384]{2,1,0:T(2,128)(2,1)S(1)} %get-tuple-element.48), channel_id=1, source_target_pairs={{0,1},{1,2},{2,3},{3,4},{4,5},{5,6},{6,7},{7,8},{8,9},{9,10},{10,1... | collective-permute-start | bytes 78344 | tf_op jit(solution)/shard_map/ppermute | solution.py:15
  17.2 6.1 %collective-permute-start.3 = (bf16[34,1,384]{2,1,0:T(2,128)(2,1)S(1)}, bf16[34,1,384]{2,1,0:T(2,128)(2,1)S(1)}, u32[]{:S(2)}, u32[]{:S(2)}) collective-permute-start(bf16[34,1,384]{2,1,0:T(2,128)(2,1)S(1)} %get-tuple-element.49), channel_id=1, source_target_pairs={{1,0},{2,1},{3,2},{4,3},{5,4},{6,5},{7,6},{8,7},{9,8},{10,9},{11,1... | collective-permute-start | bytes 78344 | tf_op jit(solution)/shard_map/ppermute | solution.py:18
  23.6 1.7 %collective-permute-done.3 = bf16[34,1,384]{2,1,0:T(2,128)(2,1)S(1)} collective-permute-done((bf16[34,1,384]{2,1,0:T(2,128)(2,1)S(1)}, bf16[34,1,384]{2,1,0:T(2,128)(2,1)S(1)}, u32[]{:S(2)}, u32[]{:S(2)}) %collective-permute-start.3) | collective-permute-done | bytes 26144 | tf_op jit(solution)/shard_map/ppermute | solution.py:18
  26.5 1.0 pad_maximum_fusion.2.x_ref
  28.0 1.3 fusion.36
  29.6 2.3 %fusion.1.delta_ref = f32[32,32,384]{2,1,0:T(8,128)} fusion(f32[32,32,384]{2,1,0:T(8,128)S(1)} %fusion.19, f32[32,32]{1,0:T(8,128)S(1)} %copy.82, f32[384]{0:T(512)S(1)} %get-tuple-element.20, f32[384]{0:T(512)S(1)} %get-tuple-element.21, pred[32]{0:T(512)(128)(4,1)S(1)} %iota_compare_fusion, f32[32,32,44]{2,1,0:T(8,128)S(1)} %slice_select_fusion, ...), kind=kOutput, calls=%fused_computation.3 | convolution fusion | flops 13369344 | bytes 3447296 | tf_op jit(solution)/shard_map/dot_general | solution.py:164
  32.0 8.5 %shard_map.129 = f32[17,32,384]{2,1,0:T(8,128)} custom-call(f32[16,32,384]{2,1,0:T(8,128)} %pad_maximum_fusion.1.neg_rate_ref, f32[32,384]{1,0:T(8,128)} %pad_maximum_fusion.17.skip_ref, bf16[32,32,384]{2,1,0:T(8,128)(2,1)} %pad_maximum_fusion.2.x_ref, f32[32,32,384]{2,1,0:T(8,128)} %fusion.1.delta_ref, f32[32,32,16]{2,1,0:T(8,128)} %get-tuple-element.43.entry_ref, ...), custom_call_target="tpu_custom_call" | custom-call | tf_op jit(solution)/shard_map/pallas_call | solution.py:114
  40.4 2.2 %fusion.33 = (f32[17,16,384]{2,1,0:T(8,128)}, f32[17,16,384]{2,1,0:T(8,128)}) fusion(f32[17,32,384]{2,1,0:T(8,128)} %shard_map.129), kind=kLoop, calls=%fused_computation.142 | loop fusion | bytes 1671168 | tf_op jit(solution)/shard_map/slice | solution.py:187
  42.6 2.4 %collective-permute-start.11 = (f32[17,16,384]{2,1,0:T(8,128)}, f32[17,16,384]{2,1,0:T(8,128)}, u32[]{:S(2)}, u32[]{:S(2)}) collective-permute-start(f32[17,16,384]{2,1,0:T(8,128)} %get-tuple-element.35), channel_id=1, source_target_pairs={{32,0},{64,32},{96,64},{128,96},{160,128},{192,160},{224,192},{33,... | collective-permute-start | bytes 1253384 | tf_op jit(solution)/shard_map/ppermute | solution.py:134
  45.0 2.0 %collective-permute-start.8 = (f32[17,16,384]{2,1,0:T(8,128)}, f32[17,16,384]{2,1,0:T(8,128)}, u32[]{:S(2)}, u32[]{:S(2)}) collective-permute-start(f32[17,16,384]{2,1,0:T(8,128)} %get-tuple-element.34), channel_id=1, source_target_pairs={{0,32},{32,64},{64,96},{96,128},{128,160},{160,192},{192,224},{1,3... | collective-permute-start | bytes 1253384 | tf_op jit(solution)/shard_map/ppermute | solution.py:134
  48.2 0.9 pad_maximum_fusion.4
  49.1 6.8 %all-to-all-start = ((bf16[32,17,384]{2,1,0:T(8,128)(2,1)}), bf16[32,17,384]{2,1,0:T(8,128)(2,1)S(1)}, u32[]{:S(2)}, u32[]{:S(2)}) async-start(bf16[32,17,384]{2,1,0:T(8,128)(2,1)} %pad_maximum_fusion.4), calls=%async_computation | async-start | bytes 1179648 | tf_op jit(solution)/shard_map/all_to_all | solution.py:224
  56.7 1.3 slice_add_fusion.1
  58.7 3.1 %collective-permute-start.12 = (f32[17,16,384]{2,1,0:T(8,128)}, f32[17,16,384]{2,1,0:T(8,128)}, u32[]{:S(2)}, u32[]{:S(2)}) collective-permute-start(f32[17,16,384]{2,1,0:T(8,128)} %pad_maximum_fusion.7), channel_id=1, source_target_pairs={{64,0},{96,32},{128,64},{160,96},{192,128},{224,160},{65,1},{97,33... | collective-permute-start | bytes 1253384 | tf_op jit(solution)/shard_map/ppermute | solution.py:134
  62.6 2.7 %collective-permute-start.9 = (f32[17,16,384]{2,1,0:T(8,128)}, f32[17,16,384]{2,1,0:T(8,128)S(1)}, u32[]{:S(2)}, u32[]{:S(2)}) collective-permute-start(f32[17,16,384]{2,1,0:T(8,128)} %pad_maximum_fusion.5), channel_id=1, source_target_pairs={{0,64},{32,96},{64,128},{96,160},{128,192},{160,224},{1,65},{33,97... | collective-permute-start | bytes 1253384 | tf_op jit(solution)/shard_map/ppermute | solution.py:134
  65.3 10.9 %all-to-all-done = bf16[32,17,384]{2,1,0:T(8,128)(2,1)S(1)} async-done(((bf16[32,17,384]{2,1,0:T(8,128)(2,1)}), bf16[32,17,384]{2,1,0:T(8,128)(2,1)S(1)}, u32[]{:S(2)}, u32[]{:S(2)}) %all-to-all-start) | async-done | bytes 417824 | tf_op jit(solution)/shard_map/all_to_all | solution.py:224
  78.4 2.3 %fusion.delta_ref = f32[128,8,384]{2,1,0:T(8,128)} fusion(f32[128,8,384]{2,1,0:T(8,128)S(1)} %fusion.18, f32[128,8]{1,0:T(8,128)S(1)} %copy.74, f32[384]{0:T(512)S(1)} %copy-done.17, f32[384]{0:T(512)S(1)} %copy-done.16, pred[8]{0:T(512)(128)(4,1)S(1)} %copy-done.18, f32[128,8,44]{2,1,0:T(8,128)S(1)} %slice_select_fusion.1, ...), kind=kOutput, calls=%fused_computation.2 | convolution fusion | flops 13369344 | bytes 3496448 | tf_op jit(solution)/shard_map/dot_general | solution.py:164
  80.7 1.4 fusion.35
  82.1 1.3 pad_maximum_fusion.x_ref
  83.4 8.7 %shard_map.127 = f32[17,8,384]{2,1,0:T(8,128)} custom-call(f32[16,8,384]{2,1,0:T(8,128)} %pad_maximum_fusion.11.neg_rate_ref, f32[8,384]{1,0:T(8,128)} %pad_maximum_fusion.19.skip_ref, bf16[128,8,384]{2,1,0:T(8,128)(2,1)} %pad_maximum_fusion.x_ref, f32[128,8,384]{2,1,0:T(8,128)} %fusion.delta_ref, f32[128,8,16]{2,1,0:T(8,128)} %get-tuple-element.41.entry_ref, ...), custom_call_target="tpu_custom_call" | custom-call | tf_op jit(solution)/shard_map/pallas_call | solution.py:114
  92.1 1.1 fusion.37
  93.2 1.3 collective-permute-start.4
  94.5 4.6 %collective-permute-start.6 = (f32[17,4,384]{2,1,0:T(4,128)S(1)}, f32[17,4,384]{2,1,0:T(4,128)S(1)}, u32[]{:S(2)}, u32[]{:S(2)}) collective-permute-start(f32[17,4,384]{2,1,0:T(4,128)S(1)} %get-tuple-element.57), channel_id=1, source_target_pairs={{8,0},{16,8},{24,16},{9,1},{17,9},{25,17},{10,2},{18,10},{26,18},{... | collective-permute-start | bytes 313352 | tf_op jit(solution)/shard_map/ppermute | solution.py:134
  99.9 1.1 multiply_add_fusion
  101.0 1.3 collective-permute-start.13
  102.4 4.2 %collective-permute-start.7 = (f32[17,4,384]{2,1,0:T(4,128)S(1)}, f32[17,4,384]{2,1,0:T(4,128)S(1)}, u32[]{:S(2)}, u32[]{:S(2)}) collective-permute-start(f32[17,4,384]{2,1,0:T(4,128)S(1)} %pad_maximum_fusion.13), channel_id=1, source_target_pairs={{16,0},{24,8},{17,1},{25,9},{18,2},{26,10},{19,3},{27,11},{20,4},{... | collective-permute-start | bytes 313352 | tf_op jit(solution)/shard_map/ppermute | solution.py:134
  106.7 1.5 collective-permute-start.5
  109.0 5.8 %collective-permute-done.5 = f32[17,4,384]{2,1,0:T(4,128)S(1)} collective-permute-done((f32[17,4,384]{2,1,0:T(4,128)S(1)}, f32[17,4,384]{2,1,0:T(4,128)S(1)}, u32[]{:S(2)}, u32[]{:S(2)}) %collective-permute-start.5) | collective-permute-done | bytes 104480 | tf_op jit(solution)/shard_map/ppermute | solution.py:134
  115.6 12.7 %shard_map.128 = (f32[128,8,384]{2,1,0:T(8,128)}, f32[17,8,384]{2,1,0:T(8,128)}) custom-call(f32[16,8,384]{2,1,0:T(8,128)} %pad_maximum_fusion.11.neg_rate_ref, f32[8,384]{1,0:T(8,128)} %pad_maximum_fusion.19.skip_ref, bf16[128,8,384]{2,1,0:T(8,128)(2,1)} %pad_maximum_fusion.x_ref, f32[128,8,384]{2,1,0:T(8,128)} %fusion.delta_ref, ...), custom_call_target="tpu_custom_call" | custom-call | tf_op jit(solution)/shard_map/pallas_call | solution.py:114
  128.3 1.7 slice.367
  130.2 1.1 reverse_add_fusion
  131.2 3.5 %all-to-all-start.1 = ((f32[128,4,384]{2,1,0:T(4,128)}), f32[128,4,384]{2,1,0:T(4,128)S(1)}, u32[]{:S(2)}, u32[]{:S(2)}) async-start(f32[128,4,384]{2,1,0:T(4,128)} %reverse_add_fusion), calls=%async_computation.1 | async-start | bytes 1572864 | tf_op jit(solution)/shard_map/all_to_all | solution.py:232
  134.8 0.8 pad_maximum_fusion.6
  135.6 6.7 %collective-permute-start.10 = (f32[17,16,384]{2,1,0:T(8,128)}, f32[17,16,384]{2,1,0:T(8,128)}, u32[]{:S(2)}, u32[]{:S(2)}) collective-permute-start(f32[17,16,384]{2,1,0:T(8,128)} %pad_maximum_fusion.6), channel_id=1, source_target_pairs={{0,128},{32,160},{64,192},{96,224},{1,129},{33,161},{65,193},{97,2... | collective-permute-start | bytes 1253384 | tf_op jit(solution)/shard_map/ppermute | solution.py:134
  143.2 5.5 %collective-permute-done.10 = f32[17,16,384]{2,1,0:T(8,128)} collective-permute-done((f32[17,16,384]{2,1,0:T(8,128)}, f32[17,16,384]{2,1,0:T(8,128)}, u32[]{:S(2)}, u32[]{:S(2)}) %collective-permute-start.10) | collective-permute-done | bytes 417824 | tf_op jit(solution)/shard_map/ppermute | solution.py:134
  149.5 1.4 fusion.14
  150.8 1.3 fusion.15
  152.1 1.0 maximum_maximum_fusion.rest_0_
  153.1 11.7 %shard_map.130 = (f32[32,32,384]{2,1,0:T(8,128)}, f32[17,32,384]{2,1,0:T(8,128)}) custom-call(f32[16,32,384]{2,1,0:T(8,128)} %pad_maximum_fusion.1.neg_rate_ref, f32[32,384]{1,0:T(8,128)} %pad_maximum_fusion.17.skip_ref, bf16[32,32,384]{2,1,0:T(8,128)(2,1)} %pad_maximum_fusion.2.x_ref, f32[32,32,384]{2,1,0:T(8,128)} %fusion.1.delta_ref, ...), custom_call_target="tpu_custom_call" | custom-call | tf_op jit(solution)/shard_map/pallas_call | solution.py:114
  164.8 1.2 slice.402
  166.1 1.3 copy-done.4
  168.5 1.2 fusion.3
  (129 shorter events, 17.6 us)
Async XLA Ops:
  0.0 3.6 %copy-start = (bf16[192,768]{1,0:T(8,128)(2,1)S(1)}, bf16[192,768]{1,0:T(8,128)(2,1)}, u32[]{:S(2)}) copy-start(bf16[192,768]{1,0:T(8,128)(2,1)} %param.16) | copy-start | bytes 884740
  0.0 8.4 %copy-start.8 = (f32[4,384,16]{1,2,0:T(8,128)S(1)}, f32[4,384,16]{1,2,0:T(8,128)}, u32[]{:S(2)}) copy-start(f32[4,384,16]{1,2,0:T(8,128)} %param.22) | copy-start | bytes 294916
  0.0 8.4 %copy-start.13 = (f32[4,384]{1,0:T(4,128)S(1)}, f32[4,384]{1,0:T(4,128)}, u32[]{:S(2)}) copy-start(f32[4,384]{1,0:T(4,128)} %param.23) | copy-start | bytes 18436
  0.0 8.4 %copy-start.10 = (bf16[3,3,384]{2,1,0:T(4,128)(2,1)S(1)}, bf16[3,3,384]{2,1,0:T(4,128)(2,1)}, u32[]{:S(2)}) copy-start(bf16[3,3,384]{2,1,0:T(4,128)(2,1)} %param.17) | copy-start | bytes 20740
  0.0 8.5 %copy-start.6 = (bf16[4,384,44]{1,0,2:T(4,128)(2,1)S(1)}, bf16[4,384,44]{1,0,2:T(4,128)(2,1)}, u32[]{:S(2)}) copy-start(bf16[4,384,44]{1,0,2:T(4,128)(2,1)} %param.19) | copy-start | bytes 405508
  1.2 7.5 %copy-start.7 = (bf16[4,12,384]{2,0,1:T(4,128)(2,1)S(1)}, bf16[4,12,384]{2,0,1:T(4,128)(2,1)}, u32[]{:S(2)}) copy-start(bf16[4,12,384]{2,0,1:T(4,128)(2,1)} %param.20) | copy-start | bytes 110596
  1.2 8.2 %copy-start.12 = (s32[32,16]{0,1:T(8,128)S(1)}, s32[32,16]{0,1:T(8,128)}, u32[]{:S(2)}) copy-start(s32[32,16]{0,1:T(8,128)} %param.14) | copy-start | bytes 6148
  1.2 8.2 %copy-start.14 = (f32[4,384]{1,0:T(4,128)S(1)}, f32[4,384]{1,0:T(4,128)}, u32[]{:S(2)}) copy-start(f32[4,384]{1,0:T(4,128)} %param.21) | copy-start | bytes 18436
  4.0 9.2 %collective-permute-start.1 = (bf16[1,16,384]{2,1,0:T(8,128)(2,1)S(1)}, bf16[1,16,384]{2,1,0:T(8,128)(2,1)S(1)}, u32[]{:S(2)}, u32[]{:S(2)}) collective-permute-start(bf16[1,16,384]{2,1,0:T(8,128)(2,1)S(1)} %get-tuple-element.39), channel_id=1, source_target_pairs={{32,0},{64,32},{96,64},{128,96},{160,128},{192,160},{224,192},{33,... | collective-permute-start | bytes 36872 | tf_op jit(solution)/shard_map/ppermute | solution.py:18
  5.9 7.3 %collective-permute-start = (bf16[1,16,384]{2,1,0:T(8,128)(2,1)S(1)}, bf16[1,16,384]{2,1,0:T(8,128)(2,1)S(1)}, u32[]{:S(2)}, u32[]{:S(2)}) collective-permute-start(bf16[1,16,384]{2,1,0:T(8,128)(2,1)S(1)} %get-tuple-element.38), channel_id=1, source_target_pairs={{0,32},{32,64},{64,96},{96,128},{128,160},{160,192},{192,224},{1,3... | collective-permute-start | bytes 36872 | tf_op jit(solution)/shard_map/ppermute | solution.py:15
  13.2 12.4 %copy-start.15 = (f32[384]{0:T(512)S(1)}, f32[384]{0:T(512)}, u32[]{:S(2)}) copy-start(f32[384]{0:T(512)} %param.18) | copy-start | bytes 4612
  13.3 10.2 %collective-permute-start.2 = (bf16[34,1,384]{2,1,0:T(2,128)(2,1)S(1)}, bf16[34,1,384]{2,1,0:T(2,128)(2,1)S(1)}, u32[]{:S(2)}, u32[]{:S(2)}) collective-permute-start(bf16[34,1,384]{2,1,0:T(2,128)(2,1)S(1)} %get-tuple-element.48), channel_id=1, source_target_pairs={{0,1},{1,2},{2,3},{3,4},{4,5},{5,6},{6,7},{7,8},{8,9},{9,10},{10,1... | collective-permute-start | bytes 78344 | tf_op jit(solution)/shard_map/ppermute | solution.py:15
  17.2 8.1 %collective-permute-start.3 = (bf16[34,1,384]{2,1,0:T(2,128)(2,1)S(1)}, bf16[34,1,384]{2,1,0:T(2,128)(2,1)S(1)}, u32[]{:S(2)}, u32[]{:S(2)}) collective-permute-start(bf16[34,1,384]{2,1,0:T(2,128)(2,1)S(1)} %get-tuple-element.49), channel_id=1, source_target_pairs={{1,0},{2,1},{3,2},{4,3},{5,4},{6,5},{7,6},{8,7},{9,8},{10,9},{11,1... | collective-permute-start | bytes 78344 | tf_op jit(solution)/shard_map/ppermute | solution.py:18
  42.6 13.3 %copy-start.1 = (f32[17,32,384]{2,1,0:T(8,128)S(1)}, f32[17,32,384]{2,1,0:T(8,128)}, u32[]{:S(2)}) copy-start(f32[17,32,384]{2,1,0:T(8,128)} %shard_map.129) | copy-start | bytes 2506756
  42.6 13.3 %collective-permute-start.11 = (f32[17,16,384]{2,1,0:T(8,128)}, f32[17,16,384]{2,1,0:T(8,128)}, u32[]{:S(2)}, u32[]{:S(2)}) collective-permute-start(f32[17,16,384]{2,1,0:T(8,128)} %get-tuple-element.35), channel_id=1, source_target_pairs={{32,0},{64,32},{96,64},{128,96},{160,128},{192,160},{224,192},{33,... | collective-permute-start | bytes 1253384 | tf_op jit(solution)/shard_map/ppermute | solution.py:134
  45.0 10.9 %collective-permute-start.8 = (f32[17,16,384]{2,1,0:T(8,128)}, f32[17,16,384]{2,1,0:T(8,128)}, u32[]{:S(2)}, u32[]{:S(2)}) collective-permute-start(f32[17,16,384]{2,1,0:T(8,128)} %get-tuple-element.34), channel_id=1, source_target_pairs={{0,32},{32,64},{64,96},{96,128},{128,160},{160,192},{192,224},{1,3... | collective-permute-start | bytes 1253384 | tf_op jit(solution)/shard_map/ppermute | solution.py:134
  49.1 27.1 %all-to-all-start = ((bf16[32,17,384]{2,1,0:T(8,128)(2,1)}), bf16[32,17,384]{2,1,0:T(8,128)(2,1)S(1)}, u32[]{:S(2)}, u32[]{:S(2)}) async-start(bf16[32,17,384]{2,1,0:T(8,128)(2,1)} %pad_maximum_fusion.4), calls=%async_computation | async-start | bytes 1179648 | tf_op jit(solution)/shard_map/all_to_all | solution.py:224
  58.7 40.4 %collective-permute-start.12 = (f32[17,16,384]{2,1,0:T(8,128)}, f32[17,16,384]{2,1,0:T(8,128)}, u32[]{:S(2)}, u32[]{:S(2)}) collective-permute-start(f32[17,16,384]{2,1,0:T(8,128)} %pad_maximum_fusion.7), channel_id=1, source_target_pairs={{64,0},{96,32},{128,64},{160,96},{192,128},{224,160},{65,1},{97,33... | collective-permute-start | bytes 1253384 | tf_op jit(solution)/shard_map/ppermute | solution.py:134
  62.6 45.6 %collective-permute-start.9 = (f32[17,16,384]{2,1,0:T(8,128)}, f32[17,16,384]{2,1,0:T(8,128)S(1)}, u32[]{:S(2)}, u32[]{:S(2)}) collective-permute-start(f32[17,16,384]{2,1,0:T(8,128)} %pad_maximum_fusion.5), channel_id=1, source_target_pairs={{0,64},{32,96},{64,128},{96,160},{128,192},{160,224},{1,65},{33,97... | collective-permute-start | bytes 1253384 | tf_op jit(solution)/shard_map/ppermute | solution.py:134
  76.4 0.8 copy-start.9
  76.5 1.2 copy-start.18
  77.7 0.7 copy-start.11
  77.7 0.7 copy-start.16
  77.7 0.7 copy-start.17
  92.1 10.2 %copy-start.3 = (f32[17,8,384]{2,1,0:T(8,128)S(1)}, f32[17,8,384]{2,1,0:T(8,128)}, u32[]{:S(2)}) copy-start(f32[17,8,384]{2,1,0:T(8,128)} %shard_map.127) | copy-start | bytes 626692
  93.2 9.0 %collective-permute-start.4 = (f32[17,4,384]{2,1,0:T(4,128)S(1)}, f32[17,4,384]{2,1,0:T(4,128)S(1)}, u32[]{:S(2)}, u32[]{:S(2)}) collective-permute-start(f32[17,4,384]{2,1,0:T(4,128)S(1)} %get-tuple-element.56), channel_id=1, source_target_pairs={{0,8},{8,16},{16,24},{1,9},{9,17},{17,25},{2,10},{10,18},{18,26},{... | collective-permute-start | bytes 313352 | tf_op jit(solution)/shard_map/ppermute | solution.py:134
  94.5 7.7 %collective-permute-start.6 = (f32[17,4,384]{2,1,0:T(4,128)S(1)}, f32[17,4,384]{2,1,0:T(4,128)S(1)}, u32[]{:S(2)}, u32[]{:S(2)}) collective-permute-start(f32[17,4,384]{2,1,0:T(4,128)S(1)} %get-tuple-element.57), channel_id=1, source_target_pairs={{8,0},{16,8},{24,16},{9,1},{17,9},{25,17},{10,2},{18,10},{26,18},{... | collective-permute-start | bytes 313352 | tf_op jit(solution)/shard_map/ppermute | solution.py:134
  101.0 41.4 %collective-permute-start.13 = (f32[17,16,384]{2,1,0:T(8,128)S(1)}, f32[17,16,384]{2,1,0:T(8,128)}, u32[]{:S(2)}, u32[]{:S(2)}) collective-permute-start(f32[17,16,384]{2,1,0:T(8,128)S(1)} %pad_maximum_fusion.8), channel_id=1, source_target_pairs={{128,0},{160,32},{192,64},{224,96},{129,1},{161,33},{193,65},{225,... | collective-permute-start | bytes 1253384 | tf_op jit(solution)/shard_map/ppermute | solution.py:134
  102.4 6.5 %collective-permute-start.7 = (f32[17,4,384]{2,1,0:T(4,128)S(1)}, f32[17,4,384]{2,1,0:T(4,128)S(1)}, u32[]{:S(2)}, u32[]{:S(2)}) collective-permute-start(f32[17,4,384]{2,1,0:T(4,128)S(1)} %pad_maximum_fusion.13), channel_id=1, source_target_pairs={{16,0},{24,8},{17,1},{25,9},{18,2},{26,10},{19,3},{27,11},{20,4},{... | collective-permute-start | bytes 313352 | tf_op jit(solution)/shard_map/ppermute | solution.py:134
  106.7 8.1 %collective-permute-start.5 = (f32[17,4,384]{2,1,0:T(4,128)S(1)}, f32[17,4,384]{2,1,0:T(4,128)S(1)}, u32[]{:S(2)}, u32[]{:S(2)}) collective-permute-start(f32[17,4,384]{2,1,0:T(4,128)S(1)} %pad_maximum_fusion.12), channel_id=1, source_target_pairs={{0,16},{8,24},{1,17},{9,25},{2,18},{10,26},{3,19},{11,27},{4,20},{... | collective-permute-start | bytes 313352 | tf_op jit(solution)/shard_map/ppermute | solution.py:134
  128.3 1.9 %copy-start.5 = (f32[128,8,384]{2,1,0:T(8,128)S(1)}, f32[128,8,384]{2,1,0:T(8,128)}, u32[]{:S(2)}) copy-start(f32[128,8,384]{2,1,0:T(8,128)} %get-tuple-element.7) | copy-start | bytes 4718596
  131.2 34.7 %all-to-all-start.1 = ((f32[128,4,384]{2,1,0:T(4,128)}), f32[128,4,384]{2,1,0:T(4,128)S(1)}, u32[]{:S(2)}, u32[]{:S(2)}) async-start(f32[128,4,384]{2,1,0:T(4,128)} %reverse_add_fusion), calls=%async_computation.1 | async-start | bytes 1572864 | tf_op jit(solution)/shard_map/all_to_all | solution.py:232
  135.6 13.1 %collective-permute-start.10 = (f32[17,16,384]{2,1,0:T(8,128)}, f32[17,16,384]{2,1,0:T(8,128)}, u32[]{:S(2)}, u32[]{:S(2)}) collective-permute-start(f32[17,16,384]{2,1,0:T(8,128)} %pad_maximum_fusion.6), channel_id=1, source_target_pairs={{0,128},{32,160},{64,192},{96,224},{1,129},{33,161},{65,193},{97,2... | collective-permute-start | bytes 1253384 | tf_op jit(solution)/shard_map/ppermute | solution.py:134
  166.0 1.4 copy-start.4
  167.6 1.0 copy-start.2
  167.6 1.0 copy-start.19
  167.6 1.0 copy-start.20

commit v6 on v4

--- a/solution.py
+++ b/solution.py
@@ -137,6 +137,18 @@
     return jnp.concatenate([state, (earlier[nstate] + later[nstate])[None]], axis=0)
 
 
+def pack(message):
+    total = message[-1]
+    high = total.astype(jnp.bfloat16)
+    low = (total - high.astype(jnp.float32)).astype(jnp.bfloat16)
+    return jnp.concatenate([message[:-1].astype(jnp.bfloat16), high[None], low[None]], axis=0)
+
+
+def unpack(message):
+    total = message[-2].astype(jnp.float32) + message[-1].astype(jnp.float32)
+    return jnp.concatenate([message[:-2].astype(jnp.float32), total[None]], axis=0)
+
+
 def carried_in(packed, neg_rate, axis, reverse):
     count = lax.axis_size(axis)
     inclusive = packed
@@ -147,7 +159,10 @@
             pairs = [(i + shift, i) for i in range(count - shift)]
         else:
             pairs = [(i, i + shift) for i in range(count - shift)]
-        got = lax.ppermute(inclusive, axis, pairs)
+        if axis == "row":
+            got = unpack(lax.ppermute(pack(inclusive), axis, pairs))
+        else:
+            got = lax.ppermute(inclusive, axis, pairs)
         exclusive = got if exclusive is None else combine(got, exclusive, neg_rate)
         if 2 * shift < count:
             inclusive = combine(got, inclusive, neg_rate)

time: 173 us -> 175 us (1.012)
  waiting for transfers between devices: 24.6 us -> 30.9 us
  starting transfers between devices: 54.4 us -> 50.5 us
  matrix products: 7.71 us -> 10.3 us
    ppermute x10 -> x4, starting transfers between devices: 29.8 us -> 10.6 us  [carried_in(): got = lax.ppermute(inclusive, axis, pairs)]
    ppermute x0 -> x6, waiting for transfers between devices: none -> 18.4 us  [carried_in(): got = unpack(lax.ppermute(pack(inclusive), axis, pairs))]
    ppermute x0 -> x6, starting transfers between devices: none -> 15.2 us  [carried_in(): got = unpack(lax.ppermute(pack(inclusive), axis, pairs))]
    all_to_all x1, waiting for transfers between devices: 10.9 us -> 4.9 us  [local(): band = lax.all_to_all(sent, 'cz', 0, 1, tiled=True)]
    ppermute x10 -> x4, waiting for transfers between devices: 12 us -> 6.54 us  [carried_in(): got = lax.ppermute(inclusive, axis, pairs)]
    convert_element_type x0 -> x7, other arithmetic: none -> 4.89 us  [the longest x5 2.86 us: pack(): low = (total - high.astype(jnp.float32)).astype(jnp.bfloat16)]
    add x8 -> x5, other arithmetic: 5.23 us -> 1.57 us  [combine(): state = decay * earlier[:nstate] + later[:nstate]]
    concatenate x6 -> x2, other arithmetic: 2.45 us -> 0.05 us  [combine(): jnp.concatenate([state, (earlier[nstate] + later[nstate])[None]], axis=0)]
  transfers between devices with their start and end apart: 16 -> 16, of which waited for: 5 -> 8; matrix products, arithmetic and copies ran while one was open for 19% -> 11% of each run, Pallas kernels for 20% -> 14%
where the time goes in v6:
time: 175 us; the launch traced here: 172 us
  starting transfers between devices  50.5 us (29%)
  Pallas kernels  41.5 us (24%)
  waiting for transfers between devices  30.9 us (18%)
  other arithmetic  24.3 us (14%)
  local copies, waits for them, and re-layouts  14.1 us (8%)
  matrix products  10.3 us (6%)
    pallas_call x4, Pallas kernels, run_scan(): return pl.pallas_call(kernel, out_shape=tuple(out_shape))(*args)  41.5 us
    ppermute x6, waiting for transfers between devices, carried_in(): got = unpack(lax.ppermute(pack(inclusive), axis, pairs))  18.4 us
    ppermute x6, starting transfers between devices, carried_in(): got = unpack(lax.ppermute(pack(inclusive), axis, pairs))  15.2 us
    ppermute x4, starting transfers between devices, carried_in(): got = lax.ppermute(inclusive, axis, pairs)  10.6 us
    ppermute x2, starting transfers between devices, padded_2(): lax.ppermute(lax.slice_in_dim(block, 0, width, axis=dim), axis, backward)  8.05 us
    all_to_all x1, starting transfers between devices, local(): band = lax.all_to_all(sent, 'cz', 0, 1, tiled=True)  6.77 us
    ppermute x4, waiting for transfers between devices, carried_in(): got = lax.ppermute(inclusive, axis, pairs)  6.54 us
    ppermute x2, starting transfers between devices, padded_2(): lax.ppermute(lax.slice_in_dim(block, block.shape[dim] - width, None, axis...  6.23 us
  transfers between devices with their start and end apart: 16, of which 8 were waited for; matrix products, arithmetic and copies ran while one was open for 11% of the time, Pallas kernels for 14%

profile of v6, /device:TPU:14, one launch (start us, length us, event | category | flops | bytes accessed | tf_op | source)
XLA Modules:
  0.0 172.4 jit_solution(15213373685046381142)
XLA Ops:
  0.0 1.1 convert_reduce_fusion
  1.2 1.2 fusion.11
  2.5 1.2 fusion.13
  4.0 1.9 %collective-permute-start.1 = (bf16[1,16,384]{2,1,0:T(8,128)(2,1)S(1)}, bf16[1,16,384]{2,1,0:T(8,128)(2,1)S(1)}, u32[]{:S(2)}, u32[]{:S(2)}) collective-permute-start(bf16[1,16,384]{2,1,0:T(8,128)(2,1)S(1)} %get-tuple-element.51), channel_id=1, source_target_pairs={{32,0},{64,32},{96,64},{128,96},{160,128},{192,160},{224,192},{33,... | collective-permute-start | bytes 36872 | tf_op jit(solution)/shard_map/ppermute | solution.py:18
  5.9 2.4 %collective-permute-start = (bf16[1,16,384]{2,1,0:T(8,128)(2,1)S(1)}, bf16[1,16,384]{2,1,0:T(8,128)(2,1)S(1)}, u32[]{:S(2)}, u32[]{:S(2)}) collective-permute-start(bf16[1,16,384]{2,1,0:T(8,128)(2,1)S(1)} %get-tuple-element.50), channel_id=1, source_target_pairs={{0,32},{32,64},{64,96},{96,128},{128,160},{160,192},{192,224},{1,3... | collective-permute-start | bytes 36872 | tf_op jit(solution)/shard_map/ppermute | solution.py:15
  10.2 1.0 pad_maximum_fusion.1.neg_rate_ref
  13.4 3.8 %collective-permute-start.2 = (bf16[34,1,384]{2,1,0:T(2,128)(2,1)S(1)}, bf16[34,1,384]{2,1,0:T(2,128)(2,1)S(1)}, u32[]{:S(2)}, u32[]{:S(2)}) collective-permute-start(bf16[34,1,384]{2,1,0:T(2,128)(2,1)S(1)} %get-tuple-element.62), channel_id=1, source_target_pairs={{0,1},{1,2},{2,3},{3,4},{4,5},{5,6},{6,7},{7,8},{8,9},{9,10},{10,1... | collective-permute-start | bytes 78344 | tf_op jit(solution)/shard_map/ppermute | solution.py:15
  17.2 6.1 %collective-permute-start.3 = (bf16[34,1,384]{2,1,0:T(2,128)(2,1)S(1)}, bf16[34,1,384]{2,1,0:T(2,128)(2,1)S(1)}, u32[]{:S(2)}, u32[]{:S(2)}) collective-permute-start(bf16[34,1,384]{2,1,0:T(2,128)(2,1)S(1)} %get-tuple-element.63), channel_id=1, source_target_pairs={{1,0},{2,1},{3,2},{4,3},{5,4},{6,5},{7,6},{8,7},{9,8},{10,9},{11,1... | collective-permute-start | bytes 78344 | tf_op jit(solution)/shard_map/ppermute | solution.py:18
  24.3 1.0 collective-permute-done.3
  28.1 1.3 fusion.58
  29.7 2.3 %fusion.1.delta_ref = f32[32,32,384]{2,1,0:T(8,128)} fusion(f32[32,32,384]{2,1,0:T(8,128)S(1)} %fusion.27, f32[32,32]{1,0:T(8,128)S(1)} %copy.82, f32[384]{0:T(512)S(1)} %get-tuple-element.20, f32[384]{0:T(512)S(1)} %get-tuple-element.21, pred[32]{0:T(512)(128)(4,1)S(1)} %iota_compare_fusion, f32[32,32,44]{2,1,0:T(8,128)S(1)} %slice_select_fusion, ...), kind=kOutput, calls=%fused_computation.3 | convolution fusion | flops 13369344 | bytes 3447296 | tf_op jit(solution)/shard_map/dot_general | solution.py:195
  32.1 8.4 %shard_map.129 = f32[17,32,384]{2,1,0:T(8,128)} custom-call(f32[16,32,384]{2,1,0:T(8,128)} %pad_maximum_fusion.1.neg_rate_ref, f32[32,384]{1,0:T(8,128)} %pad_maximum_fusion.19.skip_ref, bf16[32,32,384]{2,1,0:T(8,128)(2,1)} %pad_maximum_fusion.2.x_ref, f32[32,32,384]{2,1,0:T(8,128)} %fusion.1.delta_ref, f32[32,32,16]{2,1,0:T(8,128)} %get-tuple-element.55.entry_ref, ...), custom_call_target="tpu_custom_call" | custom-call | tf_op jit(solution)/shard_map/pallas_call | solution.py:130
  41.3 1.2 fusion.55
  42.5 2.4 %collective-permute-start.8 = (bf16[18,16,384]{2,1,0:T(8,128)(2,1)S(1)}, bf16[18,16,384]{2,1,0:T(8,128)(2,1)S(1)}, u32[]{:S(2)}, u32[]{:S(2)}) collective-permute-start(bf16[18,16,384]{2,1,0:T(8,128)(2,1)S(1)} %pad_maximum_fusion.7), channel_id=1, source_target_pairs={{0,32},{32,64},{64,96},{96,128},{128,160},{160,192},{192,224},{1,3... | collective-permute-start | bytes 663560 | tf_op jit(solution)/shard_map/ppermute | solution.py:163
  45.6 4.3 %collective-permute-done.8 = bf16[18,16,384]{2,1,0:T(8,128)(2,1)S(1)} collective-permute-done((bf16[18,16,384]{2,1,0:T(8,128)(2,1)S(1)}, bf16[18,16,384]{2,1,0:T(8,128)(2,1)S(1)}, u32[]{:S(2)}, u32[]{:S(2)}) %collective-permute-start.8) | collective-permute-done | bytes 221216 | tf_op jit(solution)/shard_map/ppermute | solution.py:163
  49.9 1.4 subtract_convert_fusion.4
  52.1 1.9 %collective-permute-start.11 = (bf16[18,16,384]{2,1,0:T(8,128)(2,1)}, bf16[18,16,384]{2,1,0:T(8,128)(2,1)S(1)}, u32[]{:S(2)}, u32[]{:S(2)}) collective-permute-start(bf16[18,16,384]{2,1,0:T(8,128)(2,1)} %pad_maximum_fusion.10), channel_id=1, source_target_pairs={{32,0},{64,32},{96,64},{128,96},{160,128},{192,160},{224,192},{33,... | collective-permute-start | bytes 663560 | tf_op jit(solution)/shard_map/ppermute | solution.py:163
  55.4 6.8 %all-to-all-start = ((bf16[32,17,384]{2,1,0:T(8,128)(2,1)}), bf16[32,17,384]{2,1,0:T(8,128)(2,1)S(1)}, u32[]{:S(2)}, u32[]{:S(2)}) async-start(bf16[32,17,384]{2,1,0:T(8,128)(2,1)} %pad_maximum_fusion.4), calls=%async_computation | async-start | bytes 1179648 | tf_op jit(solution)/shard_map/all_to_all | solution.py:255
  62.5 3.4 %collective-permute-start.9 = (bf16[18,16,384]{2,1,0:T(8,128)(2,1)S(1)}, bf16[18,16,384]{2,1,0:T(8,128)(2,1)S(1)}, u32[]{:S(2)}, u32[]{:S(2)}) collective-permute-start(bf16[18,16,384]{2,1,0:T(8,128)(2,1)S(1)} %pad_maximum_fusion.8), channel_id=1, source_target_pairs={{0,64},{32,96},{64,128},{96,160},{128,192},{160,224},{1,65},{33,97... | collective-permute-start | bytes 663560 | tf_op jit(solution)/shard_map/ppermute | solution.py:163
  65.9 2.5 %collective-permute-start.12 = (bf16[18,16,384]{2,1,0:T(8,128)(2,1)S(1)}, bf16[18,16,384]{2,1,0:T(8,128)(2,1)S(1)}, u32[]{:S(2)}, u32[]{:S(2)}) collective-permute-start(bf16[18,16,384]{2,1,0:T(8,128)(2,1)S(1)} %pad_maximum_fusion.11), channel_id=1, source_target_pairs={{64,0},{96,32},{128,64},{160,96},{192,128},{224,160},{65,1},{97,33... | collective-permute-start | bytes 663560 | tf_op jit(solution)/shard_map/ppermute | solution.py:163
  68.4 3.5 %collective-permute-done.9 = bf16[18,16,384]{2,1,0:T(8,128)(2,1)S(1)} collective-permute-done((bf16[18,16,384]{2,1,0:T(8,128)(2,1)S(1)}, bf16[18,16,384]{2,1,0:T(8,128)(2,1)S(1)}, u32[]{:S(2)}, u32[]{:S(2)}) %collective-permute-start.9) | collective-permute-done | bytes 221216 | tf_op jit(solution)/shard_map/ppermute | solution.py:163
  72.5 2.6 %collective-permute-done.12 = bf16[18,16,384]{2,1,0:T(8,128)(2,1)S(1)} collective-permute-done((bf16[18,16,384]{2,1,0:T(8,128)(2,1)S(1)}, bf16[18,16,384]{2,1,0:T(8,128)(2,1)S(1)}, u32[]{:S(2)}, u32[]{:S(2)}) %collective-permute-start.12) | collective-permute-done | bytes 221216 | tf_op jit(solution)/shard_map/ppermute | solution.py:163
  75.1 1.8 %fusion.17 = (bf16[16,16,384]{2,1,0:T(8,128)(2,1)}, bf16[16,16,384]{2,1,0:T(8,128)(2,1)}) fusion(f32[16,384]{1,0:T(8,128)S(1)} %bitcast.107, f32[16,384]{1,0:T(8,128)S(1)} %get-tuple-element.83, bf16[18,16,384]{2,1,0:T(8,128)(2,1)S(1)} %collective-permute-done.9, f32[17,32,384]{2,1,0:T(8,128)S(1)} %copy-done.1, ...), kind=kLoop, calls=%fused_computation.49 | loop fusion | flops 1769472 | bytes 2113536 | tf_op jit(solution)/shard_map/convert_element_type | solution.py:144
  76.9 4.9 %all-to-all-done = bf16[32,17,384]{2,1,0:T(8,128)(2,1)S(1)} async-done(((bf16[32,17,384]{2,1,0:T(8,128)(2,1)}), bf16[32,17,384]{2,1,0:T(8,128)(2,1)S(1)}, u32[]{:S(2)}, u32[]{:S(2)}) %all-to-all-start) | async-done | bytes 417824 | tf_op jit(solution)/shard_map/all_to_all | solution.py:255
  82.3 1.3 pad_maximum_fusion.x_ref
  84.4 1.4 fusion.57
  85.8 1.5 fusion.26
  87.6 3.7 %fusion.delta_ref = f32[128,8,384]{2,1,0:T(8,128)} fusion(f32[128,8,384]{2,1,0:T(8,128)} %fusion.26, f32[128,8]{1,0:T(8,128)S(1)} %copy.74, f32[384]{0:T(512)S(1)} %copy-done.24, f32[384]{0:T(512)S(1)} %get-tuple-element.18, pred[8]{0:T(512)(128)(4,1)S(1)} %copy-done.25, f32[128,8,44]{2,1,0:T(8,128)S(1)} %slice_select_fusion.1, ...), kind=kOutput, calls=%fused_computation.2 | convolution fusion | flops 13369344 | bytes 3496448 | tf_op jit(solution)/shard_map/dot_general | solution.py:195
  91.3 8.7 %shard_map.127 = f32[17,8,384]{2,1,0:T(8,128)} custom-call(f32[16,8,384]{2,1,0:T(8,128)} %pad_maximum_fusion.13.neg_rate_ref, f32[8,384]{1,0:T(8,128)} %pad_maximum_fusion.21.skip_ref, bf16[128,8,384]{2,1,0:T(8,128)(2,1)} %pad_maximum_fusion.x_ref, f32[128,8,384]{2,1,0:T(8,128)} %fusion.delta_ref, f32[128,8,16]{2,1,0:T(8,128)} %get-tuple-element.53.entry_ref, ...), custom_call_target="tpu_custom_call" | custom-call | tf_op jit(solution)/shard_map/pallas_call | solution.py:130
  100.1 1.1 fusion.59
  101.1 1.3 collective-permute-start.4
  102.4 4.6 %collective-permute-start.6 = (f32[17,4,384]{2,1,0:T(4,128)S(1)}, f32[17,4,384]{2,1,0:T(4,128)S(1)}, u32[]{:S(2)}, u32[]{:S(2)}) collective-permute-start(f32[17,4,384]{2,1,0:T(4,128)S(1)} %get-tuple-element.73), channel_id=1, source_target_pairs={{8,0},{16,8},{24,16},{9,1},{17,9},{25,17},{10,2},{18,10},{26,18},{... | collective-permute-start | bytes 313352 | tf_op jit(solution)/shard_map/ppermute | solution.py:165
  107.7 3.7 %collective-permute-start.10 = (bf16[18,16,384]{2,1,0:T(8,128)(2,1)}, bf16[18,16,384]{2,1,0:T(8,128)(2,1)S(1)}, u32[]{:S(2)}, u32[]{:S(2)}) collective-permute-start(bf16[18,16,384]{2,1,0:T(8,128)(2,1)} %pad_maximum_fusion.9), channel_id=1, source_target_pairs={{0,128},{32,160},{64,192},{96,224},{1,129},{33,161},{65,193},{97,2... | collective-permute-start | bytes 663560 | tf_op jit(solution)/shard_map/ppermute | solution.py:163
  112.3 1.1 slice_add_fusion.1
  113.4 3.3 %collective-permute-start.7 = (f32[17,4,384]{2,1,0:T(4,128)S(1)}, f32[17,4,384]{2,1,0:T(4,128)S(1)}, u32[]{:S(2)}, u32[]{:S(2)}) collective-permute-start(f32[17,4,384]{2,1,0:T(4,128)S(1)} %pad_maximum_fusion.15), channel_id=1, source_target_pairs={{16,0},{24,8},{17,1},{25,9},{18,2},{26,10},{19,3},{27,11},{20,4},{... | collective-permute-start | bytes 313352 | tf_op jit(solution)/shard_map/ppermute | solution.py:165
  116.8 1.5 collective-permute-start.5
  119.1 5.8 %collective-permute-done.5 = f32[17,4,384]{2,1,0:T(4,128)S(1)} collective-permute-done((f32[17,4,384]{2,1,0:T(4,128)S(1)}, f32[17,4,384]{2,1,0:T(4,128)S(1)}, u32[]{:S(2)}, u32[]{:S(2)}) %collective-permute-start.5) | collective-permute-done | bytes 104480 | tf_op jit(solution)/shard_map/ppermute | solution.py:165
  125.6 12.7 %shard_map.128 = (f32[128,8,384]{2,1,0:T(8,128)}, f32[17,8,384]{2,1,0:T(8,128)}) custom-call(f32[16,8,384]{2,1,0:T(8,128)} %pad_maximum_fusion.13.neg_rate_ref, f32[8,384]{1,0:T(8,128)} %pad_maximum_fusion.21.skip_ref, bf16[128,8,384]{2,1,0:T(8,128)(2,1)} %pad_maximum_fusion.x_ref, f32[128,8,384]{2,1,0:T(8,128)} %fusion.delta_ref, ...), custom_call_target="tpu_custom_call" | custom-call | tf_op jit(solution)/shard_map/pallas_call | solution.py:130
  138.3 1.7 slice.375
  140.2 1.1 reverse_add_fusion
  141.3 3.7 %all-to-all-start.1 = ((f32[128,4,384]{2,1,0:T(4,128)}), f32[128,4,384]{2,1,0:T(4,128)S(1)}, u32[]{:S(2)}, u32[]{:S(2)}) async-start(f32[128,4,384]{2,1,0:T(4,128)} %reverse_add_fusion), calls=%async_computation.1 | async-start | bytes 1572864 | tf_op jit(solution)/shard_map/all_to_all | solution.py:263
  145.0 1.3 collective-permute-start.13
  146.4 8.0 %collective-permute-done.13 = bf16[18,16,384]{2,1,0:T(8,128)(2,1)S(1)} collective-permute-done((bf16[18,16,384]{2,1,0:T(8,128)(2,1)S(1)}, bf16[18,16,384]{2,1,0:T(8,128)(2,1)S(1)}, u32[]{:S(2)}, u32[]{:S(2)}) %collective-permute-start.13) | collective-permute-done | bytes 221216 | tf_op jit(solution)/shard_map/ppermute | solution.py:163
  154.8 1.0 maximum_maximum_fusion.rest_0_
  155.8 11.7 %shard_map.130 = (f32[32,32,384]{2,1,0:T(8,128)}, f32[17,32,384]{2,1,0:T(8,128)}) custom-call(f32[16,32,384]{2,1,0:T(8,128)} %pad_maximum_fusion.1.neg_rate_ref, f32[32,384]{1,0:T(8,128)} %pad_maximum_fusion.19.skip_ref, bf16[32,32,384]{2,1,0:T(8,128)(2,1)} %pad_maximum_fusion.2.x_ref, f32[32,32,384]{2,1,0:T(8,128)} %fusion.1.delta_ref, ...), custom_call_target="tpu_custom_call" | custom-call | tf_op jit(solution)/shard_map/pallas_call | solution.py:130
  167.4 1.2 slice.414
  168.7 1.3 copy-done.3
  171.2 1.2 fusion.3
  (146 shorter events, 19.2 us)
Async XLA Ops:
  0.0 3.6 %copy-start = (bf16[192,768]{1,0:T(8,128)(2,1)S(1)}, bf16[192,768]{1,0:T(8,128)(2,1)}, u32[]{:S(2)}) copy-start(bf16[192,768]{1,0:T(8,128)(2,1)} %param.16) | copy-start | bytes 884740
  0.0 8.4 %copy-start.11 = (f32[4,384,16]{1,2,0:T(8,128)S(1)}, f32[4,384,16]{1,2,0:T(8,128)}, u32[]{:S(2)}) copy-start(f32[4,384,16]{1,2,0:T(8,128)} %param.22) | copy-start | bytes 294916
  0.0 8.4 %copy-start.21 = (f32[4,384]{1,0:T(4,128)S(1)}, f32[4,384]{1,0:T(4,128)}, u32[]{:S(2)}) copy-start(f32[4,384]{1,0:T(4,128)} %param.23) | copy-start | bytes 18436
  0.0 8.4 %copy-start.17 = (bf16[3,3,384]{2,1,0:T(4,128)(2,1)S(1)}, bf16[3,3,384]{2,1,0:T(4,128)(2,1)}, u32[]{:S(2)}) copy-start(bf16[3,3,384]{2,1,0:T(4,128)(2,1)} %param.17) | copy-start | bytes 20740
  0.0 8.5 %copy-start.7 = (bf16[4,384,44]{1,0,2:T(4,128)(2,1)S(1)}, bf16[4,384,44]{1,0,2:T(4,128)(2,1)}, u32[]{:S(2)}) copy-start(bf16[4,384,44]{1,0,2:T(4,128)(2,1)} %param.19) | copy-start | bytes 405508
  1.2 7.5 %copy-start.10 = (bf16[4,12,384]{2,0,1:T(4,128)(2,1)S(1)}, bf16[4,12,384]{2,0,1:T(4,128)(2,1)}, u32[]{:S(2)}) copy-start(bf16[4,12,384]{2,0,1:T(4,128)(2,1)} %param.20) | copy-start | bytes 110596
  1.2 8.2 %copy-start.20 = (s32[32,16]{0,1:T(8,128)S(1)}, s32[32,16]{0,1:T(8,128)}, u32[]{:S(2)}) copy-start(s32[32,16]{0,1:T(8,128)} %param.14) | copy-start | bytes 6148
  1.2 8.3 %copy-start.22 = (f32[4,384]{1,0:T(4,128)S(1)}, f32[4,384]{1,0:T(4,128)}, u32[]{:S(2)}) copy-start(f32[4,384]{1,0:T(4,128)} %param.21) | copy-start | bytes 18436
  4.0 9.2 %collective-permute-start.1 = (bf16[1,16,384]{2,1,0:T(8,128)(2,1)S(1)}, bf16[1,16,384]{2,1,0:T(8,128)(2,1)S(1)}, u32[]{:S(2)}, u32[]{:S(2)}) collective-permute-start(bf16[1,16,384]{2,1,0:T(8,128)(2,1)S(1)} %get-tuple-element.51), channel_id=1, source_target_pairs={{32,0},{64,32},{96,64},{128,96},{160,128},{192,160},{224,192},{33,... | collective-permute-start | bytes 36872 | tf_op jit(solution)/shard_map/ppermute | solution.py:18
  5.9 7.3 %collective-permute-start = (bf16[1,16,384]{2,1,0:T(8,128)(2,1)S(1)}, bf16[1,16,384]{2,1,0:T(8,128)(2,1)S(1)}, u32[]{:S(2)}, u32[]{:S(2)}) collective-permute-start(bf16[1,16,384]{2,1,0:T(8,128)(2,1)S(1)} %get-tuple-element.50), channel_id=1, source_target_pairs={{0,32},{32,64},{64,96},{96,128},{128,160},{160,192},{192,224},{1,3... | collective-permute-start | bytes 36872 | tf_op jit(solution)/shard_map/ppermute | solution.py:15
  13.2 12.4 %copy-start.23 = (f32[384]{0:T(512)S(1)}, f32[384]{0:T(512)}, u32[]{:S(2)}) copy-start(f32[384]{0:T(512)} %param.18) | copy-start | bytes 4612
  13.4 10.9 %collective-permute-start.2 = (bf16[34,1,384]{2,1,0:T(2,128)(2,1)S(1)}, bf16[34,1,384]{2,1,0:T(2,128)(2,1)S(1)}, u32[]{:S(2)}, u32[]{:S(2)}) collective-permute-start(bf16[34,1,384]{2,1,0:T(2,128)(2,1)S(1)} %get-tuple-element.62), channel_id=1, source_target_pairs={{0,1},{1,2},{2,3},{3,4},{4,5},{5,6},{6,7},{7,8},{8,9},{9,10},{10,1... | collective-permute-start | bytes 78344 | tf_op jit(solution)/shard_map/ppermute | solution.py:15
  17.2 8.1 %collective-permute-start.3 = (bf16[34,1,384]{2,1,0:T(2,128)(2,1)S(1)}, bf16[34,1,384]{2,1,0:T(2,128)(2,1)S(1)}, u32[]{:S(2)}, u32[]{:S(2)}) collective-permute-start(bf16[34,1,384]{2,1,0:T(2,128)(2,1)S(1)} %get-tuple-element.63), channel_id=1, source_target_pairs={{1,0},{2,1},{3,2},{4,3},{5,4},{6,5},{7,6},{8,7},{9,8},{10,9},{11,1... | collective-permute-start | bytes 78344 | tf_op jit(solution)/shard_map/ppermute | solution.py:18
  42.5 19.7 %copy-start.1 = (f32[17,32,384]{2,1,0:T(8,128)S(1)}, f32[17,32,384]{2,1,0:T(8,128)}, u32[]{:S(2)}) copy-start(f32[17,32,384]{2,1,0:T(8,128)} %shard_map.129) | copy-start | bytes 2506756
  42.5 7.4 %collective-permute-start.8 = (bf16[18,16,384]{2,1,0:T(8,128)(2,1)S(1)}, bf16[18,16,384]{2,1,0:T(8,128)(2,1)S(1)}, u32[]{:S(2)}, u32[]{:S(2)}) collective-permute-start(bf16[18,16,384]{2,1,0:T(8,128)(2,1)S(1)} %pad_maximum_fusion.7), channel_id=1, source_target_pairs={{0,32},{32,64},{64,96},{96,128},{128,160},{160,192},{192,224},{1,3... | collective-permute-start | bytes 663560 | tf_op jit(solution)/shard_map/ppermute | solution.py:163
  51.3 11.1 %copy-start.8 = (f32[16,384]{1,0:T(8,128)}, f32[16,384]{1,0:T(8,128)S(1)}, u32[]{:S(2)}) copy-start(f32[16,384]{1,0:T(8,128)S(1)} %get-tuple-element.44) | copy-start | bytes 73732
  51.3 11.1 %copy-start.9 = (f32[16,384]{1,0:T(8,128)}, f32[16,384]{1,0:T(8,128)S(1)}, u32[]{:S(2)}) copy-start(f32[16,384]{1,0:T(8,128)S(1)} %get-tuple-element.47) | copy-start | bytes 73732
  52.1 10.1 %collective-permute-start.11 = (bf16[18,16,384]{2,1,0:T(8,128)(2,1)}, bf16[18,16,384]{2,1,0:T(8,128)(2,1)S(1)}, u32[]{:S(2)}, u32[]{:S(2)}) collective-permute-start(bf16[18,16,384]{2,1,0:T(8,128)(2,1)} %pad_maximum_fusion.10), channel_id=1, source_target_pairs={{32,0},{64,32},{96,64},{128,96},{160,128},{192,160},{224,192},{33,... | collective-permute-start | bytes 663560 | tf_op jit(solution)/shard_map/ppermute | solution.py:163
  55.4 26.4 %all-to-all-start = ((bf16[32,17,384]{2,1,0:T(8,128)(2,1)}), bf16[32,17,384]{2,1,0:T(8,128)(2,1)S(1)}, u32[]{:S(2)}, u32[]{:S(2)}) async-start(bf16[32,17,384]{2,1,0:T(8,128)(2,1)} %pad_maximum_fusion.4), calls=%async_computation | async-start | bytes 1179648 | tf_op jit(solution)/shard_map/all_to_all | solution.py:255
  62.5 9.4 %collective-permute-start.9 = (bf16[18,16,384]{2,1,0:T(8,128)(2,1)S(1)}, bf16[18,16,384]{2,1,0:T(8,128)(2,1)S(1)}, u32[]{:S(2)}, u32[]{:S(2)}) collective-permute-start(bf16[18,16,384]{2,1,0:T(8,128)(2,1)S(1)} %pad_maximum_fusion.8), channel_id=1, source_target_pairs={{0,64},{32,96},{64,128},{96,160},{128,192},{160,224},{1,65},{33,97... | collective-permute-start | bytes 663560 | tf_op jit(solution)/shard_map/ppermute | solution.py:163
  65.9 9.2 %collective-permute-start.12 = (bf16[18,16,384]{2,1,0:T(8,128)(2,1)S(1)}, bf16[18,16,384]{2,1,0:T(8,128)(2,1)S(1)}, u32[]{:S(2)}, u32[]{:S(2)}) collective-permute-start(bf16[18,16,384]{2,1,0:T(8,128)(2,1)S(1)} %pad_maximum_fusion.11), channel_id=1, source_target_pairs={{64,0},{96,32},{128,64},{160,96},{192,128},{224,160},{65,1},{97,33... | collective-permute-start | bytes 663560 | tf_op jit(solution)/shard_map/ppermute | solution.py:163
  82.0 1.6 copy-start.15
  82.0 1.6 copy-start.16
  82.3 1.8 %copy-start.25 = (pred[8]{0:T(512)(128)(4,1)S(1)}, pred[8]{0:T(512)(128)(4,1)}, u32[]{:S(2)}) copy-start(pred[8]{0:T(512)(128)(4,1)} %iota_compare_fusion.1) | copy-start | bytes 28
  84.2 1.6 copy-start.13
  85.8 1.8 %copy-start.18 = (bf16[1,12,384]{2,0,1:T(2,128)(2,1)S(1)}, bf16[1,12,384]{2,0,1:T(2,128)(2,1)}, u32[]{:S(2)}) copy-start(bf16[1,12,384]{2,0,1:T(2,128)(2,1)} %get-tuple-element.84) | copy-start | bytes 27652
  85.8 1.8 %copy-start.24 = (f32[384]{0:T(512)S(1)}, f32[384]{0:T(512)}, u32[]{:S(2)}) copy-start(f32[384]{0:T(512)} %get-tuple-element.19) | copy-start | bytes 4612
  91.3 15.7 %copy-start.6 = (bf16[16,16,384]{2,1,0:T(8,128)(2,1)S(1)}, bf16[16,16,384]{2,1,0:T(8,128)(2,1)}, u32[]{:S(2)}) copy-start(bf16[16,16,384]{2,1,0:T(8,128)(2,1)} %get-tuple-element.40) | copy-start | bytes 589828
  91.3 15.7 %copy-start.14 = (bf16[1,16,384]{2,1,0:T(8,128)(2,1)S(1)}, bf16[1,16,384]{2,1,0:T(8,128)(2,1)}, u32[]{:S(2)}) copy-start(bf16[1,16,384]{2,1,0:T(8,128)(2,1)} %get-tuple-element.27) | copy-start | bytes 36868
  101.1 10.3 %collective-permute-start.4 = (f32[17,4,384]{2,1,0:T(4,128)S(1)}, f32[17,4,384]{2,1,0:T(4,128)S(1)}, u32[]{:S(2)}, u32[]{:S(2)}) collective-permute-start(f32[17,4,384]{2,1,0:T(4,128)S(1)} %get-tuple-element.72), channel_id=1, source_target_pairs={{0,8},{8,16},{16,24},{1,9},{9,17},{17,25},{2,10},{10,18},{18,26},{... | collective-permute-start | bytes 313352 | tf_op jit(solution)/shard_map/ppermute | solution.py:165
  102.4 9.0 %collective-permute-start.6 = (f32[17,4,384]{2,1,0:T(4,128)S(1)}, f32[17,4,384]{2,1,0:T(4,128)S(1)}, u32[]{:S(2)}, u32[]{:S(2)}) collective-permute-start(f32[17,4,384]{2,1,0:T(4,128)S(1)} %get-tuple-element.73), channel_id=1, source_target_pairs={{8,0},{16,8},{24,16},{9,1},{17,9},{25,17},{10,2},{18,10},{26,18},{... | collective-permute-start | bytes 313352 | tf_op jit(solution)/shard_map/ppermute | solution.py:165
  107.7 38.6 %collective-permute-start.10 = (bf16[18,16,384]{2,1,0:T(8,128)(2,1)}, bf16[18,16,384]{2,1,0:T(8,128)(2,1)S(1)}, u32[]{:S(2)}, u32[]{:S(2)}) collective-permute-start(bf16[18,16,384]{2,1,0:T(8,128)(2,1)} %pad_maximum_fusion.9), channel_id=1, source_target_pairs={{0,128},{32,160},{64,192},{96,224},{1,129},{33,161},{65,193},{97,2... | collective-permute-start | bytes 663560 | tf_op jit(solution)/shard_map/ppermute | solution.py:163
  113.4 5.6 %collective-permute-start.7 = (f32[17,4,384]{2,1,0:T(4,128)S(1)}, f32[17,4,384]{2,1,0:T(4,128)S(1)}, u32[]{:S(2)}, u32[]{:S(2)}) collective-permute-start(f32[17,4,384]{2,1,0:T(4,128)S(1)} %pad_maximum_fusion.15), channel_id=1, source_target_pairs={{16,0},{24,8},{17,1},{25,9},{18,2},{26,10},{19,3},{27,11},{20,4},{... | collective-permute-start | bytes 313352 | tf_op jit(solution)/shard_map/ppermute | solution.py:165
  116.8 8.1 %collective-permute-start.5 = (f32[17,4,384]{2,1,0:T(4,128)S(1)}, f32[17,4,384]{2,1,0:T(4,128)S(1)}, u32[]{:S(2)}, u32[]{:S(2)}) collective-permute-start(f32[17,4,384]{2,1,0:T(4,128)S(1)} %pad_maximum_fusion.14), channel_id=1, source_target_pairs={{0,16},{8,24},{1,17},{9,25},{2,18},{10,26},{3,19},{11,27},{4,20},{... | collective-permute-start | bytes 313352 | tf_op jit(solution)/shard_map/ppermute | solution.py:165
  138.3 1.9 %copy-start.4 = (f32[128,8,384]{2,1,0:T(8,128)S(1)}, f32[128,8,384]{2,1,0:T(8,128)}, u32[]{:S(2)}) copy-start(f32[128,8,384]{2,1,0:T(8,128)} %get-tuple-element.7) | copy-start | bytes 4718596
  140.2 4.8 %copy-start.5 = (bf16[16,16,384]{2,1,0:T(8,128)(2,1)S(1)}, bf16[16,16,384]{2,1,0:T(8,128)(2,1)}, u32[]{:S(2)}) copy-start(bf16[16,16,384]{2,1,0:T(8,128)(2,1)} %get-tuple-element.41) | copy-start | bytes 589828
  141.3 13.3 %copy-start.12 = (f32[16,384]{1,0:T(8,128)S(1)}, f32[16,384]{1,0:T(8,128)}, u32[]{:S(2)}) copy-start(f32[16,384]{1,0:T(8,128)} %get-tuple-element.64) | copy-start | bytes 73732
  141.3 27.4 %all-to-all-start.1 = ((f32[128,4,384]{2,1,0:T(4,128)}), f32[128,4,384]{2,1,0:T(4,128)S(1)}, u32[]{:S(2)}, u32[]{:S(2)}) async-start(f32[128,4,384]{2,1,0:T(4,128)} %reverse_add_fusion), calls=%async_computation.1 | async-start | bytes 1572864 | tf_op jit(solution)/shard_map/all_to_all | solution.py:263
  145.0 9.3 %collective-permute-start.13 = (bf16[18,16,384]{2,1,0:T(8,128)(2,1)S(1)}, bf16[18,16,384]{2,1,0:T(8,128)(2,1)S(1)}, u32[]{:S(2)}, u32[]{:S(2)}) collective-permute-start(bf16[18,16,384]{2,1,0:T(8,128)(2,1)S(1)} %pad_maximum_fusion.12), channel_id=1, source_target_pairs={{128,0},{160,32},{192,64},{224,96},{129,1},{161,33},{193,65},{225,... | collective-permute-start | bytes 663560 | tf_op jit(solution)/shard_map/ppermute | solution.py:163
  168.6 1.4 copy-start.3
  170.2 1.0 copy-start.2
  170.2 0.9 copy-start.19
  170.2 1.0 copy-start.26
  170.2 1.0 copy-start.27

commit v7 on v4

--- a/solution.py
+++ b/solution.py
@@ -107,7 +107,7 @@
         return (summed + delta, tuple(kept))
 
     summed, states = lax.fori_loop(
-        0, length, step, (jnp.zeros(slab, jnp.float32), start), unroll=4 if in_registers else 2
+        0, length, step, (jnp.zeros(slab, jnp.float32), start), unroll=8 if in_registers else 4
     )
     for n, state in enumerate(states):
         state_ref[n] = state

time: 173 us -> 172 us (level)
  transfers between devices with their start and end apart: 16 -> 16, of which waited for: 5 -> 5; matrix products, arithmetic and copies ran while one was open for 19% -> 19% of each run, Pallas kernels for 20% -> 19%
where the time goes in v7:
time: 172 us; the launch traced here: 169 us
  starting transfers between devices  54.4 us (32%)
  Pallas kernels  40.5 us (24%)
  other arithmetic  26 us (15%)
  waiting for transfers between devices  24.6 us (14%)
  local copies, waits for them, and re-layouts  14.7 us (9%)
  matrix products  7.71 us (4%)
    pallas_call x4, Pallas kernels, run_scan(): return pl.pallas_call(kernel, out_shape=tuple(out_shape))(*args)  40.5 us
    ppermute x10, starting transfers between devices, carried_in(): got = lax.ppermute(inclusive, axis, pairs)  29.8 us
    ppermute x10, waiting for transfers between devices, carried_in(): got = lax.ppermute(inclusive, axis, pairs)  12 us
    all_to_all x1, waiting for transfers between devices, local(): band = lax.all_to_all(sent, 'cz', 0, 1, tiled=True)  10.9 us
    ppermute x2, starting transfers between devices, padded_2(): lax.ppermute(lax.slice_in_dim(block, 0, width, axis=dim), axis, backward)  8.05 us
    all_to_all x1, starting transfers between devices, local(): band = lax.all_to_all(sent, 'cz', 0, 1, tiled=True)  6.76 us
    ppermute x2, starting transfers between devices, padded_2(): lax.ppermute(lax.slice_in_dim(block, block.shape[dim] - width, None, axis...  6.23 us
    add x8, other arithmetic, combine(): state = decay * earlier[:nstate] + later[:nstate]  5.23 us
  transfers between devices with their start and end apart: 16, of which 5 were waited for; matrix products, arithmetic and copies ran while one was open for 19% of the time, Pallas kernels for 19%

profile of v7, /device:TPU:14, one launch (start us, length us, event | category | flops | bytes accessed | tf_op | source)
XLA Modules:
  0.0 168.6 jit_solution(5278059380771337395)
XLA Ops:
  0.0 1.1 convert_reduce_fusion
  1.2 1.2 fusion.11
  2.5 1.2 fusion.13
  4.0 1.9 %collective-permute-start.1 = (bf16[1,16,384]{2,1,0:T(8,128)(2,1)S(1)}, bf16[1,16,384]{2,1,0:T(8,128)(2,1)S(1)}, u32[]{:S(2)}, u32[]{:S(2)}) collective-permute-start(bf16[1,16,384]{2,1,0:T(8,128)(2,1)S(1)} %get-tuple-element.39), channel_id=1, source_target_pairs={{32,0},{64,32},{96,64},{128,96},{160,128},{192,160},{224,192},{33,... | collective-permute-start | bytes 36872 | tf_op jit(solution)/shard_map/ppermute | solution.py:18
  5.9 2.4 %collective-permute-start = (bf16[1,16,384]{2,1,0:T(8,128)(2,1)S(1)}, bf16[1,16,384]{2,1,0:T(8,128)(2,1)S(1)}, u32[]{:S(2)}, u32[]{:S(2)}) collective-permute-start(bf16[1,16,384]{2,1,0:T(8,128)(2,1)S(1)} %get-tuple-element.38), channel_id=1, source_target_pairs={{0,32},{32,64},{64,96},{96,128},{128,160},{160,192},{192,224},{1,3... | collective-permute-start | bytes 36872 | tf_op jit(solution)/shard_map/ppermute | solution.py:15
  10.2 1.0 pad_maximum_fusion.1.neg_rate_ref
  13.3 3.8 %collective-permute-start.2 = (bf16[34,1,384]{2,1,0:T(2,128)(2,1)S(1)}, bf16[34,1,384]{2,1,0:T(2,128)(2,1)S(1)}, u32[]{:S(2)}, u32[]{:S(2)}) collective-permute-start(bf16[34,1,384]{2,1,0:T(2,128)(2,1)S(1)} %get-tuple-element.48), channel_id=1, source_target_pairs={{0,1},{1,2},{2,3},{3,4},{4,5},{5,6},{6,7},{7,8},{8,9},{9,10},{10,1... | collective-permute-start | bytes 78344 | tf_op jit(solution)/shard_map/ppermute | solution.py:15
  17.2 6.1 %collective-permute-start.3 = (bf16[34,1,384]{2,1,0:T(2,128)(2,1)S(1)}, bf16[34,1,384]{2,1,0:T(2,128)(2,1)S(1)}, u32[]{:S(2)}, u32[]{:S(2)}) collective-permute-start(bf16[34,1,384]{2,1,0:T(2,128)(2,1)S(1)} %get-tuple-element.49), channel_id=1, source_target_pairs={{1,0},{2,1},{3,2},{4,3},{5,4},{6,5},{7,6},{8,7},{9,8},{10,9},{11,1... | collective-permute-start | bytes 78344 | tf_op jit(solution)/shard_map/ppermute | solution.py:18
  23.6 1.7 %collective-permute-done.3 = bf16[34,1,384]{2,1,0:T(2,128)(2,1)S(1)} collective-permute-done((bf16[34,1,384]{2,1,0:T(2,128)(2,1)S(1)}, bf16[34,1,384]{2,1,0:T(2,128)(2,1)S(1)}, u32[]{:S(2)}, u32[]{:S(2)}) %collective-permute-start.3) | collective-permute-done | bytes 26144 | tf_op jit(solution)/shard_map/ppermute | solution.py:18
  26.5 1.0 pad_maximum_fusion.2.x_ref
  28.0 1.3 fusion.36
  29.6 2.3 %fusion.1.delta_ref = f32[32,32,384]{2,1,0:T(8,128)} fusion(f32[32,32,384]{2,1,0:T(8,128)S(1)} %fusion.19, f32[32,32]{1,0:T(8,128)S(1)} %copy.82, f32[384]{0:T(512)S(1)} %get-tuple-element.20, f32[384]{0:T(512)S(1)} %get-tuple-element.21, pred[32]{0:T(512)(128)(4,1)S(1)} %iota_compare_fusion, f32[32,32,44]{2,1,0:T(8,128)S(1)} %slice_select_fusion, ...), kind=kOutput, calls=%fused_computation.3 | convolution fusion | flops 13369344 | bytes 3447296 | tf_op jit(solution)/shard_map/dot_general | solution.py:180
  32.0 8.3 %shard_map.129 = f32[17,32,384]{2,1,0:T(8,128)} custom-call(f32[16,32,384]{2,1,0:T(8,128)} %pad_maximum_fusion.1.neg_rate_ref, f32[32,384]{1,0:T(8,128)} %pad_maximum_fusion.17.skip_ref, bf16[32,32,384]{2,1,0:T(8,128)(2,1)} %pad_maximum_fusion.2.x_ref, f32[32,32,384]{2,1,0:T(8,128)} %fusion.1.delta_ref, f32[32,32,16]{2,1,0:T(8,128)} %get-tuple-element.43.entry_ref, ...), custom_call_target="tpu_custom_call" | custom-call | tf_op jit(solution)/shard_map/pallas_call | solution.py:130
  40.3 2.2 %fusion.33 = (f32[17,16,384]{2,1,0:T(8,128)}, f32[17,16,384]{2,1,0:T(8,128)}) fusion(f32[17,32,384]{2,1,0:T(8,128)} %shard_map.129), kind=kLoop, calls=%fused_computation.142 | loop fusion | bytes 1671168 | tf_op jit(solution)/shard_map/slice | solution.py:203
  42.5 2.4 %collective-permute-start.11 = (f32[17,16,384]{2,1,0:T(8,128)}, f32[17,16,384]{2,1,0:T(8,128)}, u32[]{:S(2)}, u32[]{:S(2)}) collective-permute-start(f32[17,16,384]{2,1,0:T(8,128)} %get-tuple-element.35), channel_id=1, source_target_pairs={{32,0},{64,32},{96,64},{128,96},{160,128},{192,160},{224,192},{33,... | collective-permute-start | bytes 1253384 | tf_op jit(solution)/shard_map/ppermute | solution.py:150
  44.9 2.0 %collective-permute-start.8 = (f32[17,16,384]{2,1,0:T(8,128)}, f32[17,16,384]{2,1,0:T(8,128)}, u32[]{:S(2)}, u32[]{:S(2)}) collective-permute-start(f32[17,16,384]{2,1,0:T(8,128)} %get-tuple-element.34), channel_id=1, source_target_pairs={{0,32},{32,64},{64,96},{96,128},{128,160},{160,192},{192,224},{1,3... | collective-permute-start | bytes 1253384 | tf_op jit(solution)/shard_map/ppermute | solution.py:150
  48.1 0.9 pad_maximum_fusion.4
  49.0 6.8 %all-to-all-start = ((bf16[32,17,384]{2,1,0:T(8,128)(2,1)}), bf16[32,17,384]{2,1,0:T(8,128)(2,1)S(1)}, u32[]{:S(2)}, u32[]{:S(2)}) async-start(bf16[32,17,384]{2,1,0:T(8,128)(2,1)} %pad_maximum_fusion.4), calls=%async_computation | async-start | bytes 1179648 | tf_op jit(solution)/shard_map/all_to_all | solution.py:240
  56.6 1.3 slice_add_fusion.1
  58.6 3.1 %collective-permute-start.12 = (f32[17,16,384]{2,1,0:T(8,128)}, f32[17,16,384]{2,1,0:T(8,128)}, u32[]{:S(2)}, u32[]{:S(2)}) collective-permute-start(f32[17,16,384]{2,1,0:T(8,128)} %pad_maximum_fusion.7), channel_id=1, source_target_pairs={{64,0},{96,32},{128,64},{160,96},{192,128},{224,160},{65,1},{97,33... | collective-permute-start | bytes 1253384 | tf_op jit(solution)/shard_map/ppermute | solution.py:150
  62.5 2.7 %collective-permute-start.9 = (f32[17,16,384]{2,1,0:T(8,128)}, f32[17,16,384]{2,1,0:T(8,128)S(1)}, u32[]{:S(2)}, u32[]{:S(2)}) collective-permute-start(f32[17,16,384]{2,1,0:T(8,128)} %pad_maximum_fusion.5), channel_id=1, source_target_pairs={{0,64},{32,96},{64,128},{96,160},{128,192},{160,224},{1,65},{33,97... | collective-permute-start | bytes 1253384 | tf_op jit(solution)/shard_map/ppermute | solution.py:150
  65.2 10.9 %all-to-all-done = bf16[32,17,384]{2,1,0:T(8,128)(2,1)S(1)} async-done(((bf16[32,17,384]{2,1,0:T(8,128)(2,1)}), bf16[32,17,384]{2,1,0:T(8,128)(2,1)S(1)}, u32[]{:S(2)}, u32[]{:S(2)}) %all-to-all-start) | async-done | bytes 417824 | tf_op jit(solution)/shard_map/all_to_all | solution.py:240
  78.3 2.3 %fusion.delta_ref = f32[128,8,384]{2,1,0:T(8,128)} fusion(f32[128,8,384]{2,1,0:T(8,128)S(1)} %fusion.18, f32[128,8]{1,0:T(8,128)S(1)} %copy.74, f32[384]{0:T(512)S(1)} %copy-done.17, f32[384]{0:T(512)S(1)} %copy-done.16, pred[8]{0:T(512)(128)(4,1)S(1)} %copy-done.18, f32[128,8,44]{2,1,0:T(8,128)S(1)} %slice_select_fusion.1, ...), kind=kOutput, calls=%fused_computation.2 | convolution fusion | flops 13369344 | bytes 3496448 | tf_op jit(solution)/shard_map/dot_general | solution.py:180
  80.6 1.4 fusion.35
  82.0 1.3 pad_maximum_fusion.x_ref
  83.3 8.4 %shard_map.127 = f32[17,8,384]{2,1,0:T(8,128)} custom-call(f32[16,8,384]{2,1,0:T(8,128)} %pad_maximum_fusion.11.neg_rate_ref, f32[8,384]{1,0:T(8,128)} %pad_maximum_fusion.19.skip_ref, bf16[128,8,384]{2,1,0:T(8,128)(2,1)} %pad_maximum_fusion.x_ref, f32[128,8,384]{2,1,0:T(8,128)} %fusion.delta_ref, f32[128,8,16]{2,1,0:T(8,128)} %get-tuple-element.41.entry_ref, ...), custom_call_target="tpu_custom_call" | custom-call | tf_op jit(solution)/shard_map/pallas_call | solution.py:130
  91.7 1.1 fusion.37
  92.9 1.3 collective-permute-start.4
  94.2 4.6 %collective-permute-start.6 = (f32[17,4,384]{2,1,0:T(4,128)S(1)}, f32[17,4,384]{2,1,0:T(4,128)S(1)}, u32[]{:S(2)}, u32[]{:S(2)}) collective-permute-start(f32[17,4,384]{2,1,0:T(4,128)S(1)} %get-tuple-element.57), channel_id=1, source_target_pairs={{8,0},{16,8},{24,16},{9,1},{17,9},{25,17},{10,2},{18,10},{26,18},{... | collective-permute-start | bytes 313352 | tf_op jit(solution)/shard_map/ppermute | solution.py:150
  99.5 1.1 multiply_add_fusion
  100.6 1.3 collective-permute-start.13
  102.1 4.2 %collective-permute-start.7 = (f32[17,4,384]{2,1,0:T(4,128)S(1)}, f32[17,4,384]{2,1,0:T(4,128)S(1)}, u32[]{:S(2)}, u32[]{:S(2)}) collective-permute-start(f32[17,4,384]{2,1,0:T(4,128)S(1)} %pad_maximum_fusion.13), channel_id=1, source_target_pairs={{16,0},{24,8},{17,1},{25,9},{18,2},{26,10},{19,3},{27,11},{20,4},{... | collective-permute-start | bytes 313352 | tf_op jit(solution)/shard_map/ppermute | solution.py:150
  106.4 1.5 collective-permute-start.5
  108.6 5.8 %collective-permute-done.5 = f32[17,4,384]{2,1,0:T(4,128)S(1)} collective-permute-done((f32[17,4,384]{2,1,0:T(4,128)S(1)}, f32[17,4,384]{2,1,0:T(4,128)S(1)}, u32[]{:S(2)}, u32[]{:S(2)}) %collective-permute-start.5) | collective-permute-done | bytes 104480 | tf_op jit(solution)/shard_map/ppermute | solution.py:150
  115.2 12.0 %shard_map.128 = (f32[128,8,384]{2,1,0:T(8,128)}, f32[17,8,384]{2,1,0:T(8,128)}) custom-call(f32[16,8,384]{2,1,0:T(8,128)} %pad_maximum_fusion.11.neg_rate_ref, f32[8,384]{1,0:T(8,128)} %pad_maximum_fusion.19.skip_ref, bf16[128,8,384]{2,1,0:T(8,128)(2,1)} %pad_maximum_fusion.x_ref, f32[128,8,384]{2,1,0:T(8,128)} %fusion.delta_ref, ...), custom_call_target="tpu_custom_call" | custom-call | tf_op jit(solution)/shard_map/pallas_call | solution.py:130
  127.2 1.7 %slice.367 = f32[128,4,384]{2,1,0:T(4,128)S(1)} slice(f32[128,8,384]{2,1,0:T(8,128)} %get-tuple-element.7), slice={[0:128], [4:8], [0:384]} | slice | bytes 1572864 | tf_op jit(solution)/shard_map/slice | solution.py:207
  129.1 1.1 reverse_add_fusion
  130.1 3.5 %all-to-all-start.1 = ((f32[128,4,384]{2,1,0:T(4,128)}), f32[128,4,384]{2,1,0:T(4,128)S(1)}, u32[]{:S(2)}, u32[]{:S(2)}) async-start(f32[128,4,384]{2,1,0:T(4,128)} %reverse_add_fusion), calls=%async_computation.1 | async-start | bytes 1572864 | tf_op jit(solution)/shard_map/all_to_all | solution.py:248
  133.7 0.8 pad_maximum_fusion.6
  134.5 6.7 %collective-permute-start.10 = (f32[17,16,384]{2,1,0:T(8,128)}, f32[17,16,384]{2,1,0:T(8,128)}, u32[]{:S(2)}, u32[]{:S(2)}) collective-permute-start(f32[17,16,384]{2,1,0:T(8,128)} %pad_maximum_fusion.6), channel_id=1, source_target_pairs={{0,128},{32,160},{64,192},{96,224},{1,129},{33,161},{65,193},{97,2... | collective-permute-start | bytes 1253384 | tf_op jit(solution)/shard_map/ppermute | solution.py:150
  142.1 5.5 %collective-permute-done.10 = f32[17,16,384]{2,1,0:T(8,128)} collective-permute-done((f32[17,16,384]{2,1,0:T(8,128)}, f32[17,16,384]{2,1,0:T(8,128)}, u32[]{:S(2)}, u32[]{:S(2)}) %collective-permute-start.10) | collective-permute-done | bytes 417824 | tf_op jit(solution)/shard_map/ppermute | solution.py:150
  148.4 1.4 fusion.14
  149.7 1.3 fusion.15
  151.0 1.0 maximum_maximum_fusion.rest_0_
  152.0 11.7 %shard_map.130 = (f32[32,32,384]{2,1,0:T(8,128)}, f32[17,32,384]{2,1,0:T(8,128)}) custom-call(f32[16,32,384]{2,1,0:T(8,128)} %pad_maximum_fusion.1.neg_rate_ref, f32[32,384]{1,0:T(8,128)} %pad_maximum_fusion.17.skip_ref, bf16[32,32,384]{2,1,0:T(8,128)(2,1)} %pad_maximum_fusion.2.x_ref, f32[32,32,384]{2,1,0:T(8,128)} %fusion.1.delta_ref, ...), custom_call_target="tpu_custom_call" | custom-call | tf_op jit(solution)/shard_map/pallas_call | solution.py:130
  163.7 1.2 slice.402
  165.0 1.3 copy-done.4
  167.5 1.2 fusion.3
  (129 shorter events, 17.6 us)
Async XLA Ops:
  0.0 3.6 %copy-start = (bf16[192,768]{1,0:T(8,128)(2,1)S(1)}, bf16[192,768]{1,0:T(8,128)(2,1)}, u32[]{:S(2)}) copy-start(bf16[192,768]{1,0:T(8,128)(2,1)} %param.16) | copy-start | bytes 884740
  0.0 8.4 %copy-start.8 = (f32[4,384,16]{1,2,0:T(8,128)S(1)}, f32[4,384,16]{1,2,0:T(8,128)}, u32[]{:S(2)}) copy-start(f32[4,384,16]{1,2,0:T(8,128)} %param.22) | copy-start | bytes 294916
  0.0 8.4 %copy-start.13 = (f32[4,384]{1,0:T(4,128)S(1)}, f32[4,384]{1,0:T(4,128)}, u32[]{:S(2)}) copy-start(f32[4,384]{1,0:T(4,128)} %param.23) | copy-start | bytes 18436
  0.0 8.4 %copy-start.10 = (bf16[3,3,384]{2,1,0:T(4,128)(2,1)S(1)}, bf16[3,3,384]{2,1,0:T(4,128)(2,1)}, u32[]{:S(2)}) copy-start(bf16[3,3,384]{2,1,0:T(4,128)(2,1)} %param.17) | copy-start | bytes 20740
  0.0 8.5 %copy-start.6 = (bf16[4,384,44]{1,0,2:T(4,128)(2,1)S(1)}, bf16[4,384,44]{1,0,2:T(4,128)(2,1)}, u32[]{:S(2)}) copy-start(bf16[4,384,44]{1,0,2:T(4,128)(2,1)} %param.19) | copy-start | bytes 405508
  1.2 7.5 %copy-start.7 = (bf16[4,12,384]{2,0,1:T(4,128)(2,1)S(1)}, bf16[4,12,384]{2,0,1:T(4,128)(2,1)}, u32[]{:S(2)}) copy-start(bf16[4,12,384]{2,0,1:T(4,128)(2,1)} %param.20) | copy-start | bytes 110596
  1.2 8.2 %copy-start.12 = (s32[32,16]{0,1:T(8,128)S(1)}, s32[32,16]{0,1:T(8,128)}, u32[]{:S(2)}) copy-start(s32[32,16]{0,1:T(8,128)} %param.14) | copy-start | bytes 6148
  1.2 8.2 %copy-start.14 = (f32[4,384]{1,0:T(4,128)S(1)}, f32[4,384]{1,0:T(4,128)}, u32[]{:S(2)}) copy-start(f32[4,384]{1,0:T(4,128)} %param.21) | copy-start | bytes 18436
  4.0 9.2 %collective-permute-start.1 = (bf16[1,16,384]{2,1,0:T(8,128)(2,1)S(1)}, bf16[1,16,384]{2,1,0:T(8,128)(2,1)S(1)}, u32[]{:S(2)}, u32[]{:S(2)}) collective-permute-start(bf16[1,16,384]{2,1,0:T(8,128)(2,1)S(1)} %get-tuple-element.39), channel_id=1, source_target_pairs={{32,0},{64,32},{96,64},{128,96},{160,128},{192,160},{224,192},{33,... | collective-permute-start | bytes 36872 | tf_op jit(solution)/shard_map/ppermute | solution.py:18
  5.9 7.3 %collective-permute-start = (bf16[1,16,384]{2,1,0:T(8,128)(2,1)S(1)}, bf16[1,16,384]{2,1,0:T(8,128)(2,1)S(1)}, u32[]{:S(2)}, u32[]{:S(2)}) collective-permute-start(bf16[1,16,384]{2,1,0:T(8,128)(2,1)S(1)} %get-tuple-element.38), channel_id=1, source_target_pairs={{0,32},{32,64},{64,96},{96,128},{128,160},{160,192},{192,224},{1,3... | collective-permute-start | bytes 36872 | tf_op jit(solution)/shard_map/ppermute | solution.py:15
  13.2 12.4 %copy-start.15 = (f32[384]{0:T(512)S(1)}, f32[384]{0:T(512)}, u32[]{:S(2)}) copy-start(f32[384]{0:T(512)} %param.18) | copy-start | bytes 4612
  13.3 10.2 %collective-permute-start.2 = (bf16[34,1,384]{2,1,0:T(2,128)(2,1)S(1)}, bf16[34,1,384]{2,1,0:T(2,128)(2,1)S(1)}, u32[]{:S(2)}, u32[]{:S(2)}) collective-permute-start(bf16[34,1,384]{2,1,0:T(2,128)(2,1)S(1)} %get-tuple-element.48), channel_id=1, source_target_pairs={{0,1},{1,2},{2,3},{3,4},{4,5},{5,6},{6,7},{7,8},{8,9},{9,10},{10,1... | collective-permute-start | bytes 78344 | tf_op jit(solution)/shard_map/ppermute | solution.py:15
  17.2 8.1 %collective-permute-start.3 = (bf16[34,1,384]{2,1,0:T(2,128)(2,1)S(1)}, bf16[34,1,384]{2,1,0:T(2,128)(2,1)S(1)}, u32[]{:S(2)}, u32[]{:S(2)}) collective-permute-start(bf16[34,1,384]{2,1,0:T(2,128)(2,1)S(1)} %get-tuple-element.49), channel_id=1, source_target_pairs={{1,0},{2,1},{3,2},{4,3},{5,4},{6,5},{7,6},{8,7},{9,8},{10,9},{11,1... | collective-permute-start | bytes 78344 | tf_op jit(solution)/shard_map/ppermute | solution.py:18
  42.5 13.3 %copy-start.1 = (f32[17,32,384]{2,1,0:T(8,128)S(1)}, f32[17,32,384]{2,1,0:T(8,128)}, u32[]{:S(2)}) copy-start(f32[17,32,384]{2,1,0:T(8,128)} %shard_map.129) | copy-start | bytes 2506756
  42.5 13.3 %collective-permute-start.11 = (f32[17,16,384]{2,1,0:T(8,128)}, f32[17,16,384]{2,1,0:T(8,128)}, u32[]{:S(2)}, u32[]{:S(2)}) collective-permute-start(f32[17,16,384]{2,1,0:T(8,128)} %get-tuple-element.35), channel_id=1, source_target_pairs={{32,0},{64,32},{96,64},{128,96},{160,128},{192,160},{224,192},{33,... | collective-permute-start | bytes 1253384 | tf_op jit(solution)/shard_map/ppermute | solution.py:150
  44.9 10.9 %collective-permute-start.8 = (f32[17,16,384]{2,1,0:T(8,128)}, f32[17,16,384]{2,1,0:T(8,128)}, u32[]{:S(2)}, u32[]{:S(2)}) collective-permute-start(f32[17,16,384]{2,1,0:T(8,128)} %get-tuple-element.34), channel_id=1, source_target_pairs={{0,32},{32,64},{64,96},{96,128},{128,160},{160,192},{192,224},{1,3... | collective-permute-start | bytes 1253384 | tf_op jit(solution)/shard_map/ppermute | solution.py:150
  49.0 27.1 %all-to-all-start = ((bf16[32,17,384]{2,1,0:T(8,128)(2,1)}), bf16[32,17,384]{2,1,0:T(8,128)(2,1)S(1)}, u32[]{:S(2)}, u32[]{:S(2)}) async-start(bf16[32,17,384]{2,1,0:T(8,128)(2,1)} %pad_maximum_fusion.4), calls=%async_computation | async-start | bytes 1179648 | tf_op jit(solution)/shard_map/all_to_all | solution.py:240
  58.6 40.1 %collective-permute-start.12 = (f32[17,16,384]{2,1,0:T(8,128)}, f32[17,16,384]{2,1,0:T(8,128)}, u32[]{:S(2)}, u32[]{:S(2)}) collective-permute-start(f32[17,16,384]{2,1,0:T(8,128)} %pad_maximum_fusion.7), channel_id=1, source_target_pairs={{64,0},{96,32},{128,64},{160,96},{192,128},{224,160},{65,1},{97,33... | collective-permute-start | bytes 1253384 | tf_op jit(solution)/shard_map/ppermute | solution.py:150
  62.5 45.3 %collective-permute-start.9 = (f32[17,16,384]{2,1,0:T(8,128)}, f32[17,16,384]{2,1,0:T(8,128)S(1)}, u32[]{:S(2)}, u32[]{:S(2)}) collective-permute-start(f32[17,16,384]{2,1,0:T(8,128)} %pad_maximum_fusion.5), channel_id=1, source_target_pairs={{0,64},{32,96},{64,128},{96,160},{128,192},{160,224},{1,65},{33,97... | collective-permute-start | bytes 1253384 | tf_op jit(solution)/shard_map/ppermute | solution.py:150
  76.3 0.8 copy-start.9
  76.4 1.2 copy-start.18
  77.6 0.7 copy-start.11
  77.6 0.7 copy-start.16
  77.6 0.7 copy-start.17
  91.7 10.2 %copy-start.3 = (f32[17,8,384]{2,1,0:T(8,128)S(1)}, f32[17,8,384]{2,1,0:T(8,128)}, u32[]{:S(2)}) copy-start(f32[17,8,384]{2,1,0:T(8,128)} %shard_map.127) | copy-start | bytes 626692
  92.9 9.0 %collective-permute-start.4 = (f32[17,4,384]{2,1,0:T(4,128)S(1)}, f32[17,4,384]{2,1,0:T(4,128)S(1)}, u32[]{:S(2)}, u32[]{:S(2)}) collective-permute-start(f32[17,4,384]{2,1,0:T(4,128)S(1)} %get-tuple-element.56), channel_id=1, source_target_pairs={{0,8},{8,16},{16,24},{1,9},{9,17},{17,25},{2,10},{10,18},{18,26},{... | collective-permute-start | bytes 313352 | tf_op jit(solution)/shard_map/ppermute | solution.py:150
  94.2 7.7 %collective-permute-start.6 = (f32[17,4,384]{2,1,0:T(4,128)S(1)}, f32[17,4,384]{2,1,0:T(4,128)S(1)}, u32[]{:S(2)}, u32[]{:S(2)}) collective-permute-start(f32[17,4,384]{2,1,0:T(4,128)S(1)} %get-tuple-element.57), channel_id=1, source_target_pairs={{8,0},{16,8},{24,16},{9,1},{17,9},{25,17},{10,2},{18,10},{26,18},{... | collective-permute-start | bytes 313352 | tf_op jit(solution)/shard_map/ppermute | solution.py:150
  100.6 40.7 %collective-permute-start.13 = (f32[17,16,384]{2,1,0:T(8,128)S(1)}, f32[17,16,384]{2,1,0:T(8,128)}, u32[]{:S(2)}, u32[]{:S(2)}) collective-permute-start(f32[17,16,384]{2,1,0:T(8,128)S(1)} %pad_maximum_fusion.8), channel_id=1, source_target_pairs={{128,0},{160,32},{192,64},{224,96},{129,1},{161,33},{193,65},{225,... | collective-permute-start | bytes 1253384 | tf_op jit(solution)/shard_map/ppermute | solution.py:150
  102.1 6.5 %collective-permute-start.7 = (f32[17,4,384]{2,1,0:T(4,128)S(1)}, f32[17,4,384]{2,1,0:T(4,128)S(1)}, u32[]{:S(2)}, u32[]{:S(2)}) collective-permute-start(f32[17,4,384]{2,1,0:T(4,128)S(1)} %pad_maximum_fusion.13), channel_id=1, source_target_pairs={{16,0},{24,8},{17,1},{25,9},{18,2},{26,10},{19,3},{27,11},{20,4},{... | collective-permute-start | bytes 313352 | tf_op jit(solution)/shard_map/ppermute | solution.py:150
  106.4 8.1 %collective-permute-start.5 = (f32[17,4,384]{2,1,0:T(4,128)S(1)}, f32[17,4,384]{2,1,0:T(4,128)S(1)}, u32[]{:S(2)}, u32[]{:S(2)}) collective-permute-start(f32[17,4,384]{2,1,0:T(4,128)S(1)} %pad_maximum_fusion.12), channel_id=1, source_target_pairs={{0,16},{8,24},{1,17},{9,25},{2,18},{10,26},{3,19},{11,27},{4,20},{... | collective-permute-start | bytes 313352 | tf_op jit(solution)/shard_map/ppermute | solution.py:150
  127.2 1.9 %copy-start.5 = (f32[128,8,384]{2,1,0:T(8,128)S(1)}, f32[128,8,384]{2,1,0:T(8,128)}, u32[]{:S(2)}) copy-start(f32[128,8,384]{2,1,0:T(8,128)} %get-tuple-element.7) | copy-start | bytes 4718596
  130.1 34.8 %all-to-all-start.1 = ((f32[128,4,384]{2,1,0:T(4,128)}), f32[128,4,384]{2,1,0:T(4,128)S(1)}, u32[]{:S(2)}, u32[]{:S(2)}) async-start(f32[128,4,384]{2,1,0:T(4,128)} %reverse_add_fusion), calls=%async_computation.1 | async-start | bytes 1572864 | tf_op jit(solution)/shard_map/all_to_all | solution.py:248
  134.5 13.1 %collective-permute-start.10 = (f32[17,16,384]{2,1,0:T(8,128)}, f32[17,16,384]{2,1,0:T(8,128)}, u32[]{:S(2)}, u32[]{:S(2)}) collective-permute-start(f32[17,16,384]{2,1,0:T(8,128)} %pad_maximum_fusion.6), channel_id=1, source_target_pairs={{0,128},{32,160},{64,192},{96,224},{1,129},{33,161},{65,193},{97,2... | collective-permute-start | bytes 1253384 | tf_op jit(solution)/shard_map/ppermute | solution.py:150
  164.9 1.4 copy-start.4
  166.5 1.0 copy-start.2
  166.5 1.0 copy-start.19
  166.5 1.0 copy-start.20

commit v8 on v7

--- a/solution.py
+++ b/solution.py
@@ -107,7 +107,7 @@
         return (summed + delta, tuple(kept))
 
     summed, states = lax.fori_loop(
-        0, length, step, (jnp.zeros(slab, jnp.float32), start), unroll=8 if in_registers else 4
+        0, length, step, (jnp.zeros(slab, jnp.float32), start), unroll=8
     )
     for n, state in enumerate(states):
         state_ref[n] = state

time: 172 us -> 172 us (level)
  no operation moved by 1% of the time
where the time goes in v8:
time: 172 us; the launch traced here: 169 us
  starting transfers between devices  54.4 us (32%)
  Pallas kernels  40.4 us (23%)
  other arithmetic  26 us (15%)
  waiting for transfers between devices  24.8 us (14%)
  local copies, waits for them, and re-layouts  14.7 us (9%)
  matrix products  7.71 us (4%)
    pallas_call x4, Pallas kernels, run_scan(): return pl.pallas_call(kernel, out_shape=tuple(out_shape))(*args)  40.4 us
    ppermute x10, starting transfers between devices, carried_in(): got = lax.ppermute(inclusive, axis, pairs)  29.8 us
    ppermute x10, waiting for transfers between devices, carried_in(): got = lax.ppermute(inclusive, axis, pairs)  12.2 us
    all_to_all x1, waiting for transfers between devices, local(): band = lax.all_to_all(sent, 'cz', 0, 1, tiled=True)  10.9 us
    ppermute x2, starting transfers between devices, padded_2(): lax.ppermute(lax.slice_in_dim(block, 0, width, axis=dim), axis, backward)  8.05 us
    all_to_all x1, starting transfers between devices, local(): band = lax.all_to_all(sent, 'cz', 0, 1, tiled=True)  6.76 us
    ppermute x2, starting transfers between devices, padded_2(): lax.ppermute(lax.slice_in_dim(block, block.shape[dim] - width, None, axis...  6.23 us
    add x8, other arithmetic, combine(): state = decay * earlier[:nstate] + later[:nstate]  5.23 us
  transfers between devices with their start and end apart: 16, of which 5 were waited for; matrix products, arithmetic and copies ran while one was open for 19% of the time, Pallas kernels for 19%

profile of v8, /device:TPU:14, one launch (start us, length us, event | category | flops | bytes accessed | tf_op | source)
XLA Modules:
  0.0 168.8 jit_solution(7124522458256724131)
XLA Ops:
  0.0 1.1 convert_reduce_fusion
  1.2 1.2 fusion.11
  2.5 1.2 fusion.13
  4.0 1.9 %collective-permute-start.1 = (bf16[1,16,384]{2,1,0:T(8,128)(2,1)S(1)}, bf16[1,16,384]{2,1,0:T(8,128)(2,1)S(1)}, u32[]{:S(2)}, u32[]{:S(2)}) collective-permute-start(bf16[1,16,384]{2,1,0:T(8,128)(2,1)S(1)} %get-tuple-element.39), channel_id=1, source_target_pairs={{32,0},{64,32},{96,64},{128,96},{160,128},{192,160},{224,192},{33,... | collective-permute-start | bytes 36872 | tf_op jit(solution)/shard_map/ppermute | solution.py:18
  5.9 2.4 %collective-permute-start = (bf16[1,16,384]{2,1,0:T(8,128)(2,1)S(1)}, bf16[1,16,384]{2,1,0:T(8,128)(2,1)S(1)}, u32[]{:S(2)}, u32[]{:S(2)}) collective-permute-start(bf16[1,16,384]{2,1,0:T(8,128)(2,1)S(1)} %get-tuple-element.38), channel_id=1, source_target_pairs={{0,32},{32,64},{64,96},{96,128},{128,160},{160,192},{192,224},{1,3... | collective-permute-start | bytes 36872 | tf_op jit(solution)/shard_map/ppermute | solution.py:15
  10.2 1.0 pad_maximum_fusion.1.neg_rate_ref
  13.3 3.8 %collective-permute-start.2 = (bf16[34,1,384]{2,1,0:T(2,128)(2,1)S(1)}, bf16[34,1,384]{2,1,0:T(2,128)(2,1)S(1)}, u32[]{:S(2)}, u32[]{:S(2)}) collective-permute-start(bf16[34,1,384]{2,1,0:T(2,128)(2,1)S(1)} %get-tuple-element.48), channel_id=1, source_target_pairs={{0,1},{1,2},{2,3},{3,4},{4,5},{5,6},{6,7},{7,8},{8,9},{9,10},{10,1... | collective-permute-start | bytes 78344 | tf_op jit(solution)/shard_map/ppermute | solution.py:15
  17.2 6.1 %collective-permute-start.3 = (bf16[34,1,384]{2,1,0:T(2,128)(2,1)S(1)}, bf16[34,1,384]{2,1,0:T(2,128)(2,1)S(1)}, u32[]{:S(2)}, u32[]{:S(2)}) collective-permute-start(bf16[34,1,384]{2,1,0:T(2,128)(2,1)S(1)} %get-tuple-element.49), channel_id=1, source_target_pairs={{1,0},{2,1},{3,2},{4,3},{5,4},{6,5},{7,6},{8,7},{9,8},{10,9},{11,1... | collective-permute-start | bytes 78344 | tf_op jit(solution)/shard_map/ppermute | solution.py:18
  23.6 1.7 %collective-permute-done.3 = bf16[34,1,384]{2,1,0:T(2,128)(2,1)S(1)} collective-permute-done((bf16[34,1,384]{2,1,0:T(2,128)(2,1)S(1)}, bf16[34,1,384]{2,1,0:T(2,128)(2,1)S(1)}, u32[]{:S(2)}, u32[]{:S(2)}) %collective-permute-start.3) | collective-permute-done | bytes 26144 | tf_op jit(solution)/shard_map/ppermute | solution.py:18
  26.5 1.0 pad_maximum_fusion.2.x_ref
  28.0 1.3 fusion.36
  29.6 2.3 %fusion.1.delta_ref = f32[32,32,384]{2,1,0:T(8,128)} fusion(f32[32,32,384]{2,1,0:T(8,128)S(1)} %fusion.19, f32[32,32]{1,0:T(8,128)S(1)} %copy.82, f32[384]{0:T(512)S(1)} %get-tuple-element.20, f32[384]{0:T(512)S(1)} %get-tuple-element.21, pred[32]{0:T(512)(128)(4,1)S(1)} %iota_compare_fusion, f32[32,32,44]{2,1,0:T(8,128)S(1)} %slice_select_fusion, ...), kind=kOutput, calls=%fused_computation.3 | convolution fusion | flops 13369344 | bytes 3447296 | tf_op jit(solution)/shard_map/dot_general | solution.py:180
  32.0 8.3 %shard_map.129 = f32[17,32,384]{2,1,0:T(8,128)} custom-call(f32[16,32,384]{2,1,0:T(8,128)} %pad_maximum_fusion.1.neg_rate_ref, f32[32,384]{1,0:T(8,128)} %pad_maximum_fusion.17.skip_ref, bf16[32,32,384]{2,1,0:T(8,128)(2,1)} %pad_maximum_fusion.2.x_ref, f32[32,32,384]{2,1,0:T(8,128)} %fusion.1.delta_ref, f32[32,32,16]{2,1,0:T(8,128)} %get-tuple-element.43.entry_ref, ...), custom_call_target="tpu_custom_call" | custom-call | tf_op jit(solution)/shard_map/pallas_call | solution.py:130
  40.3 2.2 %fusion.33 = (f32[17,16,384]{2,1,0:T(8,128)}, f32[17,16,384]{2,1,0:T(8,128)}) fusion(f32[17,32,384]{2,1,0:T(8,128)} %shard_map.129), kind=kLoop, calls=%fused_computation.142 | loop fusion | bytes 1671168 | tf_op jit(solution)/shard_map/slice | solution.py:203
  42.4 2.4 %collective-permute-start.11 = (f32[17,16,384]{2,1,0:T(8,128)}, f32[17,16,384]{2,1,0:T(8,128)}, u32[]{:S(2)}, u32[]{:S(2)}) collective-permute-start(f32[17,16,384]{2,1,0:T(8,128)} %get-tuple-element.35), channel_id=1, source_target_pairs={{32,0},{64,32},{96,64},{128,96},{160,128},{192,160},{224,192},{33,... | collective-permute-start | bytes 1253384 | tf_op jit(solution)/shard_map/ppermute | solution.py:150
  44.9 2.0 %collective-permute-start.8 = (f32[17,16,384]{2,1,0:T(8,128)}, f32[17,16,384]{2,1,0:T(8,128)}, u32[]{:S(2)}, u32[]{:S(2)}) collective-permute-start(f32[17,16,384]{2,1,0:T(8,128)} %get-tuple-element.34), channel_id=1, source_target_pairs={{0,32},{32,64},{64,96},{96,128},{128,160},{160,192},{192,224},{1,3... | collective-permute-start | bytes 1253384 | tf_op jit(solution)/shard_map/ppermute | solution.py:150
  48.1 0.9 pad_maximum_fusion.4
  49.0 6.8 %all-to-all-start = ((bf16[32,17,384]{2,1,0:T(8,128)(2,1)}), bf16[32,17,384]{2,1,0:T(8,128)(2,1)S(1)}, u32[]{:S(2)}, u32[]{:S(2)}) async-start(bf16[32,17,384]{2,1,0:T(8,128)(2,1)} %pad_maximum_fusion.4), calls=%async_computation | async-start | bytes 1179648 | tf_op jit(solution)/shard_map/all_to_all | solution.py:240
  56.5 1.3 slice_add_fusion.1
  58.6 3.1 %collective-permute-start.12 = (f32[17,16,384]{2,1,0:T(8,128)}, f32[17,16,384]{2,1,0:T(8,128)}, u32[]{:S(2)}, u32[]{:S(2)}) collective-permute-start(f32[17,16,384]{2,1,0:T(8,128)} %pad_maximum_fusion.7), channel_id=1, source_target_pairs={{64,0},{96,32},{128,64},{160,96},{192,128},{224,160},{65,1},{97,33... | collective-permute-start | bytes 1253384 | tf_op jit(solution)/shard_map/ppermute | solution.py:150
  62.5 2.7 %collective-permute-start.9 = (f32[17,16,384]{2,1,0:T(8,128)}, f32[17,16,384]{2,1,0:T(8,128)S(1)}, u32[]{:S(2)}, u32[]{:S(2)}) collective-permute-start(f32[17,16,384]{2,1,0:T(8,128)} %pad_maximum_fusion.5), channel_id=1, source_target_pairs={{0,64},{32,96},{64,128},{96,160},{128,192},{160,224},{1,65},{33,97... | collective-permute-start | bytes 1253384 | tf_op jit(solution)/shard_map/ppermute | solution.py:150
  65.2 10.9 %all-to-all-done = bf16[32,17,384]{2,1,0:T(8,128)(2,1)S(1)} async-done(((bf16[32,17,384]{2,1,0:T(8,128)(2,1)}), bf16[32,17,384]{2,1,0:T(8,128)(2,1)S(1)}, u32[]{:S(2)}, u32[]{:S(2)}) %all-to-all-start) | async-done | bytes 417824 | tf_op jit(solution)/shard_map/all_to_all | solution.py:240
  78.3 2.3 %fusion.delta_ref = f32[128,8,384]{2,1,0:T(8,128)} fusion(f32[128,8,384]{2,1,0:T(8,128)S(1)} %fusion.18, f32[128,8]{1,0:T(8,128)S(1)} %copy.74, f32[384]{0:T(512)S(1)} %copy-done.17, f32[384]{0:T(512)S(1)} %copy-done.16, pred[8]{0:T(512)(128)(4,1)S(1)} %copy-done.18, f32[128,8,44]{2,1,0:T(8,128)S(1)} %slice_select_fusion.1, ...), kind=kOutput, calls=%fused_computation.2 | convolution fusion | flops 13369344 | bytes 3496448 | tf_op jit(solution)/shard_map/dot_general | solution.py:180
  80.6 1.4 fusion.35
  82.0 1.3 pad_maximum_fusion.x_ref
  83.2 8.4 %shard_map.127 = f32[17,8,384]{2,1,0:T(8,128)} custom-call(f32[16,8,384]{2,1,0:T(8,128)} %pad_maximum_fusion.11.neg_rate_ref, f32[8,384]{1,0:T(8,128)} %pad_maximum_fusion.19.skip_ref, bf16[128,8,384]{2,1,0:T(8,128)(2,1)} %pad_maximum_fusion.x_ref, f32[128,8,384]{2,1,0:T(8,128)} %fusion.delta_ref, f32[128,8,16]{2,1,0:T(8,128)} %get-tuple-element.41.entry_ref, ...), custom_call_target="tpu_custom_call" | custom-call | tf_op jit(solution)/shard_map/pallas_call | solution.py:130
  91.7 1.1 fusion.37
  92.8 1.5 collective-permute-start.4
  94.3 4.6 %collective-permute-start.6 = (f32[17,4,384]{2,1,0:T(4,128)S(1)}, f32[17,4,384]{2,1,0:T(4,128)S(1)}, u32[]{:S(2)}, u32[]{:S(2)}) collective-permute-start(f32[17,4,384]{2,1,0:T(4,128)S(1)} %get-tuple-element.57), channel_id=1, source_target_pairs={{8,0},{16,8},{24,16},{9,1},{17,9},{25,17},{10,2},{18,10},{26,18},{... | collective-permute-start | bytes 313352 | tf_op jit(solution)/shard_map/ppermute | solution.py:150
  99.6 1.1 multiply_add_fusion
  100.7 1.3 collective-permute-start.13
  102.2 4.2 %collective-permute-start.7 = (f32[17,4,384]{2,1,0:T(4,128)S(1)}, f32[17,4,384]{2,1,0:T(4,128)S(1)}, u32[]{:S(2)}, u32[]{:S(2)}) collective-permute-start(f32[17,4,384]{2,1,0:T(4,128)S(1)} %pad_maximum_fusion.13), channel_id=1, source_target_pairs={{16,0},{24,8},{17,1},{25,9},{18,2},{26,10},{19,3},{27,11},{20,4},{... | collective-permute-start | bytes 313352 | tf_op jit(solution)/shard_map/ppermute | solution.py:150
  106.5 1.3 collective-permute-start.5
  107.9 0.8 collective-permute-done.7
  108.8 5.8 %collective-permute-done.5 = f32[17,4,384]{2,1,0:T(4,128)S(1)} collective-permute-done((f32[17,4,384]{2,1,0:T(4,128)S(1)}, f32[17,4,384]{2,1,0:T(4,128)S(1)}, u32[]{:S(2)}, u32[]{:S(2)}) %collective-permute-start.5) | collective-permute-done | bytes 104480 | tf_op jit(solution)/shard_map/ppermute | solution.py:150
  115.3 12.0 %shard_map.128 = (f32[128,8,384]{2,1,0:T(8,128)}, f32[17,8,384]{2,1,0:T(8,128)}) custom-call(f32[16,8,384]{2,1,0:T(8,128)} %pad_maximum_fusion.11.neg_rate_ref, f32[8,384]{1,0:T(8,128)} %pad_maximum_fusion.19.skip_ref, bf16[128,8,384]{2,1,0:T(8,128)(2,1)} %pad_maximum_fusion.x_ref, f32[128,8,384]{2,1,0:T(8,128)} %fusion.delta_ref, ...), custom_call_target="tpu_custom_call" | custom-call | tf_op jit(solution)/shard_map/pallas_call | solution.py:130
  127.3 1.7 %slice.367 = f32[128,4,384]{2,1,0:T(4,128)S(1)} slice(f32[128,8,384]{2,1,0:T(8,128)} %get-tuple-element.7), slice={[0:128], [4:8], [0:384]} | slice | bytes 1572864 | tf_op jit(solution)/shard_map/slice | solution.py:207
  129.2 1.1 reverse_add_fusion
  130.3 3.5 %all-to-all-start.1 = ((f32[128,4,384]{2,1,0:T(4,128)}), f32[128,4,384]{2,1,0:T(4,128)S(1)}, u32[]{:S(2)}, u32[]{:S(2)}) async-start(f32[128,4,384]{2,1,0:T(4,128)} %reverse_add_fusion), calls=%async_computation.1 | async-start | bytes 1572864 | tf_op jit(solution)/shard_map/all_to_all | solution.py:248
  134.6 6.7 %collective-permute-start.10 = (f32[17,16,384]{2,1,0:T(8,128)}, f32[17,16,384]{2,1,0:T(8,128)}, u32[]{:S(2)}, u32[]{:S(2)}) collective-permute-start(f32[17,16,384]{2,1,0:T(8,128)} %pad_maximum_fusion.6), channel_id=1, source_target_pairs={{0,128},{32,160},{64,192},{96,224},{1,129},{33,161},{65,193},{97,2... | collective-permute-start | bytes 1253384 | tf_op jit(solution)/shard_map/ppermute | solution.py:150
  142.2 5.5 %collective-permute-done.10 = f32[17,16,384]{2,1,0:T(8,128)} collective-permute-done((f32[17,16,384]{2,1,0:T(8,128)}, f32[17,16,384]{2,1,0:T(8,128)}, u32[]{:S(2)}, u32[]{:S(2)}) %collective-permute-start.10) | collective-permute-done | bytes 417824 | tf_op jit(solution)/shard_map/ppermute | solution.py:150
  148.5 1.4 fusion.14
  149.9 1.3 fusion.15
  151.1 1.0 maximum_maximum_fusion.rest_0_
  152.1 11.7 %shard_map.130 = (f32[32,32,384]{2,1,0:T(8,128)}, f32[17,32,384]{2,1,0:T(8,128)}) custom-call(f32[16,32,384]{2,1,0:T(8,128)} %pad_maximum_fusion.1.neg_rate_ref, f32[32,384]{1,0:T(8,128)} %pad_maximum_fusion.17.skip_ref, bf16[32,32,384]{2,1,0:T(8,128)(2,1)} %pad_maximum_fusion.2.x_ref, f32[32,32,384]{2,1,0:T(8,128)} %fusion.1.delta_ref, ...), custom_call_target="tpu_custom_call" | custom-call | tf_op jit(solution)/shard_map/pallas_call | solution.py:130
  163.8 1.2 slice.402
  165.1 1.3 copy-done.4
  167.6 1.2 fusion.3
  (129 shorter events, 17.8 us)
Async XLA Ops:
  0.0 3.6 %copy-start = (bf16[192,768]{1,0:T(8,128)(2,1)S(1)}, bf16[192,768]{1,0:T(8,128)(2,1)}, u32[]{:S(2)}) copy-start(bf16[192,768]{1,0:T(8,128)(2,1)} %param.16) | copy-start | bytes 884740
  0.0 8.4 %copy-start.8 = (f32[4,384,16]{1,2,0:T(8,128)S(1)}, f32[4,384,16]{1,2,0:T(8,128)}, u32[]{:S(2)}) copy-start(f32[4,384,16]{1,2,0:T(8,128)} %param.22) | copy-start | bytes 294916
  0.0 8.4 %copy-start.13 = (f32[4,384]{1,0:T(4,128)S(1)}, f32[4,384]{1,0:T(4,128)}, u32[]{:S(2)}) copy-start(f32[4,384]{1,0:T(4,128)} %param.23) | copy-start | bytes 18436
  0.0 8.4 %copy-start.10 = (bf16[3,3,384]{2,1,0:T(4,128)(2,1)S(1)}, bf16[3,3,384]{2,1,0:T(4,128)(2,1)}, u32[]{:S(2)}) copy-start(bf16[3,3,384]{2,1,0:T(4,128)(2,1)} %param.17) | copy-start | bytes 20740
  0.0 8.5 %copy-start.6 = (bf16[4,384,44]{1,0,2:T(4,128)(2,1)S(1)}, bf16[4,384,44]{1,0,2:T(4,128)(2,1)}, u32[]{:S(2)}) copy-start(bf16[4,384,44]{1,0,2:T(4,128)(2,1)} %param.19) | copy-start | bytes 405508
  1.2 7.5 %copy-start.7 = (bf16[4,12,384]{2,0,1:T(4,128)(2,1)S(1)}, bf16[4,12,384]{2,0,1:T(4,128)(2,1)}, u32[]{:S(2)}) copy-start(bf16[4,12,384]{2,0,1:T(4,128)(2,1)} %param.20) | copy-start | bytes 110596
  1.2 8.2 %copy-start.12 = (s32[32,16]{0,1:T(8,128)S(1)}, s32[32,16]{0,1:T(8,128)}, u32[]{:S(2)}) copy-start(s32[32,16]{0,1:T(8,128)} %param.14) | copy-start | bytes 6148
  1.2 8.2 %copy-start.14 = (f32[4,384]{1,0:T(4,128)S(1)}, f32[4,384]{1,0:T(4,128)}, u32[]{:S(2)}) copy-start(f32[4,384]{1,0:T(4,128)} %param.21) | copy-start | bytes 18436
  4.0 9.2 %collective-permute-start.1 = (bf16[1,16,384]{2,1,0:T(8,128)(2,1)S(1)}, bf16[1,16,384]{2,1,0:T(8,128)(2,1)S(1)}, u32[]{:S(2)}, u32[]{:S(2)}) collective-permute-start(bf16[1,16,384]{2,1,0:T(8,128)(2,1)S(1)} %get-tuple-element.39), channel_id=1, source_target_pairs={{32,0},{64,32},{96,64},{128,96},{160,128},{192,160},{224,192},{33,... | collective-permute-start | bytes 36872 | tf_op jit(solution)/shard_map/ppermute | solution.py:18
  5.9 7.3 %collective-permute-start = (bf16[1,16,384]{2,1,0:T(8,128)(2,1)S(1)}, bf16[1,16,384]{2,1,0:T(8,128)(2,1)S(1)}, u32[]{:S(2)}, u32[]{:S(2)}) collective-permute-start(bf16[1,16,384]{2,1,0:T(8,128)(2,1)S(1)} %get-tuple-element.38), channel_id=1, source_target_pairs={{0,32},{32,64},{64,96},{96,128},{128,160},{160,192},{192,224},{1,3... | collective-permute-start | bytes 36872 | tf_op jit(solution)/shard_map/ppermute | solution.py:15
  13.2 12.4 %copy-start.15 = (f32[384]{0:T(512)S(1)}, f32[384]{0:T(512)}, u32[]{:S(2)}) copy-start(f32[384]{0:T(512)} %param.18) | copy-start | bytes 4612
  13.3 10.2 %collective-permute-start.2 = (bf16[34,1,384]{2,1,0:T(2,128)(2,1)S(1)}, bf16[34,1,384]{2,1,0:T(2,128)(2,1)S(1)}, u32[]{:S(2)}, u32[]{:S(2)}) collective-permute-start(bf16[34,1,384]{2,1,0:T(2,128)(2,1)S(1)} %get-tuple-element.48), channel_id=1, source_target_pairs={{0,1},{1,2},{2,3},{3,4},{4,5},{5,6},{6,7},{7,8},{8,9},{9,10},{10,1... | collective-permute-start | bytes 78344 | tf_op jit(solution)/shard_map/ppermute | solution.py:15
  17.2 8.1 %collective-permute-start.3 = (bf16[34,1,384]{2,1,0:T(2,128)(2,1)S(1)}, bf16[34,1,384]{2,1,0:T(2,128)(2,1)S(1)}, u32[]{:S(2)}, u32[]{:S(2)}) collective-permute-start(bf16[34,1,384]{2,1,0:T(2,128)(2,1)S(1)} %get-tuple-element.49), channel_id=1, source_target_pairs={{1,0},{2,1},{3,2},{4,3},{5,4},{6,5},{7,6},{8,7},{9,8},{10,9},{11,1... | collective-permute-start | bytes 78344 | tf_op jit(solution)/shard_map/ppermute | solution.py:18
  42.4 13.3 %copy-start.1 = (f32[17,32,384]{2,1,0:T(8,128)S(1)}, f32[17,32,384]{2,1,0:T(8,128)}, u32[]{:S(2)}) copy-start(f32[17,32,384]{2,1,0:T(8,128)} %shard_map.129) | copy-start | bytes 2506756
  42.4 13.3 %collective-permute-start.11 = (f32[17,16,384]{2,1,0:T(8,128)}, f32[17,16,384]{2,1,0:T(8,128)}, u32[]{:S(2)}, u32[]{:S(2)}) collective-permute-start(f32[17,16,384]{2,1,0:T(8,128)} %get-tuple-element.35), channel_id=1, source_target_pairs={{32,0},{64,32},{96,64},{128,96},{160,128},{192,160},{224,192},{33,... | collective-permute-start | bytes 1253384 | tf_op jit(solution)/shard_map/ppermute | solution.py:150
  44.9 10.9 %collective-permute-start.8 = (f32[17,16,384]{2,1,0:T(8,128)}, f32[17,16,384]{2,1,0:T(8,128)}, u32[]{:S(2)}, u32[]{:S(2)}) collective-permute-start(f32[17,16,384]{2,1,0:T(8,128)} %get-tuple-element.34), channel_id=1, source_target_pairs={{0,32},{32,64},{64,96},{96,128},{128,160},{160,192},{192,224},{1,3... | collective-permute-start | bytes 1253384 | tf_op jit(solution)/shard_map/ppermute | solution.py:150
  49.0 27.1 %all-to-all-start = ((bf16[32,17,384]{2,1,0:T(8,128)(2,1)}), bf16[32,17,384]{2,1,0:T(8,128)(2,1)S(1)}, u32[]{:S(2)}, u32[]{:S(2)}) async-start(bf16[32,17,384]{2,1,0:T(8,128)(2,1)} %pad_maximum_fusion.4), calls=%async_computation | async-start | bytes 1179648 | tf_op jit(solution)/shard_map/all_to_all | solution.py:240
  58.6 40.3 %collective-permute-start.12 = (f32[17,16,384]{2,1,0:T(8,128)}, f32[17,16,384]{2,1,0:T(8,128)}, u32[]{:S(2)}, u32[]{:S(2)}) collective-permute-start(f32[17,16,384]{2,1,0:T(8,128)} %pad_maximum_fusion.7), channel_id=1, source_target_pairs={{64,0},{96,32},{128,64},{160,96},{192,128},{224,160},{65,1},{97,33... | collective-permute-start | bytes 1253384 | tf_op jit(solution)/shard_map/ppermute | solution.py:150
  62.5 45.3 %collective-permute-start.9 = (f32[17,16,384]{2,1,0:T(8,128)}, f32[17,16,384]{2,1,0:T(8,128)S(1)}, u32[]{:S(2)}, u32[]{:S(2)}) collective-permute-start(f32[17,16,384]{2,1,0:T(8,128)} %pad_maximum_fusion.5), channel_id=1, source_target_pairs={{0,64},{32,96},{64,128},{96,160},{128,192},{160,224},{1,65},{33,97... | collective-permute-start | bytes 1253384 | tf_op jit(solution)/shard_map/ppermute | solution.py:150
  76.2 0.8 copy-start.9
  76.3 1.2 copy-start.18
  77.5 0.7 copy-start.11
  77.5 0.7 copy-start.16
  77.5 0.7 copy-start.17
  91.7 10.4 %copy-start.3 = (f32[17,8,384]{2,1,0:T(8,128)S(1)}, f32[17,8,384]{2,1,0:T(8,128)}, u32[]{:S(2)}) copy-start(f32[17,8,384]{2,1,0:T(8,128)} %shard_map.127) | copy-start | bytes 626692
  92.8 9.2 %collective-permute-start.4 = (f32[17,4,384]{2,1,0:T(4,128)S(1)}, f32[17,4,384]{2,1,0:T(4,128)S(1)}, u32[]{:S(2)}, u32[]{:S(2)}) collective-permute-start(f32[17,4,384]{2,1,0:T(4,128)S(1)} %get-tuple-element.56), channel_id=1, source_target_pairs={{0,8},{8,16},{16,24},{1,9},{9,17},{17,25},{2,10},{10,18},{18,26},{... | collective-permute-start | bytes 313352 | tf_op jit(solution)/shard_map/ppermute | solution.py:150
  94.3 7.7 %collective-permute-start.6 = (f32[17,4,384]{2,1,0:T(4,128)S(1)}, f32[17,4,384]{2,1,0:T(4,128)S(1)}, u32[]{:S(2)}, u32[]{:S(2)}) collective-permute-start(f32[17,4,384]{2,1,0:T(4,128)S(1)} %get-tuple-element.57), channel_id=1, source_target_pairs={{8,0},{16,8},{24,16},{9,1},{17,9},{25,17},{10,2},{18,10},{26,18},{... | collective-permute-start | bytes 313352 | tf_op jit(solution)/shard_map/ppermute | solution.py:150
  100.7 40.7 %collective-permute-start.13 = (f32[17,16,384]{2,1,0:T(8,128)S(1)}, f32[17,16,384]{2,1,0:T(8,128)}, u32[]{:S(2)}, u32[]{:S(2)}) collective-permute-start(f32[17,16,384]{2,1,0:T(8,128)S(1)} %pad_maximum_fusion.8), channel_id=1, source_target_pairs={{128,0},{160,32},{192,64},{224,96},{129,1},{161,33},{193,65},{225,... | collective-permute-start | bytes 1253384 | tf_op jit(solution)/shard_map/ppermute | solution.py:150
  102.2 6.5 %collective-permute-start.7 = (f32[17,4,384]{2,1,0:T(4,128)S(1)}, f32[17,4,384]{2,1,0:T(4,128)S(1)}, u32[]{:S(2)}, u32[]{:S(2)}) collective-permute-start(f32[17,4,384]{2,1,0:T(4,128)S(1)} %pad_maximum_fusion.13), channel_id=1, source_target_pairs={{16,0},{24,8},{17,1},{25,9},{18,2},{26,10},{19,3},{27,11},{20,4},{... | collective-permute-start | bytes 313352 | tf_op jit(solution)/shard_map/ppermute | solution.py:150
  106.5 8.1 %collective-permute-start.5 = (f32[17,4,384]{2,1,0:T(4,128)S(1)}, f32[17,4,384]{2,1,0:T(4,128)S(1)}, u32[]{:S(2)}, u32[]{:S(2)}) collective-permute-start(f32[17,4,384]{2,1,0:T(4,128)S(1)} %pad_maximum_fusion.12), channel_id=1, source_target_pairs={{0,16},{8,24},{1,17},{9,25},{2,18},{10,26},{3,19},{11,27},{4,20},{... | collective-permute-start | bytes 313352 | tf_op jit(solution)/shard_map/ppermute | solution.py:150
  127.3 1.9 %copy-start.5 = (f32[128,8,384]{2,1,0:T(8,128)S(1)}, f32[128,8,384]{2,1,0:T(8,128)}, u32[]{:S(2)}) copy-start(f32[128,8,384]{2,1,0:T(8,128)} %get-tuple-element.7) | copy-start | bytes 4718596
  130.3 34.8 %all-to-all-start.1 = ((f32[128,4,384]{2,1,0:T(4,128)}), f32[128,4,384]{2,1,0:T(4,128)S(1)}, u32[]{:S(2)}, u32[]{:S(2)}) async-start(f32[128,4,384]{2,1,0:T(4,128)} %reverse_add_fusion), calls=%async_computation.1 | async-start | bytes 1572864 | tf_op jit(solution)/shard_map/all_to_all | solution.py:248
  134.6 13.1 %collective-permute-start.10 = (f32[17,16,384]{2,1,0:T(8,128)}, f32[17,16,384]{2,1,0:T(8,128)}, u32[]{:S(2)}, u32[]{:S(2)}) collective-permute-start(f32[17,16,384]{2,1,0:T(8,128)} %pad_maximum_fusion.6), channel_id=1, source_target_pairs={{0,128},{32,160},{64,192},{96,224},{1,129},{33,161},{65,193},{97,2... | collective-permute-start | bytes 1253384 | tf_op jit(solution)/shard_map/ppermute | solution.py:150
  165.0 1.4 copy-start.4
  166.6 1.0 copy-start.2
  166.6 1.0 copy-start.19
  166.6 1.0 copy-start.20
